TPU v7x, 512 devices: a whole 4x4x16 slice. The times are simulated.
512 devices in a mesh: wa: 32 (over x, y, core), ha: 16 (over z).
Axes of the slice: x: 4, y: 4, z: 16, core: 2. Of those that a mesh axis runs over, the one named last changes fastest.
Arguments:
- residual_in: bfloat16 [192, 16384], P('ha', 'wa'), may hold values from -43.25 to 43.25
- grad_out: bfloat16 [192, 16384], P('ha', 'wa'), may hold values from -6 to 6
- norm_gain: bfloat16 [16384], P('wa'), may hold values from 0.099609375 to 1.8984375
- w_gate: bfloat16 [16384, 26624], P('wa', 'ha'), may hold values from -0.0390625 to 0.0390625
- w_up: bfloat16 [16384, 26624], P('wa', 'ha'), may hold values from -0.0390625 to 0.0390625
- w_down: bfloat16 [26624, 16384], P('ha', 'wa'), may hold values from -0.030643146 to 0.030643146
Outputs:
- grad_in: bfloat16 [192, 16384], P('ha', 'wa')
All inputs are finite; a program needn't handle non-finite values.
Results may differ from a plain program's by a relative error of at most 0.0053.
Values may be sent and summed in bfloat16 or wider, within the bound.
No kernel may reach another device: no remote copies, remote signals or barrier semaphores. Data moves between devices by JAX's collectives and lax.ppermute only.
A program may use at most 64 MiB of HBM per device.

v0:
```python
import jax
import jax.numpy as jnp
from jax import lax
from jax.sharding import PartitionSpec as P

D = 16384


def gate_grads(gate, up, d_hidden):
    sig = jax.nn.sigmoid(gate)
    d_up = (d_hidden * gate * sig).astype(jnp.bfloat16)
    d_gate = (d_hidden * up * sig * (1.0 + gate * (1.0 - sig))).astype(jnp.bfloat16)
    return jnp.stack([d_gate, d_up])


def local(residual_in, grad_out, norm_gain, w_gate, w_up, w_down):
    stream = residual_in.astype(jnp.float32)
    squares = lax.psum(jnp.sum(stream * stream, axis=1), "wa")
    inv_rms = lax.rsqrt(squares / D + 1e-05)[:, None]
    gain_f = norm_gain.astype(jnp.float32)
    normed = (stream * inv_rms * gain_f).astype(jnp.bfloat16)
    stacked = jnp.stack([normed, grad_out])
    piece = lax.all_gather(stacked, "ha", axis=1, tiled=True)
    gate_part = jnp.dot(piece[0], w_gate, preferred_element_type=jnp.float32)
    up_part = jnp.dot(piece[0], w_up, preferred_element_type=jnp.float32)
    back_part = lax.dot_general(
        piece[1], w_down, (((1,), (1,)), ((), ())), preferred_element_type=jnp.float32
    )
    partial_sums = jnp.stack([gate_part, up_part, back_part])
    summed = lax.psum(partial_sums, "wa")
    grads = gate_grads(summed[0], summed[1], summed[2])
    total = lax.dot_general(
        grads[0], w_gate, (((1,), (1,)), ((), ())), preferred_element_type=jnp.float32
    )
    d_normed = lax.psum_scatter(
        total
        + lax.dot_general(
            grads[1], w_up, (((1,), (1,)), ((), ())), preferred_element_type=jnp.float32
        ),
        "ha",
        scatter_dimension=0,
        tiled=True,
    )
    scaled = d_normed * gain_f
    row_dot = lax.psum(jnp.sum(scaled * stream, axis=1), "wa")[:, None]
    grad_in = grad_out.astype(jnp.float32) + inv_rms * scaled - stream * inv_rms**3 * row_dot / D
    return grad_in.astype(jnp.bfloat16)


def solution(mesh):
    placed = (P("ha", "wa"), P("ha", "wa"), P("wa"), P("wa", "ha"), P("wa", "ha"), P("ha", "wa"))
    return jax.shard_map(
        local, mesh=mesh, in_specs=placed, out_specs=P("ha", "wa"), check_vma=False
    )
```

profile of v0, /device:TPU:1, one launch (start us, length us, event | category | flops | bytes accessed | tf_op | source)
XLA Modules:
  0.0 384.8 jit_solution(6059536915146214695)
XLA Ops:
  6.5 0.0 copy-start
  6.5 0.0 copy-start.2
  6.5 0.0 all-reduce.4.cloned.1.call-start
  6.5 1.0 fusion.8
  7.5 69.0 %psum.21 = f32[12]{0:T(128)S(1)} all-reduce(f32[12]{0:T(128)S(1)} %fusion.8), channel_id=1, replica_groups=mesh['wa'=32,'ha'=16] {'wa'}, use_global_device_ids=true, to_apply=%region_1.0 | all-reduce | flops 12 | bytes 96 | tf_op jit(solution)/shard_map/psum | solution.py:18
  76.5 0.7 convert_element_type.23
  77.2 0.8 fusion.16
  78.0 0.7 pad_maximum_fusion.1
  78.8 25.4 %all_gather.3 = bf16[2,192,512]{2,0,1:T(2,128)(2,1)S(1)} all-gather(bf16[2,12,512]{2,0,1:T(2,128)(2,1)S(1)} %copy.7), channel_id=1, replica_groups=mesh['wa'=32,'ha'=16] {'ha'}, dimensions={1}, use_global_device_ids=true | all-gather | bytes 417792 | tf_op jit(solution)/shard_map/all_gather | solution.py:23
  104.2 0.5 fusion.19
  104.7 0.0 copy-done.2
  104.7 0.5 convolution_bitcast_fusion.1
  105.3 0.0 copy-done
  105.3 0.0 copy-start.1
  105.3 0.5 convolution_bitcast_fusion.2
  105.8 0.9 copy-done.1
  106.7 0.7 convolution_bitcast_fusion
  107.4 2.1 pad_maximum_fusion
  109.6 0.0 all-reduce.4.cloned.1.call-update
  109.6 143.8 %all-reduce.4.cloned.1.call-done = f32[3,192,1664]{2,1,0:T(8,128)} async-done(((f32[3,192,1664]{2,1,0:T(8,128)}), f32[3,192,1664]{2,1,0:T(8,128)}) %all-reduce.4.cloned.1.call-update) | async-done | bytes 3833872 | tf_op jit(solution)/shard_map/psum | solution.py:30
  253.4 2.8 fusion.6
  256.2 0.0 copy-start.3
  256.2 0.0 copy-start.4
  256.2 3.2 convolution_add_fusion
  259.5 29.2 %fusion = f32[16,512]{1,0:T(8,128)S(1)} fusion(f32[192,512]{1,0:T(8,128)} %convolution_add_fusion), kind=kCustom, calls=%all-reduce-scatter | all-reduce-scatter fusion | flops 131073 | bytes 428032
  288.7 1.7 collective-permute-start
  290.4 2.7 collective-permute-start.1
  293.2 4.9 %collective-permute-start.2 = (f32[16,512]{1,0:T(8,128)S(1)}, f32[16,512]{1,0:T(8,128)S(1)}, u32[]{:S(2)}, u32[]{:S(2)}) collective-permute-start(f32[16,512]{1,0:T(8,128)S(1)} %fusion), channel_id=1, source_target_pairs={{0,3},{1,4},{2,5},{3,6},{4,7},{5,8},{6,9},{7,10},{8,11},{9,12},{10... | collective-permute-start | bytes 98312
  298.1 5.6 %collective-permute-start.3 = (f32[12,512]{1,0:T(8,128)S(1)}, f32[12,512]{1,0:T(8,128)S(1)}, u32[]{:S(2)}, u32[]{:S(2)}) collective-permute-start(f32[12,512]{1,0:T(8,128)S(1)} %slice.26), channel_id=1, source_target_pairs={{0,4},{1,5},{2,6},{3,7},{4,8},{5,9},{6,10},{7,11},{8,12},{9,13},{1... | collective-permute-start | bytes 73736
  303.7 1.3 dynamic-slice.4
  305.6 0.0 collective-permute-done.3
  305.6 0.0 collective-permute-done
  305.6 0.0 collective-permute-done.1
  305.6 0.0 collective-permute-done.2
  305.6 0.5 concatenate
  306.2 0.0 copy-done.3
  306.2 0.1 fusion.15
  306.3 71.0 %psum.23 = f32[12]{0:T(128)S(1)} all-reduce(f32[12]{0:T(128)S(1)} %fusion.15), channel_id=1, replica_groups=mesh['wa'=32,'ha'=16] {'wa'}, use_global_device_ids=true, to_apply=%region_5.0 | all-reduce | flops 12 | bytes 96 | tf_op jit(solution)/shard_map/psum | solution.py:45
  377.3 0.0 copy-done.4
  377.3 0.7 fusion.14
  (3 shorter events, 0.0 us)
Async XLA Ops:
  6.5 98.7 %copy-start = (bf16[512,1664]{1,0:T(8,128)(2,1)S(1)}, bf16[512,1664]{1,0:T(8,128)(2,1)}, u32[]{:S(2)}) copy-start(bf16[512,1664]{1,0:T(8,128)(2,1)} %param.9) | copy-start | bytes 5111812
  6.5 98.2 %copy-start.2 = (bf16[512,1664]{1,0:T(8,128)(2,1)S(1)}, bf16[512,1664]{1,0:T(8,128)(2,1)}, u32[]{:S(2)}) copy-start(bf16[512,1664]{1,0:T(8,128)(2,1)} %param.10) | copy-start | bytes 5111812
  6.5 246.9 %all-reduce.4.cloned.1.call-start = ((), (), s32[]{:S(2)}) async-start(), calls=%async_computation | async-start | bytes 7667712 | tf_op jit(solution)/shard_map/psum | solution.py:30
  105.3 1.5 copy-start.1
  256.2 50.0 %copy-start.3 = (bf16[12,512]{1,0:T(8,128)(2,1)S(1)}, bf16[12,512]{1,0:T(8,128)(2,1)}, u32[]{:S(2)}) copy-start(bf16[12,512]{1,0:T(8,128)(2,1)} %param.6) | copy-start | bytes 36868
  256.2 121.0 %copy-start.4 = (bf16[12,512]{1,0:T(8,128)(2,1)S(1)}, bf16[12,512]{1,0:T(8,128)(2,1)}, u32[]{:S(2)}) copy-start(bf16[12,512]{1,0:T(8,128)(2,1)} %param.7) | copy-start | bytes 36868
  288.7 16.9 %collective-permute-start = (f32[16,512]{1,0:T(8,128)S(1)}, f32[16,512]{1,0:T(8,128)S(1)}, u32[]{:S(2)}, u32[]{:S(2)}) collective-permute-start(f32[16,512]{1,0:T(8,128)S(1)} %fusion), channel_id=1, source_target_pairs={{0,1},{1,2},{2,3},{3,4},{4,5},{5,6},{6,7},{7,8},{8,9},{9,10},{10,1... | collective-permute-start | bytes 98312
  290.4 15.2 %collective-permute-start.1 = (f32[16,512]{1,0:T(8,128)S(1)}, f32[16,512]{1,0:T(8,128)S(1)}, u32[]{:S(2)}, u32[]{:S(2)}) collective-permute-start(f32[16,512]{1,0:T(8,128)S(1)} %fusion), channel_id=1, source_target_pairs={{0,2},{1,3},{2,4},{3,5},{4,6},{5,7},{6,8},{7,9},{8,10},{9,11},{10,... | collective-permute-start | bytes 98312
  293.2 12.5 %collective-permute-start.2 = (f32[16,512]{1,0:T(8,128)S(1)}, f32[16,512]{1,0:T(8,128)S(1)}, u32[]{:S(2)}, u32[]{:S(2)}) collective-permute-start(f32[16,512]{1,0:T(8,128)S(1)} %fusion), channel_id=1, source_target_pairs={{0,3},{1,4},{2,5},{3,6},{4,7},{5,8},{6,9},{7,10},{8,11},{9,12},{10... | collective-permute-start | bytes 98312
  298.1 7.5 %collective-permute-start.3 = (f32[12,512]{1,0:T(8,128)S(1)}, f32[12,512]{1,0:T(8,128)S(1)}, u32[]{:S(2)}, u32[]{:S(2)}) collective-permute-start(f32[12,512]{1,0:T(8,128)S(1)} %slice.26), channel_id=1, source_target_pairs={{0,4},{1,5},{2,6},{3,7},{4,8},{5,9},{6,10},{7,11},{8,12},{9,13},{1... | collective-permute-start | bytes 73736
Sparse Core Ops, SparseCore 0:
  109.7 143.6 all-reduce.3
where the time goes:
time: 385 us
  blocking collectives  195 us (51%)
  waiting for transfers between devices  144 us (37%)
  starting transfers between devices  14.9 us (4%)
  between operations  14.2 us (4%)
  matrix products  7.8 us (2%)
  other arithmetic  6.15 us (2%)
    psum x1, waiting for transfers between devices, local(): summed = lax.psum(partial_sums, 'wa')  144 us
    psum x1, blocking collectives, local(): row_dot = lax.psum(jnp.sum(scaled * stream, axis=1), 'wa')[:, None]  71 us
    psum x1, blocking collectives, local(): squares = lax.psum(jnp.sum(stream * stream, axis=1), 'wa')  69 us
    unnamed x1, blocking collectives  29.2 us
    all_gather x1, blocking collectives, local(): piece = lax.all_gather(stacked, 'ha', axis=1, tiled=True)  25.4 us
    unnamed x4, starting transfers between devices  14.9 us
  transfers between devices with their start and end apart: 5, of which 1 were waited for; matrix products, arithmetic and copies ran while one was open for 0% of the time, Pallas kernels for 0%

commit v1 on v0

v1 whole, which is shorter than its diff:
```python
import jax
import jax.numpy as jnp
from jax import lax
from jax.sharding import PartitionSpec as P

D = 16384
EXTRA = 128


def gate_grads(gate, up, d_hidden):
    sig = jax.nn.sigmoid(gate)
    d_up = (d_hidden * gate * sig).astype(jnp.bfloat16)
    d_gate = (d_hidden * up * sig * (1.0 + gate * (1.0 - sig))).astype(jnp.bfloat16)
    return d_gate, d_up


def local(residual_in, grad_out, norm_gain, w_gate, w_up, w_down):
    n_ha = lax.axis_size("ha")
    rows = residual_in.shape[0]
    ff = w_gate.shape[1]
    gain_f = norm_gain.astype(jnp.float32)

    piece = lax.all_gather(jnp.stack([residual_in, grad_out]), "ha", axis=1, tiled=True)
    stream_all = piece[0].astype(jnp.float32)
    sq_part = jnp.sum(stream_all * stream_all, axis=1)
    scaled_in = (stream_all * gain_f).astype(jnp.bfloat16)

    gate_part = jnp.dot(scaled_in, w_gate, preferred_element_type=jnp.float32)
    up_part = jnp.dot(scaled_in, w_up, preferred_element_type=jnp.float32)
    back_part = lax.dot_general(
        piece[1], w_down, (((1,), (1,)), ((), ())), preferred_element_type=jnp.float32
    )
    sq_cols = jnp.broadcast_to(sq_part[:, None], (sq_part.shape[0], EXTRA))
    summed = lax.psum(jnp.concatenate([gate_part, up_part, back_part, sq_cols], axis=1), "wa")
    gate_raw = summed[:, :ff]
    up_raw = summed[:, ff : 2 * ff]
    d_hidden = summed[:, 2 * ff : 3 * ff]
    inv_rms_all = lax.rsqrt(summed[:, 3 * ff] / D + 1e-05)[:, None]

    d_gate, d_up = gate_grads(inv_rms_all * gate_raw, inv_rms_all * up_raw, d_hidden)
    dot_part = jnp.sum(
        d_gate.astype(jnp.float32) * gate_raw + d_up.astype(jnp.float32) * up_raw, axis=1
    )
    total = lax.dot_general(
        d_gate, w_gate, (((1,), (1,)), ((), ())), preferred_element_type=jnp.float32
    ) + lax.dot_general(
        d_up, w_up, (((1,), (1,)), ((), ())), preferred_element_type=jnp.float32
    )
    dot_cols = jnp.broadcast_to(dot_part[:, None], (dot_part.shape[0], EXTRA))
    packed = jnp.concatenate([total, dot_cols], axis=1)
    packed = packed.reshape(n_ha, rows, packed.shape[1])
    mine = lax.psum_scatter(packed, "ha", scatter_dimension=0, tiled=True)[0]
    d_normed = mine[:, : total.shape[1]]
    row_dot = mine[:, total.shape[1]][:, None]

    start = lax.axis_index("ha") * rows
    inv_rms = lax.dynamic_slice_in_dim(inv_rms_all, start, rows, axis=0)
    stream = residual_in.astype(jnp.float32)
    scaled = d_normed * gain_f
    grad_in = grad_out.astype(jnp.float32) + inv_rms * scaled - stream * inv_rms**3 * row_dot / D
    return grad_in.astype(jnp.bfloat16)


def solution(mesh):
    placed = (P("ha", "wa"), P("ha", "wa"), P("wa"), P("wa", "ha"), P("wa", "ha"), P("ha", "wa"))
    return jax.shard_map(
        local, mesh=mesh, in_specs=placed, out_specs=P("ha", "wa"), check_vma=False
    )
```

time: 385 us -> 275 us (0.71)
  the two profiles are of different devices: /device:TPU:1 before, /device:TPU:2 now
where the time goes in v1:
time: 275 us
  waiting for transfers between devices  208 us (76%)
  blocking collectives  37.8 us (14%)
  between operations  13.5 us (5%)
  other arithmetic  9.46 us (3%)
  matrix products  3.21 us (1%)
  local copies, waits for them, and re-layouts  2.93 us (1%)
    psum x1, waiting for transfers between devices, local(): lax.psum(jnp.concatenate([gate_part, up_part, back_part, sq_cols], axis=1...  137 us
    reduce_scatter x1, waiting for transfers between devices, local(): mine = lax.psum_scatter(packed, 'ha', scatter_dimension=0, tiled=True)[0]  71 us
    all_gather x1, blocking collectives, local(): lax.all_gather(jnp.stack([residual_in, grad_out]), 'ha', axis=1, tiled=True)  37.8 us
  transfers between devices with their start and end apart: 2, of which 2 were waited for; matrix products, arithmetic and copies ran while one was open for 0% of the time, Pallas kernels for 0%

profile of v1, /device:TPU:2, one launch (start us, length us, event | category | flops | bytes accessed | tf_op | source)
XLA Modules:
  0.0 274.5 jit_solution(7453442533865699771)
XLA Ops:
  6.5 0.0 copy-start
  6.5 0.0 copy-start.5
  6.5 0.0 copy-start.1
  6.5 0.0 all-reduce.2.cloned.1.call-start
  6.5 0.9 pad_maximum_fusion.2
  7.5 37.8 %all_gather.3 = bf16[2,192,512]{2,0,1:T(2,128)(2,1)S(1)} all-gather(bf16[2,12,512]{2,0,1:T(2,128)(2,1)S(1)} %copy.7), channel_id=1, replica_groups=mesh['wa'=32,'ha'=16] {'ha'}, dimensions={1}, use_global_device_ids=true | all-gather | bytes 417792 | tf_op jit(solution)/shard_map/all_gather | solution.py:23
  45.3 0.5 fusion.14
  45.8 0.0 copy-done.5
  45.9 0.1 fusion.1
  46.0 0.0 copy-done.1
  46.0 0.5 fusion.5
  46.5 0.0 copy-done
  46.5 0.0 copy-start.2
  46.6 0.5 fusion.7
  47.1 0.9 copy-done.2
  48.0 0.7 fusion.2
  48.7 0.1 broadcast_in_dim.4
  48.8 2.4 pad_maximum_fusion
  51.2 0.0 all-reduce.2.cloned.1.call-update
  51.2 0.0 reduce-scatter.2.cloned.1.call-start
  51.2 136.5 %all-reduce.2.cloned.1.call-done = f32[192,5120]{1,0:T(8,128)} async-done(((f32[192,5120]{1,0:T(8,128)}), f32[192,5120]{1,0:T(8,128)}) %all-reduce.2.cloned.1.call-update) | async-done | bytes 3932176 | tf_op jit(solution)/shard_map/psum | solution.py:34
  187.8 1.0 fusion.4
  188.8 3.0 %add_reduce_fusion = (f32[192]{0:T(256)S(1)}, bf16[192,1664]{1,0:T(8,128)(2,1)S(1)}, bf16[192,1664]{1,0:T(8,128)(2,1)S(1)}) fusion(f32[192,5120]{1,0:T(8,128)} %all-reduce.2.cloned.1.call-done, f32[192]{0:T(256)S(1)} %get-tuple-element.9), kind=kLoop, calls=%fused_computation.1 | loop fusion | flops 6709056 | bytes 5113344 | tf_op jit(solution)/shard_map/reduce_sum | solution.py:41
  191.8 0.7 fusion.15
  192.5 0.7 convolution_add_fusion
  193.3 0.1 broadcast_in_dim.5
  193.4 0.0 copy-start.3
  193.4 0.0 copy-start.4
  193.4 0.9 reshape.22
  194.3 0.0 reduce-scatter.2.cloned.1.call-update
  194.3 0.1 dynamic-slice_reduce_fusion
  194.5 71.0 %reduce-scatter.2.cloned.1.call-done = f32[1,12,640]{2,1,0:T(8,128)} async-done(((f32[16,12,640]{2,1,0:T(8,128)}), f32[1,12,640]{2,1,0:T(8,128)}) %reduce-scatter.2.cloned.1.call-update) | async-done | bytes 30736 | tf_op jit(solution)/shard_map/reduce_scatter | solution.py:52
  265.4 0.8 slice_reduce_fusion
  266.2 0.0 copy-done.3
  266.2 0.0 copy-done.4
  266.2 1.4 fusion.12
  (4 shorter events, 0.1 us)
Async XLA Ops:
  6.5 40.0 %copy-start = (bf16[512,1664]{1,0:T(8,128)(2,1)S(1)}, bf16[512,1664]{1,0:T(8,128)(2,1)}, u32[]{:S(2)}) copy-start(bf16[512,1664]{1,0:T(8,128)(2,1)} %param.9) | copy-start | bytes 5111812
  6.5 39.3 %copy-start.5 = (bf16[512]{0:T(512)(128)(2,1)S(1)}, bf16[512]{0:T(512)(128)(2,1)}, u32[]{:S(2)}) copy-start(bf16[512]{0:T(512)(128)(2,1)} %param.8) | copy-start | bytes 3076
  6.5 39.4 %copy-start.1 = (bf16[512,1664]{1,0:T(8,128)(2,1)S(1)}, bf16[512,1664]{1,0:T(8,128)(2,1)}, u32[]{:S(2)}) copy-start(bf16[512,1664]{1,0:T(8,128)(2,1)} %param.10) | copy-start | bytes 5111812
  6.5 181.2 %all-reduce.2.cloned.1.call-start = ((), (), s32[]{:S(2)}) async-start(), calls=%async_computation.1 | async-start | bytes 7864320 | tf_op jit(solution)/shard_map/psum | solution.py:34
  46.5 1.5 copy-start.2
  51.2 214.2 %reduce-scatter.2.cloned.1.call-start = ((), (), s32[]{:S(2)}) async-start(), calls=%async_computation.2 | async-start | bytes 696320 | tf_op jit(solution)/shard_map/reduce_scatter | solution.py:52
  193.4 72.9 %copy-start.3 = (bf16[12,512]{1,0:T(8,128)(2,1)S(1)}, bf16[12,512]{1,0:T(8,128)(2,1)}, u32[]{:S(2)}) copy-start(bf16[12,512]{1,0:T(8,128)(2,1)} %param.7) | copy-start | bytes 36868
  193.4 72.9 %copy-start.4 = (bf16[12,512]{1,0:T(8,128)(2,1)S(1)}, bf16[12,512]{1,0:T(8,128)(2,1)}, u32[]{:S(2)}) copy-start(bf16[12,512]{1,0:T(8,128)(2,1)} %param.6) | copy-start | bytes 36868
Sparse Core Ops, SparseCore 0:
  51.3 136.4 all-reduce.1
  194.5 70.9 reduce-scatter.1

commit v2 on v1

v2 whole, which is shorter than its diff:
```python
import jax
import jax.numpy as jnp
from jax import lax
from jax.sharding import Mesh
from jax.sharding import PartitionSpec as P

D = 16384
WA = ("x", "y", "core")


def gate_grads(gate, up, d_hidden):
    sig = jax.nn.sigmoid(gate)
    d_up = (d_hidden * gate * sig).astype(jnp.bfloat16)
    d_gate = (d_hidden * up * sig * (1.0 + gate * (1.0 - sig))).astype(jnp.bfloat16)
    return d_gate, d_up


def local(residual_in, grad_out, norm_gain, w_gate, w_up, w_down):
    rows = residual_in.shape[0]
    gain_f = norm_gain.astype(jnp.float32)

    piece = lax.all_gather(jnp.stack([residual_in, grad_out]), "ha", axis=1, tiled=True)
    stream_all = piece[0].astype(jnp.float32)
    squares = jnp.sum(stream_all * stream_all, axis=1)
    squares = lax.psum(lax.psum(lax.psum(squares, "core"), "y"), "x")
    inv_rms_all = lax.rsqrt(squares / D + 1e-05)[:, None]
    normed = (stream_all * inv_rms_all * gain_f).astype(jnp.bfloat16)

    gate_part = jnp.dot(normed, w_gate, preferred_element_type=jnp.float32)
    up_part = jnp.dot(normed, w_up, preferred_element_type=jnp.float32)
    back_part = lax.dot_general(
        piece[1], w_down, (((1,), (1,)), ((), ())), preferred_element_type=jnp.float32
    )
    summed = lax.psum(jnp.stack([gate_part, up_part, back_part]), WA)
    gate, up, d_hidden = summed[0], summed[1], summed[2]

    d_gate, d_up = gate_grads(gate, up, d_hidden)
    dot_part = jnp.sum(d_gate.astype(jnp.float32) * gate + d_up.astype(jnp.float32) * up, axis=1)
    total = lax.dot_general(
        d_gate, w_gate, (((1,), (1,)), ((), ())), preferred_element_type=jnp.float32
    ) + lax.dot_general(
        d_up, w_up, (((1,), (1,)), ((), ())), preferred_element_type=jnp.float32
    )
    n_ha, width = lax.axis_size("ha"), total.shape[1]
    dot_rows = jnp.pad(dot_part.reshape(n_ha, 1, rows), ((0, 0), (0, 0), (0, width - rows)))
    packed = jnp.concatenate([total.reshape(n_ha, rows, width), dot_rows], axis=1)
    mine = lax.psum_scatter(packed.reshape(-1, width), "ha", scatter_dimension=0, tiled=True)
    d_normed = mine[:rows]

    start = lax.axis_index("ha") * rows
    inv_rms = lax.dynamic_slice_in_dim(inv_rms_all, start, rows, axis=0)
    row_dot = mine[rows, :rows][:, None] / inv_rms
    stream = residual_in.astype(jnp.float32)
    scaled = d_normed * gain_f
    grad_in = grad_out.astype(jnp.float32) + inv_rms * scaled - stream * inv_rms**3 * row_dot / D
    return grad_in.astype(jnp.bfloat16)


def solution(mesh):
    devices = mesh.devices if mesh.axis_names[0] == "wa" else mesh.devices.T
    view = Mesh(devices.reshape(4, 4, 2, devices.shape[1]), WA + ("ha",))
    placed = (P("ha", WA), P("ha", WA), P(WA), P(WA, "ha"), P(WA, "ha"), P("ha", WA))
    return jax.shard_map(
        local, mesh=view, in_specs=placed, out_specs=P("ha", WA), check_vma=False
    )
```

time: 275 us -> 364 us (1.32)
  waiting for transfers between devices: 208 us -> 270 us
  blocking collectives: 37.8 us -> 59.6 us
    unnamed x2 -> x3, waiting for transfers between devices: 0.03 us -> 136 us
    reduce_scatter x1 -> x0, waiting for transfers between devices: 71 us -> none  [local(): mine = lax.psum_scatter(packed, 'ha', scatter_dimension=0, tiled=True)[0]]
    psum x0 -> x3, blocking collectives: none -> 21.8 us  [local(): squares = lax.psum(lax.psum(lax.psum(squares, 'core'), 'y'), 'x')]
where the time goes in v2:
time: 364 us
  waiting for transfers between devices  270 us (74%)
  blocking collectives  59.6 us (16%)
  between operations  14.2 us (4%)
  other arithmetic  9.68 us (3%)
  matrix products  5.11 us (1%)
  local copies, waits for them, and re-layouts  4.91 us (1%)
    unnamed x3, waiting for transfers between devices  136 us
    psum x1, waiting for transfers between devices, local(): summed = lax.psum(jnp.stack([gate_part, up_part, back_part]), WA)  134 us
    all_gather x1, blocking collectives, local(): lax.all_gather(jnp.stack([residual_in, grad_out]), 'ha', axis=1, tiled=True)  37.8 us
    psum x3, blocking collectives, local(): squares = lax.psum(lax.psum(lax.psum(squares, 'core'), 'y'), 'x')  21.8 us
  transfers between devices with their start and end apart: 2, of which 2 were waited for; matrix products, arithmetic and copies ran while one was open for 0% of the time, Pallas kernels for 0%

profile of v2, /device:TPU:2, one launch (start us, length us, event | category | flops | bytes accessed | tf_op | source)
XLA Modules:
  0.0 363.5 jit_solution(15139991436451758172)
XLA Ops:
  6.5 0.0 copy-start
  6.5 0.0 copy-start.8
  6.5 0.0 copy-start.1
  6.5 0.0 all-reduce.5.cloned.1.call-start
  6.5 0.9 pad_maximum_fusion.1
  7.5 37.8 %all_gather.3 = bf16[2,192,512]{2,0,1:T(2,128)(2,1)S(1)} all-gather(bf16[2,12,512]{2,0,1:T(2,128)(2,1)S(1)} %copy.9), channel_id=1, replica_groups=mesh['x'=4,'y'=4,'core'=2,'ha'=16] {'ha'}, dimensions={1}, use_global_device_ids=true | all-gather | bytes 417792 | tf_op jit(solution)/shard_map/all_gather | solution.py:22
  45.3 1.3 slice_convert_fusion
  46.6 0.0 copy-start.2
  46.6 0.7 copy-done.2
  47.3 0.1 fusion
  47.4 2.5 psum.28
  49.9 10.7 %psum.29 = f32[192]{0:T(256)S(1)} all-reduce(f32[192]{0:T(256)S(1)} %psum.28), channel_id=1, replica_groups=mesh['x'=4,'y'=4,'core'=2,'ha'=16] {'y'}, use_global_device_ids=true, to_apply=%region_2.0 | all-reduce | flops 192 | bytes 1536 | tf_op jit(solution)/shard_map/psum | solution.py:25
  60.6 8.6 %psum.30 = f32[192]{0:T(256)S(1)} all-reduce(f32[192]{0:T(256)S(1)} %psum.29), channel_id=1, replica_groups=mesh['x'=4,'y'=4,'core'=2,'ha'=16] {'x'}, use_global_device_ids=true, to_apply=%region_3.0 | all-reduce | flops 192 | bytes 1536 | tf_op jit(solution)/shard_map/psum | solution.py:25
  69.2 0.0 copy-done.8
  69.2 0.0 copy-done.1
  69.2 0.0 copy-start.3
  69.3 1.6 convolution_bitcast_fusion.1
  70.9 0.0 copy-done
  70.9 0.0 copy-done.3
  70.9 0.0 copy-start.4
  70.9 0.0 copy-start.5
  70.9 0.6 convolution_bitcast_fusion.2
  71.5 0.8 copy-done.4
  72.4 0.1 copy-done.5
  72.4 0.7 convolution_bitcast_fusion
  73.2 2.1 pad_maximum_fusion
  75.3 0.0 all-reduce.5.cloned.1.call-update
  75.3 0.0 all-reduce.7.cloned.1.call-start
  75.4 134.0 %all-reduce.5.cloned.1.call-done = f32[3,192,1664]{2,1,0:T(8,128)} async-done(((f32[3,192,1664]{2,1,0:T(8,128)}), f32[3,192,1664]{2,1,0:T(8,128)}) %all-reduce.5.cloned.1.call-update) | async-done | bytes 3833872 | tf_op jit(solution)/shard_map/psum | solution.py:34
  209.3 2.9 add_reduce_fusion
  212.3 0.7 fusion.11
  213.0 1.5 convolution_add_fusion
  214.5 1.0 reshape.21
  215.5 0.0 copy-start.6
  215.5 0.0 copy-start.7
  215.5 0.1 reshape.22
  215.6 0.1 select_maximum_fusion
  215.7 0.8 reshape.23
  216.5 0.0 all-reduce.7.cloned.1.call-update
  216.5 1.3 dynamic-slice.4
  218.4 0.1 multiply_multiply_fusion
  218.5 136.0 %all-reduce.7.cloned.1.call-done = f32[208,512]{1,0:T(8,128)} async-done(((f32[208,512]{1,0:T(8,128)}), f32[208,512]{1,0:T(8,128)}) %all-reduce.7.cloned.1.call-update) | async-done | bytes 426000
  354.5 0.7 fusion.8
  355.2 0.0 copy-done.6
  355.2 0.0 copy-done.7
  355.2 1.5 fusion.6
  (3 shorter events, 0.0 us)
Async XLA Ops:
  6.5 64.4 %copy-start = (bf16[512,1664]{1,0:T(8,128)(2,1)S(1)}, bf16[512,1664]{1,0:T(8,128)(2,1)}, u32[]{:S(2)}) copy-start(bf16[512,1664]{1,0:T(8,128)(2,1)} %param.9) | copy-start | bytes 5111812
  6.5 62.7 %copy-start.8 = (bf16[512]{0:T(512)(128)(2,1)S(1)}, bf16[512]{0:T(512)(128)(2,1)}, u32[]{:S(2)}) copy-start(bf16[512]{0:T(512)(128)(2,1)} %param.8) | copy-start | bytes 3076
  6.5 62.7 %copy-start.1 = (bf16[512,1664]{1,0:T(8,128)(2,1)S(1)}, bf16[512,1664]{1,0:T(8,128)(2,1)}, u32[]{:S(2)}) copy-start(bf16[512,1664]{1,0:T(8,128)(2,1)} %param.10) | copy-start | bytes 5111812
  6.5 202.8 %all-reduce.5.cloned.1.call-start = ((), (), s32[]{:S(2)}) async-start(), calls=%async_computation | async-start | bytes 7667712 | tf_op jit(solution)/shard_map/psum | solution.py:34
  46.6 0.7 copy-start.2
  69.2 1.7 copy-start.3
  70.9 1.5 copy-start.4
  70.9 1.5 copy-start.5
  75.3 279.2 %all-reduce.7.cloned.1.call-start = ((), (), s32[]{:S(2)}) async-start(), calls=%async_computation.1 | async-start | bytes 851968
  215.5 139.7 %copy-start.6 = (bf16[12,512]{1,0:T(8,128)(2,1)S(1)}, bf16[12,512]{1,0:T(8,128)(2,1)}, u32[]{:S(2)}) copy-start(bf16[12,512]{1,0:T(8,128)(2,1)} %param.7) | copy-start | bytes 36868
  215.5 139.7 %copy-start.7 = (bf16[12,512]{1,0:T(8,128)(2,1)S(1)}, bf16[12,512]{1,0:T(8,128)(2,1)}, u32[]{:S(2)}) copy-start(bf16[12,512]{1,0:T(8,128)(2,1)} %param.6) | copy-start | bytes 36868
Sparse Core Ops, SparseCore 0:
  75.4 133.8 all-reduce.4
  216.6 137.8 all-reduce.6

commit v3 on v2

--- a/solution.py
+++ b/solution.py
@@ -15,11 +15,42 @@
     return d_gate, d_up
 
 
+def _partner(axis, bit):
+    n = lax.axis_size(axis)
+    return [(i, i ^ (1 << bit)) for i in range(n)]
+
+
+def _bit(axis, bit):
+    return (lax.axis_index(axis) >> bit) & 1
+
+
+def gather_rows(x, axis):
+    n = lax.axis_size(axis)
+    held = x[:, None]
+    for bit in reversed(range(n.bit_length() - 1)):
+        got = lax.ppermute(held, axis, _partner(axis, bit))
+        low = _bit(axis, bit) == 0
+        held = jnp.stack([jnp.where(low, held, got), jnp.where(low, got, held)], axis=2)
+        held = held.reshape(held.shape[0], -1, *held.shape[3:])
+    return held.reshape(x.shape[0], n * x.shape[1], x.shape[2])
+
+
+def scatter_sum(x, axis):
+    n = lax.axis_size(axis)
+    for bit in range(n.bit_length() - 1):
+        pairs = x.reshape(-1, 2, *x.shape[1:])
+        mine = _bit(axis, bit)
+        keep = lax.dynamic_index_in_dim(pairs, mine, axis=1, keepdims=False)
+        send = lax.dynamic_index_in_dim(pairs, 1 - mine, axis=1, keepdims=False)
+        x = keep + lax.ppermute(send, axis, _partner(axis, bit))
+    return x[0]
+
+
 def local(residual_in, grad_out, norm_gain, w_gate, w_up, w_down):
     rows = residual_in.shape[0]
     gain_f = norm_gain.astype(jnp.float32)
 
-    piece = lax.all_gather(jnp.stack([residual_in, grad_out]), "ha", axis=1, tiled=True)
+    piece = gather_rows(jnp.stack([residual_in, grad_out]), "ha")
     stream_all = piece[0].astype(jnp.float32)
     squares = jnp.sum(stream_all * stream_all, axis=1)
     squares = lax.psum(lax.psum(lax.psum(squares, "core"), "y"), "x")
@@ -44,7 +75,7 @@
     n_ha, width = lax.axis_size("ha"), total.shape[1]
     dot_rows = jnp.pad(dot_part.reshape(n_ha, 1, rows), ((0, 0), (0, 0), (0, width - rows)))
     packed = jnp.concatenate([total.reshape(n_ha, rows, width), dot_rows], axis=1)
-    mine = lax.psum_scatter(packed.reshape(-1, width), "ha", scatter_dimension=0, tiled=True)
+    mine = scatter_sum(packed, "ha")
     d_normed = mine[:rows]
 
     start = lax.axis_index("ha") * rows

time: 364 us -> 290 us (0.80)
  the two profiles are of different devices: /device:TPU:2 before, /device:TPU:1 now
where the time goes in v3:
time: 290 us; the launch traced here: 289 us
  waiting for transfers between devices  165 us (57%)
  starting transfers between devices  59.8 us (21%)
  blocking collectives  26.1 us (9%)
  between operations  13.8 us (5%)
  other arithmetic  9.22 us (3%)
  matrix products  9.04 us (3%)
  local copies, waits for them, and re-layouts  5.93 us (2%)
    psum x1, waiting for transfers between devices, local(): summed = lax.psum(jnp.stack([gate_part, up_part, back_part]), WA)  141 us
    ppermute x4, starting transfers between devices, scatter_sum(): x = keep + lax.ppermute(send, axis, _partner(axis, bit))  31 us
    ppermute x4, starting transfers between devices, gather_rows(): got = lax.ppermute(held, axis, _partner(axis, bit))  28.8 us
    psum x3, blocking collectives, local(): squares = lax.psum(lax.psum(lax.psum(squares, 'core'), 'y'), 'x')  26.1 us
    ppermute x4, waiting for transfers between devices, gather_rows(): got = lax.ppermute(held, axis, _partner(axis, bit))  12.5 us
    ppermute x4, waiting for transfers between devices, scatter_sum(): x = keep + lax.ppermute(send, axis, _partner(axis, bit))  11.4 us
  transfers between devices with their start and end apart: 9, of which 9 were waited for; matrix products, arithmetic and copies ran while one was open for 0% of the time, Pallas kernels for 0%

profile of v3, /device:TPU:1, one launch (start us, length us, event | category | flops | bytes accessed | tf_op | source)
XLA Modules:
  0.0 288.8 jit_solution(557949555505917510)
XLA Ops:
  6.5 0.9 maximum_bitcast_fusion.1
  7.4 16.3 %collective-permute-start = (bf16[2,1,12,512]{3,2,0,1:T(8,128)(2,1)S(1)}, bf16[2,1,12,512]{3,2,0,1:T(8,128)(2,1)S(1)}, u32[]{:S(2)}, u32[]{:S(2)}) collective-permute-start(bf16[2,1,12,512]{3,2,0,1:T(8,128)(2,1)S(1)} %maximum_bitcast_fusion.1), channel_id=1, source_target_pairs={{0,8},{1,9},{2,10},{3,11},{4,12},{5,13},{6,14},{7,15},{8,0},{9,1},... | collective-permute-start | bytes 73736 | tf_op jit(solution)/shard_map/ppermute | solution.py:31
  23.7 1.4 collective-permute-done
  25.1 0.7 select_bitcast_fusion.5
  25.8 5.3 %collective-permute-start.1 = (bf16[2,2,12,512]{3,2,0,1:T(8,128)(2,1)S(1)}, bf16[2,2,12,512]{3,2,0,1:T(8,128)(2,1)S(1)}, u32[]{:S(2)}, u32[]{:S(2)}) collective-permute-start(bf16[2,2,12,512]{3,2,0,1:T(8,128)(2,1)S(1)} %maximum_bitcast_fusion), channel_id=1, source_target_pairs={{0,4},{1,5},{2,6},{3,7},{4,0},{5,1},{6,2},{7,3},{8,12},{9,13},{10,... | collective-permute-start | bytes 147464 | tf_op jit(solution)/shard_map/ppermute | solution.py:31
  31.2 4.3 %collective-permute-done.1 = bf16[2,2,12,512]{3,2,0,1:T(8,128)(2,1)S(1)} collective-permute-done((bf16[2,2,12,512]{3,2,0,1:T(8,128)(2,1)S(1)}, bf16[2,2,12,512]{3,2,0,1:T(8,128)(2,1)S(1)}, u32[]{:S(2)}, u32[]{:S(2)}) %collective-permute-start.1) | collective-permute-done | bytes 49184 | tf_op jit(solution)/shard_map/ppermute | solution.py:31
  35.5 0.1 copy.33
  35.6 5.3 %collective-permute-start.2 = (bf16[2,4,12,512]{3,0,2,1:T(2,128)(2,1)S(1)}, bf16[2,4,12,512]{3,0,2,1:T(2,128)(2,1)S(1)}, u32[]{:S(2)}, u32[]{:S(2)}) collective-permute-start(bf16[2,4,12,512]{3,0,2,1:T(2,128)(2,1)S(1)} %bitcast.115), channel_id=1, source_target_pairs={{0,2},{1,3},{2,0},{3,1},{4,6},{5,7},{6,4},{7,5},{8,10},{9,11},{10,... | collective-permute-start | bytes 294920 | tf_op jit(solution)/shard_map/ppermute | solution.py:31
  40.9 2.0 collective-permute-done.2
  42.9 0.2 fusion.4
  43.1 0.3 pad_maximum_fusion.2
  43.4 0.1 copy.34
  43.6 1.9 collective-permute-start.3
  45.6 4.9 %collective-permute-done.3 = bf16[2,8,12,512]{3,1,2,0:T(8,128)(2,1)S(1)} collective-permute-done((bf16[2,8,12,512]{3,1,2,0:T(8,128)(2,1)S(1)}, bf16[2,8,12,512]{3,1,2,0:T(8,128)(2,1)S(1)}, u32[]{:S(2)}, u32[]{:S(2)}) %collective-permute-start.3) | collective-permute-done | bytes 196640 | tf_op jit(solution)/shard_map/ppermute | solution.py:31
  50.4 0.1 select_bitcast_fusion.1
  50.6 0.1 multiply_reduce_fusion
  50.7 0.7 fusion.3
  51.5 0.1 reduce_sum.21
  51.6 9.0 %psum.28 = f32[192]{0:T(256)S(1)} all-reduce(f32[192]{0:T(256)S(1)} %reduce_sum.21), channel_id=1, replica_groups=mesh['x'=4,'y'=4,'core'=2,'ha'=16] {'core'}, use_global_device_ids=true, to_apply=%region_1.2 | all-reduce | flops 192 | bytes 1536 | tf_op jit(solution)/shard_map/psum | solution.py:56
  60.6 8.7 %psum.29 = f32[192]{0:T(256)S(1)} all-reduce(f32[192]{0:T(256)S(1)} %psum.28), channel_id=1, replica_groups=mesh['x'=4,'y'=4,'core'=2,'ha'=16] {'y'}, use_global_device_ids=true, to_apply=%region_2.3 | all-reduce | flops 192 | bytes 1536 | tf_op jit(solution)/shard_map/psum | solution.py:56
  69.3 8.5 %psum.30 = f32[192]{0:T(256)S(1)} all-reduce(f32[192]{0:T(256)S(1)} %psum.29), channel_id=1, replica_groups=mesh['x'=4,'y'=4,'core'=2,'ha'=16] {'x'}, use_global_device_ids=true, to_apply=%region_3.4 | all-reduce | flops 192 | bytes 1536 | tf_op jit(solution)/shard_map/psum | solution.py:56
  77.7 0.2 copy.41
  78.0 0.8 reshape.52
  78.8 2.8 convolution_bitcast_fusion.2
  81.6 1.6 convolution_bitcast_fusion.1
  83.2 0.8 copy.42
  84.0 1.7 squeeze.44
  85.7 2.4 convolution_bitcast_fusion
  88.1 2.1 pad_maximum_fusion
  90.3 140.9 %all-reduce.3.cloned.1.call-done = f32[3,192,1664]{2,1,0:T(8,128)} async-done(((f32[3,192,1664]{2,1,0:T(8,128)}), f32[3,192,1664]{2,1,0:T(8,128)}) %all-reduce.3.cloned.1.call-update) | async-done | bytes 3833872 | tf_op jit(solution)/shard_map/psum | solution.py:65
  231.2 2.9 %add_reduce_fusion = (f32[192]{0:T(256)S(1)}, bf16[192,1664]{1,0:T(8,128)(2,1)S(1)}, bf16[192,1664]{1,0:T(8,128)(2,1)S(1)}) fusion(f32[3,192,1664]{2,1,0:T(8,128)} %all-reduce.3.cloned.1.call-done), kind=kLoop, calls=%fused_computation.7 | loop fusion | flops 6070080 | bytes 5112576 | tf_op jit(solution)/shard_map/reduce_sum | solution.py:69
  234.1 0.7 fusion.11
  234.8 1.5 convolution_add_fusion
  236.3 1.0 concatenate.8
  237.6 0.1 copy.63
  237.7 3.2 %collective-permute-start.4 = (f32[8,13,512]{2,0,1:T(8,128)S(1)}, f32[8,13,512]{2,0,1:T(8,128)S(1)}, u32[]{:S(2)}, u32[]{:S(2)}) collective-permute-start(f32[8,13,512]{2,0,1:T(8,128)S(1)} %bitcast.116), channel_id=1, source_target_pairs={{0,1},{1,0},{2,3},{3,2},{4,5},{5,4},{6,7},{7,6},{8,9},{9,8},{10,11... | collective-permute-start | bytes 638984 | tf_op jit(solution)/shard_map/ppermute | solution.py:45
  240.9 5.1 %collective-permute-done.4 = f32[8,13,512]{2,0,1:T(8,128)S(1)} collective-permute-done((f32[8,13,512]{2,0,1:T(8,128)S(1)}, f32[8,13,512]{2,0,1:T(8,128)S(1)}, u32[]{:S(2)}, u32[]{:S(2)}) %collective-permute-start.4) | collective-permute-done | bytes 213024 | tf_op jit(solution)/shard_map/ppermute | solution.py:45
  246.0 0.1 bitcast_add_fusion
  246.1 0.1 reshape.50
  246.3 0.2 constant_dynamic-slice_fusion.4
  246.5 4.2 %collective-permute-start.5 = (f32[4,13,512]{2,0,1:T(4,128)S(1)}, f32[4,13,512]{2,0,1:T(4,128)S(1)}, u32[]{:S(2)}, u32[]{:S(2)}) collective-permute-start(f32[4,13,512]{2,0,1:T(4,128)S(1)} %bitcast.121), channel_id=1, source_target_pairs={{0,2},{1,3},{2,0},{3,1},{4,6},{5,7},{6,4},{7,5},{8,10},{9,11},{10,... | collective-permute-start | bytes 319496 | tf_op jit(solution)/shard_map/ppermute | solution.py:45
  250.7 3.7 %collective-permute-done.5 = f32[4,13,512]{2,0,1:T(4,128)S(1)} collective-permute-done((f32[4,13,512]{2,0,1:T(4,128)S(1)}, f32[4,13,512]{2,0,1:T(4,128)S(1)}, u32[]{:S(2)}, u32[]{:S(2)}) %collective-permute-start.5) | collective-permute-done | bytes 106528 | tf_op jit(solution)/shard_map/ppermute | solution.py:45
  254.5 0.1 constant_dynamic-slice_fusion.2
  254.7 7.3 %collective-permute-start.6 = (f32[2,13,512]{2,0,1:T(2,128)S(1)}, f32[2,13,512]{2,0,1:T(2,128)S(1)}, u32[]{:S(2)}, u32[]{:S(2)}) collective-permute-start(f32[2,13,512]{2,0,1:T(2,128)S(1)} %bitcast.122), channel_id=1, source_target_pairs={{0,4},{1,5},{2,6},{3,7},{4,0},{5,1},{6,2},{7,3},{8,12},{9,13},{10,... | collective-permute-start | bytes 159752 | tf_op jit(solution)/shard_map/ppermute | solution.py:45
  262.0 1.5 collective-permute-done.6
  263.6 16.3 %collective-permute-start.7 = (f32[1,13,512]{2,0,1:T(1,128)S(1)}, f32[1,13,512]{2,0,1:T(1,128)S(1)}, u32[]{:S(2)}, u32[]{:S(2)}) collective-permute-start(f32[1,13,512]{2,0,1:T(1,128)S(1)} %constant_dynamic-slice_fusion), channel_id=1, source_target_pairs={{0,8},{1,9},{2,10},{3,11},{4,12},{5,13},{6,14},{7,15},{8,0},{9,1},... | collective-permute-start | bytes 79880 | tf_op jit(solution)/shard_map/ppermute | solution.py:45
  280.0 1.1 collective-permute-done.7
  281.2 0.7 fusion.9
  (42 shorter events, 0.9 us)
Async XLA Ops:
  6.5 72.2 %copy-start = (bf16[512,1664]{1,0:T(8,128)(2,1)S(1)}, bf16[512,1664]{1,0:T(8,128)(2,1)}, u32[]{:S(2)}) copy-start(bf16[512,1664]{1,0:T(8,128)(2,1)} %param.9) | copy-start | bytes 5111812
  6.5 224.6 %all-reduce.3.cloned.1.call-start = ((), (), s32[]{:S(2)}) async-start(), calls=%async_computation | async-start | bytes 7667712 | tf_op jit(solution)/shard_map/psum | solution.py:65
  7.4 17.7 %collective-permute-start = (bf16[2,1,12,512]{3,2,0,1:T(8,128)(2,1)S(1)}, bf16[2,1,12,512]{3,2,0,1:T(8,128)(2,1)S(1)}, u32[]{:S(2)}, u32[]{:S(2)}) collective-permute-start(bf16[2,1,12,512]{3,2,0,1:T(8,128)(2,1)S(1)} %maximum_bitcast_fusion.1), channel_id=1, source_target_pairs={{0,8},{1,9},{2,10},{3,11},{4,12},{5,13},{6,14},{7,15},{8,0},{9,1},... | collective-permute-start | bytes 73736 | tf_op jit(solution)/shard_map/ppermute | solution.py:31
  25.8 19.7 %copy-start.8 = (bf16[512]{0:T(512)(128)(2,1)S(1)}, bf16[512]{0:T(512)(128)(2,1)}, u32[]{:S(2)}) copy-start(bf16[512]{0:T(512)(128)(2,1)} %param.8) | copy-start | bytes 3076
  25.8 9.6 %collective-permute-start.1 = (bf16[2,2,12,512]{3,2,0,1:T(8,128)(2,1)S(1)}, bf16[2,2,12,512]{3,2,0,1:T(8,128)(2,1)S(1)}, u32[]{:S(2)}, u32[]{:S(2)}) collective-permute-start(bf16[2,2,12,512]{3,2,0,1:T(8,128)(2,1)S(1)} %maximum_bitcast_fusion), channel_id=1, source_target_pairs={{0,4},{1,5},{2,6},{3,7},{4,0},{5,1},{6,2},{7,3},{8,12},{9,13},{10,... | collective-permute-start | bytes 147464 | tf_op jit(solution)/shard_map/ppermute | solution.py:31
  35.6 7.3 %collective-permute-start.2 = (bf16[2,4,12,512]{3,0,2,1:T(2,128)(2,1)S(1)}, bf16[2,4,12,512]{3,0,2,1:T(2,128)(2,1)S(1)}, u32[]{:S(2)}, u32[]{:S(2)}) collective-permute-start(bf16[2,4,12,512]{3,0,2,1:T(2,128)(2,1)S(1)} %bitcast.115), channel_id=1, source_target_pairs={{0,2},{1,3},{2,0},{3,1},{4,6},{5,7},{6,4},{7,5},{8,10},{9,11},{10,... | collective-permute-start | bytes 294920 | tf_op jit(solution)/shard_map/ppermute | solution.py:31
  43.6 6.8 %collective-permute-start.3 = (bf16[2,8,12,512]{3,1,2,0:T(8,128)(2,1)S(1)}, bf16[2,8,12,512]{3,1,2,0:T(8,128)(2,1)S(1)}, u32[]{:S(2)}, u32[]{:S(2)}) collective-permute-start(bf16[2,8,12,512]{3,1,2,0:T(8,128)(2,1)S(1)} %copy.36), channel_id=1, source_target_pairs={{0,1},{1,0},{2,3},{3,2},{4,5},{5,4},{6,7},{7,6},{8,9},{9,8},{10,11... | collective-permute-start | bytes 589832 | tf_op jit(solution)/shard_map/ppermute | solution.py:31
  78.8 2.8 copy-start.1
  78.8 2.8 copy-start.4
  81.6 1.6 copy-start.5
  85.7 2.4 copy-start.2
  85.7 2.4 copy-start.3
  237.7 8.3 %collective-permute-start.4 = (f32[8,13,512]{2,0,1:T(8,128)S(1)}, f32[8,13,512]{2,0,1:T(8,128)S(1)}, u32[]{:S(2)}, u32[]{:S(2)}) collective-permute-start(f32[8,13,512]{2,0,1:T(8,128)S(1)} %bitcast.116), channel_id=1, source_target_pairs={{0,1},{1,0},{2,3},{3,2},{4,5},{5,4},{6,7},{7,6},{8,9},{9,8},{10,11... | collective-permute-start | bytes 638984 | tf_op jit(solution)/shard_map/ppermute | solution.py:45
  246.1 35.1 %copy-start.6 = (bf16[12,512]{1,0:T(8,128)(2,1)S(1)}, bf16[12,512]{1,0:T(8,128)(2,1)}, u32[]{:S(2)}) copy-start(bf16[12,512]{1,0:T(8,128)(2,1)} %param.7) | copy-start | bytes 36868
  246.1 35.1 %copy-start.7 = (bf16[12,512]{1,0:T(8,128)(2,1)S(1)}, bf16[12,512]{1,0:T(8,128)(2,1)}, u32[]{:S(2)}) copy-start(bf16[12,512]{1,0:T(8,128)(2,1)} %param.6) | copy-start | bytes 36868
  246.5 7.9 %collective-permute-start.5 = (f32[4,13,512]{2,0,1:T(4,128)S(1)}, f32[4,13,512]{2,0,1:T(4,128)S(1)}, u32[]{:S(2)}, u32[]{:S(2)}) collective-permute-start(f32[4,13,512]{2,0,1:T(4,128)S(1)} %bitcast.121), channel_id=1, source_target_pairs={{0,2},{1,3},{2,0},{3,1},{4,6},{5,7},{6,4},{7,5},{8,10},{9,11},{10,... | collective-permute-start | bytes 319496 | tf_op jit(solution)/shard_map/ppermute | solution.py:45
  254.7 8.8 %collective-permute-start.6 = (f32[2,13,512]{2,0,1:T(2,128)S(1)}, f32[2,13,512]{2,0,1:T(2,128)S(1)}, u32[]{:S(2)}, u32[]{:S(2)}) collective-permute-start(f32[2,13,512]{2,0,1:T(2,128)S(1)} %bitcast.122), channel_id=1, source_target_pairs={{0,4},{1,5},{2,6},{3,7},{4,0},{5,1},{6,2},{7,3},{8,12},{9,13},{10,... | collective-permute-start | bytes 159752 | tf_op jit(solution)/shard_map/ppermute | solution.py:45
  263.6 17.5 %collective-permute-start.7 = (f32[1,13,512]{2,0,1:T(1,128)S(1)}, f32[1,13,512]{2,0,1:T(1,128)S(1)}, u32[]{:S(2)}, u32[]{:S(2)}) collective-permute-start(f32[1,13,512]{2,0,1:T(1,128)S(1)} %constant_dynamic-slice_fusion), channel_id=1, source_target_pairs={{0,8},{1,9},{2,10},{3,11},{4,12},{5,13},{6,14},{7,15},{8,0},{9,1},... | collective-permute-start | bytes 79880 | tf_op jit(solution)/shard_map/ppermute | solution.py:45
Sparse Core Ops, SparseCore 0:
  90.4 140.7 all-reduce.2

commit v4 on v3

--- a/solution.py
+++ b/solution.py
@@ -50,7 +50,7 @@
     rows = residual_in.shape[0]
     gain_f = norm_gain.astype(jnp.float32)
 
-    piece = gather_rows(jnp.stack([residual_in, grad_out]), "ha")
+    piece = lax.all_gather(jnp.stack([residual_in, grad_out]), "ha", axis=1, tiled=True)
     stream_all = piece[0].astype(jnp.float32)
     squares = jnp.sum(stream_all * stream_all, axis=1)
     squares = lax.psum(lax.psum(lax.psum(squares, "core"), "y"), "x")
@@ -62,11 +62,16 @@
     back_part = lax.dot_general(
         piece[1], w_down, (((1,), (1,)), ((), ())), preferred_element_type=jnp.float32
     )
-    summed = lax.psum(jnp.stack([gate_part, up_part, back_part]), WA)
-    gate, up, d_hidden = summed[0], summed[1], summed[2]
+    partial = jnp.stack([gate_part, up_part, back_part])
+    half = lax.psum_scatter(partial, "core", scatter_dimension=1, tiled=True)
+    half = lax.psum(half, ("x", "y"))
+    gate, up, d_hidden = half[0], half[1], half[2]
 
     d_gate, d_up = gate_grads(gate, up, d_hidden)
-    dot_part = jnp.sum(d_gate.astype(jnp.float32) * gate + d_up.astype(jnp.float32) * up, axis=1)
+    dot_half = jnp.sum(d_gate.astype(jnp.float32) * gate + d_up.astype(jnp.float32) * up, axis=1)
+    grads = lax.all_gather(jnp.stack([d_gate, d_up]), "core", axis=1, tiled=True)
+    d_gate, d_up = grads[0], grads[1]
+    dot_part = lax.all_gather(dot_half, "core", axis=0, tiled=True)
     total = lax.dot_general(
         d_gate, w_gate, (((1,), (1,)), ((), ())), preferred_element_type=jnp.float32
     ) + lax.dot_general(

time: 290 us -> 297 us (1.024)
  starting transfers between devices: 59.8 us -> 21.6 us
  blocking collectives: 26.1 us -> 62.9 us
  waiting for transfers between devices: 165 us -> 176 us
    all_gather x0 -> x1, blocking collectives: none -> 31.2 us  [local(): lax.all_gather(jnp.stack([residual_in, grad_out]), 'ha', axis=1, tiled=True)]
    ppermute x4 -> x0, starting transfers between devices: 28.8 us -> none  [gather_rows(): got = lax.ppermute(held, axis, _partner(axis, bit))]
    reduce_scatter x0 -> x1, waiting for transfers between devices: none -> 18 us  [local(): half = lax.psum_scatter(partial, 'core', scatter_dimension=1, tiled=True)]
    psum x1, waiting for transfers between devices: 141 us -> 124 us  [local(): half = lax.psum(half, ('x', 'y'))]
    all_gather x0 -> x1, waiting for transfers between devices: none -> 13.6 us  [local(): lax.all_gather(jnp.stack([d_gate, d_up]), 'core', axis=1, tiled=True)]
    ppermute x4 -> x0, waiting for transfers between devices: 12.5 us -> none  [gather_rows(): got = lax.ppermute(held, axis, _partner(axis, bit))]
    ppermute x4, waiting for transfers between devices: 11.4 us -> 21.1 us  [scatter_sum(): x = keep + lax.ppermute(send, axis, _partner(axis, bit))]
    ppermute x4, starting transfers between devices: 31 us -> 21.5 us  [scatter_sum(): x = keep + lax.ppermute(send, axis, _partner(axis, bit))]
  transfers between devices with their start and end apart: 9 -> 7, of which waited for: 9 -> 7; matrix products, arithmetic and copies ran while one was open for 0% -> 1% of each run, Pallas kernels for 0% -> 0%
where the time goes in v4:
time: 297 us; the launch traced here: 296 us
  waiting for transfers between devices  176 us (59%)
  blocking collectives  62.9 us (21%)
  starting transfers between devices  21.6 us (7%)
  between operations  14.1 us (5%)
  other arithmetic  10.1 us (3%)
  matrix products  6.27 us (2%)
  local copies, waits for them, and re-layouts  5.16 us (2%)
    psum x1, waiting for transfers between devices, local(): half = lax.psum(half, ('x', 'y'))  124 us
    all_gather x1, blocking collectives, local(): lax.all_gather(jnp.stack([residual_in, grad_out]), 'ha', axis=1, tiled=True)  31.2 us
    psum x3, blocking collectives, local(): squares = lax.psum(lax.psum(lax.psum(squares, 'core'), 'y'), 'x')  27.4 us
    ppermute x4, starting transfers between devices, scatter_sum(): x = keep + lax.ppermute(send, axis, _partner(axis, bit))  21.5 us
    ppermute x4, waiting for transfers between devices, scatter_sum(): x = keep + lax.ppermute(send, axis, _partner(axis, bit))  21.1 us
    reduce_scatter x1, waiting for transfers between devices, local(): half = lax.psum_scatter(partial, 'core', scatter_dimension=1, tiled=True)  18 us
    all_gather x1, waiting for transfers between devices, local(): lax.all_gather(jnp.stack([d_gate, d_up]), 'core', axis=1, tiled=True)  13.6 us
  transfers between devices with their start and end apart: 7, of which 7 were waited for; matrix products, arithmetic and copies ran while one was open for 1% of the time, Pallas kernels for 0%

profile of v4, /device:TPU:1, one launch (start us, length us, event | category | flops | bytes accessed | tf_op | source)
XLA Modules:
  0.0 296.4 jit_solution(17267899748325876350)
XLA Ops:
  6.5 0.9 pad_maximum_fusion.2
  7.5 31.2 %all_gather.9 = bf16[2,192,512]{2,0,1:T(2,128)(2,1)S(1)} all-gather(bf16[2,12,512]{2,0,1:T(2,128)(2,1)S(1)} %copy.11), channel_id=1, replica_groups=mesh['x'=4,'y'=4,'core'=2,'ha'=16] {'ha'}, dimensions={1}, use_global_device_ids=true | all-gather | bytes 417792 | tf_op jit(solution)/shard_map/all_gather | solution.py:53
  38.7 1.3 slice_convert_fusion
  40.0 0.8 copy-done.2
  40.7 0.1 fusion.12
  40.8 10.2 %psum.28 = f32[192]{0:T(256)S(1)} all-reduce(f32[192]{0:T(256)S(1)} %fusion.12), channel_id=1, replica_groups=mesh['x'=4,'y'=4,'core'=2,'ha'=16] {'core'}, use_global_device_ids=true, to_apply=%region_1.0 | all-reduce | flops 192 | bytes 1536 | tf_op jit(solution)/shard_map/psum | solution.py:56
  51.1 8.7 %psum.29 = f32[192]{0:T(256)S(1)} all-reduce(f32[192]{0:T(256)S(1)} %psum.28), channel_id=1, replica_groups=mesh['x'=4,'y'=4,'core'=2,'ha'=16] {'y'}, use_global_device_ids=true, to_apply=%region_2.0 | all-reduce | flops 192 | bytes 1536 | tf_op jit(solution)/shard_map/psum | solution.py:56
  59.8 8.5 %psum.30 = f32[192]{0:T(256)S(1)} all-reduce(f32[192]{0:T(256)S(1)} %psum.29), channel_id=1, replica_groups=mesh['x'=4,'y'=4,'core'=2,'ha'=16] {'x'}, use_global_device_ids=true, to_apply=%region_3.0 | all-reduce | flops 192 | bytes 1536 | tf_op jit(solution)/shard_map/psum | solution.py:56
  68.3 1.6 convolution_bitcast_fusion.1
  69.9 0.6 convolution_bitcast_fusion.2
  70.5 0.8 copy-done.4
  71.4 0.1 copy-done.6
  71.4 0.7 convolution_bitcast_fusion
  72.1 2.1 pad_maximum_fusion
  74.2 0.0 reduce-scatter.2.cloned.1.call-update
  74.3 0.0 all-reduce.4.cloned.1.call-start
  74.3 18.0 %reduce-scatter.2.cloned.1.call-done = f32[3,96,1664]{2,1,0:T(8,128)} async-done(((f32[3,192,1664]{2,1,0:T(8,128)}), f32[3,96,1664]{2,1,0:T(8,128)}) %reduce-scatter.2.cloned.1.call-update) | async-done | bytes 1916944 | tf_op jit(solution)/shard_map/reduce_scatter | solution.py:66
  92.3 0.0 all-gather.2.cloned.1.call-start
  92.3 123.7 %all-reduce.4.cloned.1.call-done = f32[3,96,1664]{2,1,0:T(8,128)} async-done(((f32[3,96,1664]{2,1,0:T(8,128)}), f32[3,96,1664]{2,1,0:T(8,128)}) %all-reduce.4.cloned.1.call-update) | async-done | bytes 1916944 | tf_op jit(solution)/shard_map/psum | solution.py:67
  216.0 1.7 multiply_convert_fusion.1
  217.7 0.9 pad_maximum_fusion.1
  218.6 0.0 all-gather.2.cloned.1.call-update
  218.7 1.3 dynamic-slice.6
  220.6 1.9 fusion.8
  222.5 0.2 dynamic-update-slice
  222.8 4.3 %all-reduce.1 = f32[192]{0:T(256)S(1)} all-reduce(f32[192]{0:T(256)S(1)} %dynamic-update-slice), channel_id=1, replica_groups=mesh['x'=4,'y'=4,'core'=2,'ha'=16] {'core'}, use_global_device_ids=true, to_apply=%add.1 | all-reduce | flops 192 | bytes 1536
  227.1 0.1 reshape.32
  227.3 13.6 %all-gather.2.cloned.1.call-done = bf16[2,192,1664]{2,1,0:T(8,128)(2,1)} async-done(((bf16[2,96,1664]{2,1,0:T(8,128)(2,1)}), bf16[2,192,1664]{2,1,0:T(8,128)(2,1)}) %all-gather.2.cloned.1.call-update) | async-done | bytes 1277968 | tf_op jit(solution)/shard_map/all_gather | solution.py:72
  240.8 1.9 fusion
  242.7 1.5 convolution_add_fusion
  244.2 1.0 concatenate.8
  245.2 0.1 fusion.16
  245.3 0.1 copy.37
  245.5 2.2 collective-permute-start
  247.7 6.3 %collective-permute-done = f32[8,13,512]{2,0,1:T(8,128)S(1)} collective-permute-done((f32[8,13,512]{2,0,1:T(8,128)S(1)}, f32[8,13,512]{2,0,1:T(8,128)S(1)}, u32[]{:S(2)}, u32[]{:S(2)}) %collective-permute-start) | collective-permute-done | bytes 213024 | tf_op jit(solution)/shard_map/ppermute | solution.py:45
  254.0 0.1 bitcast_add_fusion
  254.1 0.1 reshape.33
  254.2 0.2 constant_dynamic-slice_fusion.4
  254.5 3.2 %collective-permute-start.1 = (f32[4,13,512]{2,0,1:T(4,128)S(1)}, f32[4,13,512]{2,0,1:T(4,128)S(1)}, u32[]{:S(2)}, u32[]{:S(2)}) collective-permute-start(f32[4,13,512]{2,0,1:T(4,128)S(1)} %bitcast.124), channel_id=1, source_target_pairs={{0,2},{1,3},{2,0},{3,1},{4,6},{5,7},{6,4},{7,5},{8,10},{9,11},{10,... | collective-permute-start | bytes 319496 | tf_op jit(solution)/shard_map/ppermute | solution.py:45
  257.7 6.5 %collective-permute-done.1 = f32[4,13,512]{2,0,1:T(4,128)S(1)} collective-permute-done((f32[4,13,512]{2,0,1:T(4,128)S(1)}, f32[4,13,512]{2,0,1:T(4,128)S(1)}, u32[]{:S(2)}, u32[]{:S(2)}) %collective-permute-start.1) | collective-permute-done | bytes 106528 | tf_op jit(solution)/shard_map/ppermute | solution.py:45
  264.2 0.1 reshape.34
  264.3 0.1 constant_dynamic-slice_fusion.2
  264.4 4.5 %collective-permute-start.2 = (f32[2,13,512]{2,0,1:T(2,128)S(1)}, f32[2,13,512]{2,0,1:T(2,128)S(1)}, u32[]{:S(2)}, u32[]{:S(2)}) collective-permute-start(f32[2,13,512]{2,0,1:T(2,128)S(1)} %bitcast.127), channel_id=1, source_target_pairs={{0,4},{1,5},{2,6},{3,7},{4,0},{5,1},{6,2},{7,3},{8,12},{9,13},{10,... | collective-permute-start | bytes 159752 | tf_op jit(solution)/shard_map/ppermute | solution.py:45
  269.0 6.7 %collective-permute-done.2 = f32[2,13,512]{2,0,1:T(2,128)S(1)} collective-permute-done((f32[2,13,512]{2,0,1:T(2,128)S(1)}, f32[2,13,512]{2,0,1:T(2,128)S(1)}, u32[]{:S(2)}, u32[]{:S(2)}) %collective-permute-start.2) | collective-permute-done | bytes 53280 | tf_op jit(solution)/shard_map/ppermute | solution.py:45
  275.8 11.6 %collective-permute-start.3 = (f32[1,13,512]{2,0,1:T(1,128)S(1)}, f32[1,13,512]{2,0,1:T(1,128)S(1)}, u32[]{:S(2)}, u32[]{:S(2)}) collective-permute-start(f32[1,13,512]{2,0,1:T(1,128)S(1)} %constant_dynamic-slice_fusion), channel_id=1, source_target_pairs={{0,8},{1,9},{2,10},{3,11},{4,12},{5,13},{6,14},{7,15},{8,0},{9,1},... | collective-permute-start | bytes 79880 | tf_op jit(solution)/shard_map/ppermute | solution.py:45
  287.5 0.1 multiply_multiply_fusion
  287.5 1.6 collective-permute-done.3
  289.2 0.7 fusion.20
  (34 shorter events, 0.4 us)
Async XLA Ops:
  6.5 63.3 %copy-start = (bf16[512,1664]{1,0:T(8,128)(2,1)S(1)}, bf16[512,1664]{1,0:T(8,128)(2,1)}, u32[]{:S(2)}) copy-start(bf16[512,1664]{1,0:T(8,128)(2,1)} %param.9) | copy-start | bytes 5111812
  6.5 61.7 %copy-start.9 = (bf16[512]{0:T(512)(128)(2,1)S(1)}, bf16[512]{0:T(512)(128)(2,1)}, u32[]{:S(2)}) copy-start(bf16[512]{0:T(512)(128)(2,1)} %param.8) | copy-start | bytes 3076
  6.5 61.7 %copy-start.1 = (bf16[512,1664]{1,0:T(8,128)(2,1)S(1)}, bf16[512,1664]{1,0:T(8,128)(2,1)}, u32[]{:S(2)}) copy-start(bf16[512,1664]{1,0:T(8,128)(2,1)} %param.10) | copy-start | bytes 5111812
  6.5 85.7 %reduce-scatter.2.cloned.1.call-start = ((), (), s32[]{:S(2)}) async-start(), calls=%async_computation.1 | async-start | bytes 5750784 | tf_op jit(solution)/shard_map/reduce_scatter | solution.py:66
  40.0 0.8 copy-start.2
  68.2 1.7 copy-start.3
  69.9 1.5 copy-start.4
  69.9 1.5 copy-start.6
  74.3 141.7 %all-reduce.4.cloned.1.call-start = ((), (), s32[]{:S(2)}) async-start(), calls=%async_computation.2 | async-start | bytes 3833856 | tf_op jit(solution)/shard_map/psum | solution.py:67
  92.3 148.5 %all-gather.2.cloned.1.call-start = ((), (), s32[]{:S(2)}) async-start(), calls=%async_computation.3 | async-start | bytes 1916928 | tf_op jit(solution)/shard_map/all_gather | solution.py:72
  240.8 1.9 copy-start.5
  245.3 43.9 %copy-start.7 = (bf16[12,512]{1,0:T(8,128)(2,1)S(1)}, bf16[12,512]{1,0:T(8,128)(2,1)}, u32[]{:S(2)}) copy-start(bf16[12,512]{1,0:T(8,128)(2,1)} %param.7) | copy-start | bytes 36868
  245.3 43.9 %copy-start.8 = (bf16[12,512]{1,0:T(8,128)(2,1)S(1)}, bf16[12,512]{1,0:T(8,128)(2,1)}, u32[]{:S(2)}) copy-start(bf16[12,512]{1,0:T(8,128)(2,1)} %param.6) | copy-start | bytes 36868
  245.5 8.5 %collective-permute-start = (f32[8,13,512]{2,0,1:T(8,128)S(1)}, f32[8,13,512]{2,0,1:T(8,128)S(1)}, u32[]{:S(2)}, u32[]{:S(2)}) collective-permute-start(f32[8,13,512]{2,0,1:T(8,128)S(1)} %bitcast.123), channel_id=1, source_target_pairs={{0,1},{1,0},{2,3},{3,2},{4,5},{5,4},{6,7},{7,6},{8,9},{9,8},{10,11... | collective-permute-start | bytes 638984 | tf_op jit(solution)/shard_map/ppermute | solution.py:45
  254.5 9.7 %collective-permute-start.1 = (f32[4,13,512]{2,0,1:T(4,128)S(1)}, f32[4,13,512]{2,0,1:T(4,128)S(1)}, u32[]{:S(2)}, u32[]{:S(2)}) collective-permute-start(f32[4,13,512]{2,0,1:T(4,128)S(1)} %bitcast.124), channel_id=1, source_target_pairs={{0,2},{1,3},{2,0},{3,1},{4,6},{5,7},{6,4},{7,5},{8,10},{9,11},{10,... | collective-permute-start | bytes 319496 | tf_op jit(solution)/shard_map/ppermute | solution.py:45
  264.4 11.3 %collective-permute-start.2 = (f32[2,13,512]{2,0,1:T(2,128)S(1)}, f32[2,13,512]{2,0,1:T(2,128)S(1)}, u32[]{:S(2)}, u32[]{:S(2)}) collective-permute-start(f32[2,13,512]{2,0,1:T(2,128)S(1)} %bitcast.127), channel_id=1, source_target_pairs={{0,4},{1,5},{2,6},{3,7},{4,0},{5,1},{6,2},{7,3},{8,12},{9,13},{10,... | collective-permute-start | bytes 159752 | tf_op jit(solution)/shard_map/ppermute | solution.py:45
  275.8 13.3 %collective-permute-start.3 = (f32[1,13,512]{2,0,1:T(1,128)S(1)}, f32[1,13,512]{2,0,1:T(1,128)S(1)}, u32[]{:S(2)}, u32[]{:S(2)}) collective-permute-start(f32[1,13,512]{2,0,1:T(1,128)S(1)} %constant_dynamic-slice_fusion), channel_id=1, source_target_pairs={{0,8},{1,9},{2,10},{3,11},{4,12},{5,13},{6,14},{7,15},{8,0},{9,1},... | collective-permute-start | bytes 79880 | tf_op jit(solution)/shard_map/ppermute | solution.py:45
Sparse Core Ops, SparseCore 0:
  74.4 17.8 reduce-scatter.1
  95.7 120.2 all-reduce.3
  218.8 21.9 all-gather.1

commit v5 on v2

--- a/solution.py
+++ b/solution.py
@@ -13,6 +13,19 @@
     d_up = (d_hidden * gate * sig).astype(jnp.bfloat16)
     d_gate = (d_hidden * up * sig * (1.0 + gate * (1.0 - sig))).astype(jnp.bfloat16)
     return d_gate, d_up
+
+
+def scatter_sum(x, axis):
+    n = lax.axis_size(axis)
+    for shift in range(0, n.bit_length() - 1, 2):
+        groups = x.reshape(-1, 4, *x.shape[1:])
+        mine = (lax.axis_index(axis) >> shift) & 3
+        total = lax.dynamic_index_in_dim(groups, mine, axis=1, keepdims=False)
+        for k in (1, 2, 3):
+            send = lax.dynamic_index_in_dim(groups, mine ^ k, axis=1, keepdims=False)
+            total = total + lax.ppermute(send, axis, [(i, i ^ (k << shift)) for i in range(n)])
+        x = total
+    return x[0]
 
 
 def local(residual_in, grad_out, norm_gain, w_gate, w_up, w_down):
@@ -44,7 +57,7 @@
     n_ha, width = lax.axis_size("ha"), total.shape[1]
     dot_rows = jnp.pad(dot_part.reshape(n_ha, 1, rows), ((0, 0), (0, 0), (0, width - rows)))
     packed = jnp.concatenate([total.reshape(n_ha, rows, width), dot_rows], axis=1)
-    mine = lax.psum_scatter(packed.reshape(-1, width), "ha", scatter_dimension=0, tiled=True)
+    mine = scatter_sum(packed, "ha")
     d_normed = mine[:rows]
 
     start = lax.axis_index("ha") * rows

time: 364 us -> 267 us (0.73)
  the two profiles are of different devices: /device:TPU:2 before, /device:TPU:1 now
where the time goes in v5:
time: 267 us; the launch traced here: 264 us
  waiting for transfers between devices  149 us (56%)
  blocking collectives  58.6 us (22%)
  starting transfers between devices  26.6 us (10%)
  between operations  13.7 us (5%)
  other arithmetic  8.24 us (3%)
  matrix products  5.11 us (2%)
  local copies, waits for them, and re-layouts  2.9 us (1%)
    psum x1, waiting for transfers between devices, local(): summed = lax.psum(jnp.stack([gate_part, up_part, back_part]), WA)  137 us
    all_gather x1, blocking collectives, local(): lax.all_gather(jnp.stack([residual_in, grad_out]), 'ha', axis=1, tiled=True)  31.2 us
    psum x3, blocking collectives, local(): squares = lax.psum(lax.psum(lax.psum(squares, 'core'), 'y'), 'x')  27.4 us
    ppermute x6, starting transfers between devices, scatter_sum(): lax.ppermute(send, axis, [(i, i ^ k << shift) for i in range(n)])  26.6 us
    ppermute x6, waiting for transfers between devices, scatter_sum(): lax.ppermute(send, axis, [(i, i ^ k << shift) for i in range(n)])  12.6 us
  transfers between devices with their start and end apart: 7, of which 5 were waited for; matrix products, arithmetic and copies ran while one was open for 0% of the time, Pallas kernels for 0%

profile of v5, /device:TPU:1, one launch (start us, length us, event | category | flops | bytes accessed | tf_op | source)
XLA Modules:
  0.0 264.4 jit_solution(15511601264904462946)
XLA Ops:
  6.5 0.0 copy-start
  6.5 0.0 all-reduce.3.cloned.1.call-start
  6.5 0.9 pad_maximum_fusion.1
  7.5 31.2 %all_gather.3 = bf16[2,192,512]{2,0,1:T(2,128)(2,1)S(1)} all-gather(bf16[2,12,512]{2,0,1:T(2,128)(2,1)S(1)} %copy.7), channel_id=1, replica_groups=mesh['x'=4,'y'=4,'core'=2,'ha'=16] {'ha'}, dimensions={1}, use_global_device_ids=true | all-gather | bytes 417792 | tf_op jit(solution)/shard_map/all_gather | solution.py:35
  38.7 1.3 slice_convert_fusion
  40.0 0.8 copy-done.2
  40.7 0.1 fusion
  40.8 10.2 %psum.28 = f32[192]{0:T(256)S(1)} all-reduce(f32[192]{0:T(256)S(1)} %fusion), channel_id=1, replica_groups=mesh['x'=4,'y'=4,'core'=2,'ha'=16] {'core'}, use_global_device_ids=true, to_apply=%region_1.0 | all-reduce | flops 192 | bytes 1536 | tf_op jit(solution)/shard_map/psum | solution.py:38
  51.1 8.7 %psum.29 = f32[192]{0:T(256)S(1)} all-reduce(f32[192]{0:T(256)S(1)} %psum.28), channel_id=1, replica_groups=mesh['x'=4,'y'=4,'core'=2,'ha'=16] {'y'}, use_global_device_ids=true, to_apply=%region_2.0 | all-reduce | flops 192 | bytes 1536 | tf_op jit(solution)/shard_map/psum | solution.py:38
  59.8 8.5 %psum.30 = f32[192]{0:T(256)S(1)} all-reduce(f32[192]{0:T(256)S(1)} %psum.29), channel_id=1, replica_groups=mesh['x'=4,'y'=4,'core'=2,'ha'=16] {'x'}, use_global_device_ids=true, to_apply=%region_3.0 | all-reduce | flops 192 | bytes 1536 | tf_op jit(solution)/shard_map/psum | solution.py:38
  68.2 0.0 copy-done.8
  68.2 0.0 copy-done.1
  68.2 0.0 copy-start.3
  68.3 1.6 convolution_bitcast_fusion.1
  69.9 0.0 copy-done
  69.9 0.0 copy-done.3
  69.9 0.0 copy-start.4
  69.9 0.6 convolution_bitcast_fusion.2
  70.5 0.9 copy-done.4
  71.4 0.1 copy-done.5
  71.4 0.7 convolution_bitcast_fusion
  72.2 2.1 pad_maximum_fusion
  74.3 0.0 all-reduce.3.cloned.1.call-update
  74.3 136.6 %all-reduce.3.cloned.1.call-done = f32[3,192,1664]{2,1,0:T(8,128)} async-done(((f32[3,192,1664]{2,1,0:T(8,128)}), f32[3,192,1664]{2,1,0:T(8,128)}) %all-reduce.3.cloned.1.call-update) | async-done | bytes 3833872 | tf_op jit(solution)/shard_map/psum | solution.py:47
  211.0 2.9 %add_reduce_fusion = (f32[192]{0:T(256)S(1)}, bf16[192,1664]{1,0:T(8,128)(2,1)S(1)}, bf16[192,1664]{1,0:T(8,128)(2,1)S(1)}) fusion(f32[3,192,1664]{2,1,0:T(8,128)} %all-reduce.3.cloned.1.call-done), kind=kLoop, calls=%fused_computation.7 | loop fusion | flops 6070080 | bytes 5112576 | tf_op jit(solution)/shard_map/reduce_sum | solution.py:51
  213.9 0.7 fusion.22
  214.6 1.5 convolution_add_fusion
  216.1 1.0 concatenate.8
  217.1 0.1 reshape.30
  217.2 0.0 copy-start.6
  217.2 0.0 copy-start.7
  217.3 0.1 fusion.11
  217.3 3.2 %collective-permute-start = (f32[4,13,512]{2,1,0:T(8,128)S(1)}, f32[4,13,512]{2,1,0:T(8,128)S(1)}, u32[]{:S(2)}, u32[]{:S(2)}) collective-permute-start(f32[4,13,512]{2,1,0:T(8,128)S(1)} %get-tuple-element.10), channel_id=1, source_target_pairs={{0,1},{1,0},{2,3},{3,2},{4,5},{5,4},{6,7},{7,6},{8,9},{9,8},{10,11... | collective-permute-start | bytes 319496 | tf_op jit(solution)/shard_map/ppermute | solution.py:26
  220.5 4.2 %collective-permute-start.1 = (f32[4,13,512]{2,1,0:T(8,128)S(1)}, f32[4,13,512]{2,1,0:T(8,128)S(1)}, u32[]{:S(2)}, u32[]{:S(2)}) collective-permute-start(f32[4,13,512]{2,1,0:T(8,128)S(1)} %get-tuple-element.11), channel_id=1, source_target_pairs={{0,2},{1,3},{2,0},{3,1},{4,6},{5,7},{6,4},{7,5},{8,10},{9,11},{10,... | collective-permute-start | bytes 319496 | tf_op jit(solution)/shard_map/ppermute | solution.py:26
  224.7 1.9 collective-permute-start.2
  226.7 0.0 collective-permute-done
  226.7 4.3 %collective-permute-done.1 = f32[4,13,512]{2,1,0:T(8,128)S(1)} collective-permute-done((f32[4,13,512]{2,1,0:T(8,128)S(1)}, f32[4,13,512]{2,1,0:T(8,128)S(1)}, u32[]{:S(2)}, u32[]{:S(2)}) %collective-permute-start.1) | collective-permute-done | bytes 106528 | tf_op jit(solution)/shard_map/ppermute | solution.py:26
  231.0 1.3 collective-permute-done.2
  232.4 7.4 %collective-permute-start.3 = (f32[1,13,512]{2,1,0:T(8,128)S(1)}, f32[1,13,512]{2,1,0:T(8,128)S(1)}, u32[]{:S(2)}, u32[]{:S(2)}) collective-permute-start(f32[1,13,512]{2,1,0:T(8,128)S(1)} %get-tuple-element.15), channel_id=1, source_target_pairs={{0,4},{1,5},{2,6},{3,7},{4,0},{5,1},{6,2},{7,3},{8,12},{9,13},{10,... | collective-permute-start | bytes 79880 | tf_op jit(solution)/shard_map/ppermute | solution.py:26
  239.8 8.1 %collective-permute-start.4 = (f32[1,13,512]{2,1,0:T(8,128)S(1)}, f32[1,13,512]{2,1,0:T(8,128)S(1)}, u32[]{:S(2)}, u32[]{:S(2)}) collective-permute-start(f32[1,13,512]{2,1,0:T(8,128)S(1)} %get-tuple-element.17), channel_id=1, source_target_pairs={{0,8},{1,9},{2,10},{3,11},{4,12},{5,13},{6,14},{7,15},{8,0},{9,1},... | collective-permute-start | bytes 79880 | tf_op jit(solution)/shard_map/ppermute | solution.py:26
  247.8 1.9 collective-permute-start.5
  249.8 0.1 multiply_multiply_fusion
  249.8 0.0 collective-permute-done.3
  249.8 3.3 %collective-permute-done.4 = f32[1,13,512]{2,1,0:T(8,128)S(1)} collective-permute-done((f32[1,13,512]{2,1,0:T(8,128)S(1)}, f32[1,13,512]{2,1,0:T(8,128)S(1)}, u32[]{:S(2)}, u32[]{:S(2)}) %collective-permute-start.4) | collective-permute-done | bytes 26656 | tf_op jit(solution)/shard_map/ppermute | solution.py:26
  253.2 3.7 %collective-permute-done.5 = f32[1,13,512]{2,1,0:T(8,128)S(1)} collective-permute-done((f32[1,13,512]{2,1,0:T(8,128)S(1)}, f32[1,13,512]{2,1,0:T(8,128)S(1)}, u32[]{:S(2)}, u32[]{:S(2)}) %collective-permute-start.5) | collective-permute-done | bytes 26656 | tf_op jit(solution)/shard_map/ppermute | solution.py:26
  256.9 0.0 copy-done.6
  256.9 0.0 copy-done.7
  256.9 0.7 fusion.18
  (13 shorter events, 0.2 us)
Async XLA Ops:
  6.5 63.4 %copy-start = (bf16[512,1664]{1,0:T(8,128)(2,1)S(1)}, bf16[512,1664]{1,0:T(8,128)(2,1)}, u32[]{:S(2)}) copy-start(bf16[512,1664]{1,0:T(8,128)(2,1)} %param.9) | copy-start | bytes 5111812
  6.5 61.7 %copy-start.8 = (bf16[512]{0:T(512)(128)(2,1)S(1)}, bf16[512]{0:T(512)(128)(2,1)}, u32[]{:S(2)}) copy-start(bf16[512]{0:T(512)(128)(2,1)} %param.8) | copy-start | bytes 3076
  6.5 61.7 %copy-start.1 = (bf16[512,1664]{1,0:T(8,128)(2,1)S(1)}, bf16[512,1664]{1,0:T(8,128)(2,1)}, u32[]{:S(2)}) copy-start(bf16[512,1664]{1,0:T(8,128)(2,1)} %param.10) | copy-start | bytes 5111812
  6.5 204.4 %all-reduce.3.cloned.1.call-start = ((), (), s32[]{:S(2)}) async-start(), calls=%async_computation | async-start | bytes 7667712 | tf_op jit(solution)/shard_map/psum | solution.py:47
  40.0 0.8 copy-start.2
  68.2 1.7 copy-start.3
  69.9 1.5 copy-start.4
  69.9 1.5 copy-start.5
  217.2 39.7 %copy-start.6 = (bf16[12,512]{1,0:T(8,128)(2,1)S(1)}, bf16[12,512]{1,0:T(8,128)(2,1)}, u32[]{:S(2)}) copy-start(bf16[12,512]{1,0:T(8,128)(2,1)} %param.7) | copy-start | bytes 36868
  217.2 39.7 %copy-start.7 = (bf16[12,512]{1,0:T(8,128)(2,1)S(1)}, bf16[12,512]{1,0:T(8,128)(2,1)}, u32[]{:S(2)}) copy-start(bf16[12,512]{1,0:T(8,128)(2,1)} %param.6) | copy-start | bytes 36868
  217.3 9.3 %collective-permute-start = (f32[4,13,512]{2,1,0:T(8,128)S(1)}, f32[4,13,512]{2,1,0:T(8,128)S(1)}, u32[]{:S(2)}, u32[]{:S(2)}) collective-permute-start(f32[4,13,512]{2,1,0:T(8,128)S(1)} %get-tuple-element.10), channel_id=1, source_target_pairs={{0,1},{1,0},{2,3},{3,2},{4,5},{5,4},{6,7},{7,6},{8,9},{9,8},{10,11... | collective-permute-start | bytes 319496 | tf_op jit(solution)/shard_map/ppermute | solution.py:26
  220.5 10.5 %collective-permute-start.1 = (f32[4,13,512]{2,1,0:T(8,128)S(1)}, f32[4,13,512]{2,1,0:T(8,128)S(1)}, u32[]{:S(2)}, u32[]{:S(2)}) collective-permute-start(f32[4,13,512]{2,1,0:T(8,128)S(1)} %get-tuple-element.11), channel_id=1, source_target_pairs={{0,2},{1,3},{2,0},{3,1},{4,6},{5,7},{6,4},{7,5},{8,10},{9,11},{10,... | collective-permute-start | bytes 319496 | tf_op jit(solution)/shard_map/ppermute | solution.py:26
  224.7 7.6 %collective-permute-start.2 = (f32[4,13,512]{2,1,0:T(8,128)S(1)}, f32[4,13,512]{2,1,0:T(8,128)S(1)}, u32[]{:S(2)}, u32[]{:S(2)}) collective-permute-start(f32[4,13,512]{2,1,0:T(8,128)S(1)} %get-tuple-element.12), channel_id=1, source_target_pairs={{0,3},{1,2},{2,1},{3,0},{4,7},{5,6},{6,5},{7,4},{8,11},{9,10},{10,... | collective-permute-start | bytes 319496 | tf_op jit(solution)/shard_map/ppermute | solution.py:26
  232.4 17.5 %collective-permute-start.3 = (f32[1,13,512]{2,1,0:T(8,128)S(1)}, f32[1,13,512]{2,1,0:T(8,128)S(1)}, u32[]{:S(2)}, u32[]{:S(2)}) collective-permute-start(f32[1,13,512]{2,1,0:T(8,128)S(1)} %get-tuple-element.15), channel_id=1, source_target_pairs={{0,4},{1,5},{2,6},{3,7},{4,0},{5,1},{6,2},{7,3},{8,12},{9,13},{10,... | collective-permute-start | bytes 79880 | tf_op jit(solution)/shard_map/ppermute | solution.py:26
  239.8 13.4 %collective-permute-start.4 = (f32[1,13,512]{2,1,0:T(8,128)S(1)}, f32[1,13,512]{2,1,0:T(8,128)S(1)}, u32[]{:S(2)}, u32[]{:S(2)}) collective-permute-start(f32[1,13,512]{2,1,0:T(8,128)S(1)} %get-tuple-element.17), channel_id=1, source_target_pairs={{0,8},{1,9},{2,10},{3,11},{4,12},{5,13},{6,14},{7,15},{8,0},{9,1},... | collective-permute-start | bytes 79880 | tf_op jit(solution)/shard_map/ppermute | solution.py:26
  247.8 9.0 %collective-permute-start.5 = (f32[1,13,512]{2,1,0:T(8,128)S(1)}, f32[1,13,512]{2,1,0:T(8,128)S(1)}, u32[]{:S(2)}, u32[]{:S(2)}) collective-permute-start(f32[1,13,512]{2,1,0:T(8,128)S(1)} %get-tuple-element.16), channel_id=1, source_target_pairs={{0,12},{1,13},{2,14},{3,15},{4,8},{5,9},{6,10},{7,11},{8,4},{9,5},... | collective-permute-start | bytes 79880 | tf_op jit(solution)/shard_map/ppermute | solution.py:26
Sparse Core Ops, SparseCore 0:
  74.4 136.4 all-reduce.2

commit v6 on v5

--- a/solution.py
+++ b/solution.py
@@ -28,6 +28,38 @@
     return x[0]
 
 
+def _exchange(axis, k):
+    return [(i, i ^ k) for i in range(lax.axis_size(axis))]
+
+
+def scatter_blocks(x, axes):
+    for axis in axes:
+        g = lax.axis_size(axis)
+        groups = x.reshape(x.shape[0], -1, g, *x.shape[2:])
+        mine = lax.axis_index(axis)
+        total = lax.dynamic_index_in_dim(groups, mine, axis=2, keepdims=False)
+        for k in range(1, g):
+            send = lax.dynamic_index_in_dim(groups, mine ^ k, axis=2, keepdims=False)
+            total = total + lax.ppermute(send, axis, _exchange(axis, k))
+        x = total
+    return x
+
+
+def gather_blocks(x, axes):
+    for axis in reversed(axes):
+        g = lax.axis_size(axis)
+        mine = lax.axis_index(axis)
+        held = [x] + [lax.ppermute(x, axis, _exchange(axis, k)) for k in range(1, g)]
+        placed = []
+        for d in range(g):
+            pick = held[g - 1]
+            for k in reversed(range(g - 1)):
+                pick = jnp.where((mine ^ d) == k, held[k], pick)
+            placed.append(pick)
+        x = jnp.stack(placed, axis=2).reshape(x.shape[0], -1, *x.shape[2:])
+    return x
+
+
 def local(residual_in, grad_out, norm_gain, w_gate, w_up, w_down):
     rows = residual_in.shape[0]
     gain_f = norm_gain.astype(jnp.float32)
@@ -44,11 +76,19 @@
     back_part = lax.dot_general(
         piece[1], w_down, (((1,), (1,)), ((), ())), preferred_element_type=jnp.float32
     )
-    summed = lax.psum(jnp.stack([gate_part, up_part, back_part]), WA)
-    gate, up, d_hidden = summed[0], summed[1], summed[2]
-
+    n_wa, width = lax.axis_size(WA), gate_part.shape[1]
+    partial = jnp.stack([gate_part, up_part, back_part]).reshape(3, n_wa, -1, width)
+    part = scatter_blocks(partial, WA[::-1])[:, 0]
+    gate, up, d_hidden = part[0], part[1], part[2]
     d_gate, d_up = gate_grads(gate, up, d_hidden)
-    dot_part = jnp.sum(d_gate.astype(jnp.float32) * gate + d_up.astype(jnp.float32) * up, axis=1)
+    dot_rows = jnp.sum(d_gate.astype(jnp.float32) * gate + d_up.astype(jnp.float32) * up, axis=1)
+    dot_hi = dot_rows.astype(jnp.bfloat16)
+    dot_lo = (dot_rows - dot_hi.astype(jnp.float32)).astype(jnp.bfloat16)
+    extra = jnp.zeros_like(d_gate).at[:, 0].set(dot_hi).at[:, 1].set(dot_lo)
+    grads = gather_blocks(jnp.stack([d_gate, d_up, extra])[:, None], WA[::-1])
+    grads = grads.reshape(3, -1, width)
+    d_gate, d_up = grads[0], grads[1]
+    dot_part = grads[2][:, 0].astype(jnp.float32) + grads[2][:, 1].astype(jnp.float32)
     total = lax.dot_general(
         d_gate, w_gate, (((1,), (1,)), ((), ())), preferred_element_type=jnp.float32
     ) + lax.dot_general(

time: 267 us -> 267 us (level)
  waiting for transfers between devices: 149 us -> 55.3 us
  starting transfers between devices: 26.6 us -> 75.8 us
  local copies, waits for them, and re-layouts: 2.9 us -> 35.8 us
  other arithmetic: 8.24 us -> 25.9 us
  between operations: 13.7 us -> 0.7 us
  matrix products: 5.11 us -> 10.9 us
    psum x1 -> x0, waiting for transfers between devices: 137 us -> none  [local(): summed = lax.psum(jnp.stack([gate_part, up_part, back_part]), WA)]
    ppermute x0 -> x14, starting transfers between devices: none -> 50.3 us  [the longest x7 25.4 us: scatter_blocks(): total = total + lax.ppermute(send, axis, _exchange(axis, k))]
    ppermute x0 -> x14, waiting for transfers between devices: none -> 44.6 us  [the longest x7 26.4 us: scatter_blocks(): total = total + lax.ppermute(send, axis, _exchange(axis, k))]
    another operation x1 -> x12, other arithmetic: 2.13 us -> 11.2 us  [the longest x7 8.17 us: gather_blocks(): x = jnp.stack(placed, axis=2).reshape(x.shape[0], -1, *x.shape[2:])]
    squeeze x0 -> x6, local copies, waits for them, and re-layouts: none -> 7.87 us  [the longest x2 4.2 us: local(): d_gate, d_up = (grads[0], grads[1])]
    add x0 -> x4, other arithmetic: none -> 7.77 us  [the longest x3 6.73 us: scatter_blocks(): total = total + lax.ppermute(send, axis, _exchange(axis, k))]
    dynamic_slice x0 -> x1, local copies, waits for them, and re-layouts: none -> 6.32 us  [scatter_blocks(): total = lax.dynamic_index_in_dim(groups, mine, axis=2, keepdims=False)]
    reshape x1 -> x2, local copies, waits for them, and re-layouts: 0.08 us -> 5.27 us  [the longest x1 2.84 us: scatter_blocks(): groups = x.reshape(x.shape[0], -1, g, *x.shape[2:])]
  transfers between devices with their start and end apart: 7 -> 20, of which waited for: 5 -> 12; matrix products, arithmetic and copies ran while one was open for 0% -> 1% of each run, Pallas kernels for 0% -> 0%
where the time goes in v6:
time: 267 us; the launch traced here: 263 us
  starting transfers between devices  75.8 us (28%)
  blocking collectives  58.6 us (22%)
  waiting for transfers between devices  55.3 us (21%)
  local copies, waits for them, and re-layouts  35.8 us (13%)
  other arithmetic  25.9 us (10%)
  matrix products  10.9 us (4%)
    all_gather x1, blocking collectives, local(): lax.all_gather(jnp.stack([residual_in, grad_out]), 'ha', axis=1, tiled=True)  31.2 us
    psum x3, blocking collectives, local(): squares = lax.psum(lax.psum(lax.psum(squares, 'core'), 'y'), 'x')  27.3 us
    ppermute x7, waiting for transfers between devices, scatter_blocks(): total = total + lax.ppermute(send, axis, _exchange(axis, k))  26.4 us
    ppermute x6, starting transfers between devices, scatter_sum(): lax.ppermute(send, axis, [(i, i ^ k << shift) for i in range(n)])  25.5 us
    ppermute x7, starting transfers between devices, scatter_blocks(): total = total + lax.ppermute(send, axis, _exchange(axis, k))  25.4 us
    ppermute x7, starting transfers between devices, gather_blocks(): lax.ppermute(x, axis, _exchange(axis, k))  24.9 us
    ppermute x7, waiting for transfers between devices, gather_blocks(): lax.ppermute(x, axis, _exchange(axis, k))  18.2 us
    ppermute x6, waiting for transfers between devices, scatter_sum(): lax.ppermute(send, axis, [(i, i ^ k << shift) for i in range(n)])  10.6 us
  transfers between devices with their start and end apart: 20, of which 12 were waited for; matrix products, arithmetic and copies ran while one was open for 1% of the time, Pallas kernels for 0%

profile of v6, /device:TPU:1, one launch (start us, length us, event | category | flops | bytes accessed | tf_op | source)
XLA Modules:
  0.0 262.9 jit_solution(431258762766638906)
XLA Ops:
  0.9 31.2 %all_gather.3 = bf16[2,192,512]{2,0,1:T(2,128)(2,1)S(1)} all-gather(bf16[2,12,512]{2,0,1:T(2,128)(2,1)S(1)} %copy.79), channel_id=1, replica_groups=mesh['x'=4,'y'=4,'core'=2,'ha'=16] {'ha'}, dimensions={1}, use_global_device_ids=true | all-gather | bytes 417792 | tf_op jit(solution)/shard_map/all_gather | solution.py:67
  32.1 2.3 multiply_reduce_fusion
  34.4 1.9 slice_reduce_fusion
  36.3 10.2 %psum.21 = f32[192]{0:T(256)S(1)} all-reduce(f32[192]{0:T(256)S(1)} %get-tuple-element.29), channel_id=1, replica_groups=mesh['x'=4,'y'=4,'core'=2,'ha'=16] {'core'}, use_global_device_ids=true, to_apply=%region_1.0 | all-reduce | flops 192 | bytes 1536 | tf_op jit(solution)/shard_map/psum | solution.py:70
  46.5 8.7 %psum.22 = f32[192]{0:T(256)S(1)} all-reduce(f32[192]{0:T(256)S(1)} %psum.21), channel_id=1, replica_groups=mesh['x'=4,'y'=4,'core'=2,'ha'=16] {'y'}, use_global_device_ids=true, to_apply=%region_2.0 | all-reduce | flops 192 | bytes 1536 | tf_op jit(solution)/shard_map/psum | solution.py:70
  55.2 8.5 %psum.23 = f32[192]{0:T(256)S(1)} all-reduce(f32[192]{0:T(256)S(1)} %psum.22), channel_id=1, replica_groups=mesh['x'=4,'y'=4,'core'=2,'ha'=16] {'x'}, use_global_device_ids=true, to_apply=%region_3.0 | all-reduce | flops 192 | bytes 1536 | tf_op jit(solution)/shard_map/psum | solution.py:70
  63.8 1.9 reshape.301
  70.1 1.7 reshape.296
  71.8 2.4 convolution_bitcast_fusion
  77.1 6.3 %collective-permute-start = (f32[3,16,6,1664]{3,1,2,0:T(8,128)}, f32[3,16,6,1664]{3,1,2,0:T(8,128)}, u32[]{:S(2)}, u32[]{:S(2)}) collective-permute-start(f32[3,16,6,1664]{3,1,2,0:T(8,128)} %dynamic-slice_bitcast_fusion), channel_id=1, source_target_pairs={{0,16},{16,0},{1,17},{17,1},{2,18},{18,2},{3,19},{19,3},{4,20},{20... | collective-permute-start | bytes 5750792 | tf_op jit(solution)/shard_map/ppermute | solution.py:43
  83.4 3.8 %collective-permute-done = f32[3,16,6,1664]{3,1,2,0:T(8,128)} collective-permute-done((f32[3,16,6,1664]{3,1,2,0:T(8,128)}, f32[3,16,6,1664]{3,1,2,0:T(8,128)}, u32[]{:S(2)}, u32[]{:S(2)}) %collective-permute-start) | collective-permute-done | bytes 1916960 | tf_op jit(solution)/shard_map/ppermute | solution.py:43
  87.2 3.6 %bitcast_add_fusion = f32[3,16,6,1664]{3,1,2,0:T(8,128)} fusion(f32[3,16,6,1664]{3,1,2,0:T(8,128)} %collective-permute-done, f32[3,16,2,6,1664]{4,1,3,2,0:T(8,128)} %copy-done.1, s32[]{:T(128)S(6)} %select_n.228), kind=kLoop, calls=%fused_computation.8 | loop fusion | flops 479232 | bytes 5750788 | tf_op jit(solution)/shard_map/add | solution.py:43
  90.8 2.8 %reshape.297 = f32[3,4,4,6,1664]{4,2,1,3,0:T(4,128)} reshape(f32[3,16,6,1664]{3,1,2,0:T(8,128)} %bitcast_add_fusion) | data formatting | bytes 3833856 | tf_op jit(solution)/shard_map/reshape | solution.py:38
  93.6 6.3 %constant_dynamic-slice_fusion.9 = (f32[3,4,1,6,1664]{4,2,1,3,0:T(1,128)}, f32[3,4,1,6,1664]{4,2,1,3,0:T(1,128)S(1)}, f32[3,4,1,6,1664]{4,2,1,3,0:T(1,128)S(1)}, f32[3,4,1,6,1664]{4,2,1,3,0:T(1,128)S(1)}) fusion(f32[3,4,4,6,1664]{4,2,1,3,0:T(4,128)} %reshape.297, s32[]{:T(128)S(6)} %select_n.230, s32[]{:T(128)S(6)} %select_n.233, s32[]{:T(128)S(6)} %select_n.232, ...), kind=kLoop, calls=%fused_computation.117 | loop fusion | bytes 3833872 | tf_op jit(solution)/shard_map/jit(dynamic_index_in_dim)/dynamic_slice | solution.py:40
  100.9 1.9 collective-permute-start.1
  103.7 2.5 collective-permute-start.2
  107.1 5.1 %collective-permute-start.3 = (f32[3,4,6,1664]{3,1,2,0:T(4,128)}, f32[3,4,6,1664]{3,1,2,0:T(4,128)}, u32[]{:S(2)}, u32[]{:S(2)}) collective-permute-start(f32[3,4,6,1664]{3,1,2,0:T(4,128)} %bitcast.224), channel_id=1, source_target_pairs={{0,96},{32,64},{64,32},{96,0},{1,97},{33,65},{65,33},{97,1},{2,98}... | collective-permute-start | bytes 1437704 | tf_op jit(solution)/shard_map/ppermute | solution.py:43
  112.3 2.9 %collective-permute-done.1 = f32[3,4,6,1664]{3,1,2,0:T(4,128)} collective-permute-done((f32[3,4,6,1664]{3,1,2,0:T(4,128)}, f32[3,4,6,1664]{3,1,2,0:T(4,128)}, u32[]{:S(2)}, u32[]{:S(2)}) %collective-permute-start.1) | collective-permute-done | bytes 479264 | tf_op jit(solution)/shard_map/ppermute | solution.py:43
  115.2 9.5 %collective-permute-done.2 = f32[3,4,6,1664]{3,1,2,0:T(4,128)} collective-permute-done((f32[3,4,6,1664]{3,1,2,0:T(4,128)}, f32[3,4,6,1664]{3,1,2,0:T(4,128)}, u32[]{:S(2)}, u32[]{:S(2)}) %collective-permute-start.2) | collective-permute-done | bytes 479264 | tf_op jit(solution)/shard_map/ppermute | solution.py:43
  124.7 8.8 %collective-permute-done.3 = f32[3,4,6,1664]{3,1,2,0:T(4,128)} collective-permute-done((f32[3,4,6,1664]{3,1,2,0:T(4,128)}, f32[3,4,6,1664]{3,1,2,0:T(4,128)}, u32[]{:S(2)}, u32[]{:S(2)}) %collective-permute-start.3) | collective-permute-done | bytes 479264 | tf_op jit(solution)/shard_map/ppermute | solution.py:43
  133.5 1.7 fusion.6
  137.0 1.9 collective-permute-start.4
  138.9 2.5 collective-permute-start.5
  141.5 5.1 %collective-permute-start.6 = (f32[3,1,6,1664]{3,1,2,0:T(1,128)S(1)}, f32[3,1,6,1664]{3,1,2,0:T(1,128)}, u32[]{:S(2)}, u32[]{:S(2)}) collective-permute-start(f32[3,1,6,1664]{3,1,2,0:T(1,128)S(1)} %get-tuple-element.50), channel_id=1, source_target_pairs={{0,384},{128,256},{256,128},{384,0},{1,385},{129,257},{257,129},{3... | collective-permute-start | bytes 359432 | tf_op jit(solution)/shard_map/ppermute | solution.py:43
  153.3 3.7 %collective-permute-start.7 = (bf16[3,1,6,1664]{3,2,0,1:T(8,128)(2,1)}, bf16[3,1,6,1664]{3,2,0,1:T(8,128)(2,1)}, u32[]{:S(2)}, u32[]{:S(2)}) collective-permute-start(bf16[3,1,6,1664]{3,2,0,1:T(8,128)(2,1)} %maximum_bitcast_fusion.1), channel_id=1, source_target_pairs={{0,128},{128,0},{256,384},{384,256},{1,129},{129,1},{257,385},{385... | collective-permute-start | bytes 179720 | tf_op jit(solution)/shard_map/ppermute | solution.py:52
  157.0 3.6 %collective-permute-start.8 = (bf16[3,1,6,1664]{3,2,0,1:T(8,128)(2,1)}, bf16[3,1,6,1664]{3,2,0,1:T(8,128)(2,1)}, u32[]{:S(2)}, u32[]{:S(2)}) collective-permute-start(bf16[3,1,6,1664]{3,2,0,1:T(8,128)(2,1)} %maximum_bitcast_fusion.1), channel_id=1, source_target_pairs={{0,256},{128,384},{256,0},{384,128},{1,257},{129,385},{257,1},{385... | collective-permute-start | bytes 179720 | tf_op jit(solution)/shard_map/ppermute | solution.py:52
  160.6 2.7 %collective-permute-start.9 = (bf16[3,1,6,1664]{3,2,0,1:T(8,128)(2,1)}, bf16[3,1,6,1664]{3,2,0,1:T(8,128)(2,1)}, u32[]{:S(2)}, u32[]{:S(2)}) collective-permute-start(bf16[3,1,6,1664]{3,2,0,1:T(8,128)(2,1)} %maximum_bitcast_fusion.1), channel_id=1, source_target_pairs={{0,384},{128,256},{256,128},{384,0},{1,385},{129,257},{257,129},{3... | collective-permute-start | bytes 179720 | tf_op jit(solution)/shard_map/ppermute | solution.py:52
  164.7 2.6 collective-permute-done.9
  170.2 1.9 collective-permute-start.10
  172.2 5.4 %collective-permute-start.11 = (bf16[3,4,6,1664]{3,2,0,1:T(8,128)(2,1)}, bf16[3,4,6,1664]{3,2,0,1:T(8,128)(2,1)}, u32[]{:S(2)}, u32[]{:S(2)}) collective-permute-start(bf16[3,4,6,1664]{3,2,0,1:T(8,128)(2,1)} %maximum_bitcast_fusion), channel_id=1, source_target_pairs={{0,64},{32,96},{64,0},{96,32},{1,65},{33,97},{65,1},{97,33},{2,66}... | collective-permute-start | bytes 718856 | tf_op jit(solution)/shard_map/ppermute | solution.py:52
  177.6 2.4 collective-permute-start.12
  180.1 5.1 %collective-permute-done.11 = bf16[3,4,6,1664]{3,2,0,1:T(8,128)(2,1)} collective-permute-done((bf16[3,4,6,1664]{3,2,0,1:T(8,128)(2,1)}, bf16[3,4,6,1664]{3,2,0,1:T(8,128)(2,1)}, u32[]{:S(2)}, u32[]{:S(2)}) %collective-permute-start.11) | collective-permute-done | bytes 239648 | tf_op jit(solution)/shard_map/ppermute | solution.py:52
  185.2 6.7 %collective-permute-done.12 = bf16[3,4,6,1664]{3,2,0,1:T(8,128)(2,1)} collective-permute-done((bf16[3,4,6,1664]{3,2,0,1:T(8,128)(2,1)}, bf16[3,4,6,1664]{3,2,0,1:T(8,128)(2,1)}, u32[]{:S(2)}, u32[]{:S(2)}) %collective-permute-start.12) | collective-permute-done | bytes 239648 | tf_op jit(solution)/shard_map/ppermute | solution.py:52
  196.6 2.4 reshape.300
  199.0 5.3 %collective-permute-start.13 = (bf16[3,16,6,1664]{3,1,2,0:T(8,128)(2,1)}, bf16[3,16,6,1664]{3,1,2,0:T(8,128)(2,1)}, u32[]{:S(2)}, u32[]{:S(2)}) collective-permute-start(bf16[3,16,6,1664]{3,1,2,0:T(8,128)(2,1)} %reshape.300), channel_id=1, source_target_pairs={{0,16},{16,0},{1,17},{17,1},{2,18},{18,2},{3,19},{19,3},{4,20},{20... | collective-permute-start | bytes 2875400 | tf_op jit(solution)/shard_map/ppermute | solution.py:52
  204.3 2.4 collective-permute-done.13
  210.8 2.1 squeeze.108
  212.9 2.6 fusion.55
  216.5 2.1 squeeze.109
  218.6 2.7 %convolution_add_fusion = f32[192,512]{1,0:T(8,128)} fusion(f32[192,512]{1,0:T(8,128)} %fusion.55, bf16[192,1664]{1,0:T(8,128)(2,1)} %squeeze.109, bf16[512,1664]{1,0:T(8,128)(2,1)S(1)} %copy-done.2), kind=kOutput, calls=%fused_computation.14 | convolution fusion | flops 327254016 | bytes 3129344 | tf_op jit(solution)/shard_map/dot_general | solution.py:94
  225.9 1.9 collective-permute-start.14
  227.8 1.9 collective-permute-start.15
  229.7 5.4 %collective-permute-start.16 = (f32[4,13,512]{2,1,0:T(8,128)S(1)}, f32[4,13,512]{2,1,0:T(8,128)S(1)}, u32[]{:S(2)}, u32[]{:S(2)}) collective-permute-start(f32[4,13,512]{2,1,0:T(8,128)S(1)} %get-tuple-element.48), channel_id=1, source_target_pairs={{0,3},{1,2},{2,1},{3,0},{4,7},{5,6},{6,5},{7,4},{8,11},{9,10},{10,... | collective-permute-start | bytes 319496 | tf_op jit(solution)/shard_map/ppermute | solution.py:26
  235.2 5.7 %collective-permute-done.15 = f32[4,13,512]{2,1,0:T(8,128)S(1)} collective-permute-done((f32[4,13,512]{2,1,0:T(8,128)S(1)}, f32[4,13,512]{2,1,0:T(8,128)S(1)}, u32[]{:S(2)}, u32[]{:S(2)}) %collective-permute-start.15) | collective-permute-done | bytes 106528 | tf_op jit(solution)/shard_map/ppermute | solution.py:26
  241.0 2.6 collective-permute-start.17
  243.6 9.6 %collective-permute-start.18 = (f32[1,13,512]{2,1,0:T(8,128)S(1)}, f32[1,13,512]{2,1,0:T(8,128)S(1)}, u32[]{:S(2)}, u32[]{:S(2)}) collective-permute-start(f32[1,13,512]{2,1,0:T(8,128)S(1)} %get-tuple-element.58), channel_id=1, source_target_pairs={{0,8},{1,9},{2,10},{3,11},{4,12},{5,13},{6,14},{7,15},{8,0},{9,1},... | collective-permute-start | bytes 79880 | tf_op jit(solution)/shard_map/ppermute | solution.py:26
  253.2 4.0 %collective-permute-start.19 = (f32[1,13,512]{2,1,0:T(8,128)S(1)}, f32[1,13,512]{2,1,0:T(8,128)S(1)}, u32[]{:S(2)}, u32[]{:S(2)}) collective-permute-start(f32[1,13,512]{2,1,0:T(8,128)S(1)} %get-tuple-element.57), channel_id=1, source_target_pairs={{0,12},{1,13},{2,14},{3,15},{4,8},{5,9},{6,10},{7,11},{8,4},{9,5},... | collective-permute-start | bytes 79880 | tf_op jit(solution)/shard_map/ppermute | solution.py:26
  257.3 4.9 %collective-permute-done.19 = f32[1,13,512]{2,1,0:T(8,128)S(1)} collective-permute-done((f32[1,13,512]{2,1,0:T(8,128)S(1)}, f32[1,13,512]{2,1,0:T(8,128)S(1)}, u32[]{:S(2)}, u32[]{:S(2)}) %collective-permute-start.19) | collective-permute-done | bytes 26656 | tf_op jit(solution)/shard_map/ppermute | solution.py:26
  (96 shorter events, 38.9 us)
Async XLA Ops:
  0.0 68.4 %copy-start = (bf16[512,1664]{1,0:T(8,128)(2,1)S(1)}, bf16[512,1664]{1,0:T(8,128)(2,1)}, u32[]{:S(2)}) copy-start(bf16[512,1664]{1,0:T(8,128)(2,1)} %param.13) | copy-start | bytes 5111812
  0.0 65.6 %copy-start.16 = (bf16[512]{0:T(512)(128)(2,1)S(1)}, bf16[512]{0:T(512)(128)(2,1)}, u32[]{:S(2)}) copy-start(bf16[512]{0:T(512)(128)(2,1)} %param.12) | copy-start | bytes 3076
  0.9 65.9 %copy-start.2 = (bf16[512,1664]{1,0:T(8,128)(2,1)S(1)}, bf16[512,1664]{1,0:T(8,128)(2,1)}, u32[]{:S(2)}) copy-start(bf16[512,1664]{1,0:T(8,128)(2,1)} %param.14) | copy-start | bytes 5111812
  71.8 2.4 copy-start.3
  71.8 2.4 copy-start.4
  74.6 2.5 copy-start.1
  77.1 10.1 %collective-permute-start = (f32[3,16,6,1664]{3,1,2,0:T(8,128)}, f32[3,16,6,1664]{3,1,2,0:T(8,128)}, u32[]{:S(2)}, u32[]{:S(2)}) collective-permute-start(f32[3,16,6,1664]{3,1,2,0:T(8,128)} %dynamic-slice_bitcast_fusion), channel_id=1, source_target_pairs={{0,16},{16,0},{1,17},{17,1},{2,18},{18,2},{3,19},{19,3},{4,20},{20... | collective-permute-start | bytes 5750792 | tf_op jit(solution)/shard_map/ppermute | solution.py:43
  100.9 14.3 %collective-permute-start.1 = (f32[3,4,6,1664]{3,1,2,0:T(4,128)}, f32[3,4,6,1664]{3,1,2,0:T(4,128)}, u32[]{:S(2)}, u32[]{:S(2)}) collective-permute-start(f32[3,4,6,1664]{3,1,2,0:T(4,128)} %bitcast.226), channel_id=1, source_target_pairs={{0,32},{32,0},{64,96},{96,64},{1,33},{33,1},{65,97},{97,65},{2,34}... | collective-permute-start | bytes 1437704 | tf_op jit(solution)/shard_map/ppermute | solution.py:43
  103.7 21.0 %collective-permute-start.2 = (f32[3,4,6,1664]{3,1,2,0:T(4,128)}, f32[3,4,6,1664]{3,1,2,0:T(4,128)}, u32[]{:S(2)}, u32[]{:S(2)}) collective-permute-start(f32[3,4,6,1664]{3,1,2,0:T(4,128)} %bitcast.225), channel_id=1, source_target_pairs={{0,64},{32,96},{64,0},{96,32},{1,65},{33,97},{65,1},{97,33},{2,66}... | collective-permute-start | bytes 1437704 | tf_op jit(solution)/shard_map/ppermute | solution.py:43
  107.1 26.4 %collective-permute-start.3 = (f32[3,4,6,1664]{3,1,2,0:T(4,128)}, f32[3,4,6,1664]{3,1,2,0:T(4,128)}, u32[]{:S(2)}, u32[]{:S(2)}) collective-permute-start(f32[3,4,6,1664]{3,1,2,0:T(4,128)} %bitcast.224), channel_id=1, source_target_pairs={{0,96},{32,64},{64,32},{96,0},{1,97},{33,65},{65,33},{97,1},{2,98}... | collective-permute-start | bytes 1437704 | tf_op jit(solution)/shard_map/ppermute | solution.py:43
  135.2 0.8 copy-start.6
  137.0 10.9 %collective-permute-start.4 = (f32[3,1,6,1664]{3,1,2,0:T(1,128)}, f32[3,1,6,1664]{3,1,2,0:T(1,128)}, u32[]{:S(2)}, u32[]{:S(2)}) collective-permute-start(f32[3,1,6,1664]{3,1,2,0:T(1,128)} %get-tuple-element.49), channel_id=1, source_target_pairs={{0,128},{128,0},{256,384},{384,256},{1,129},{129,1},{257,385},{385... | collective-permute-start | bytes 359432 | tf_op jit(solution)/shard_map/ppermute | solution.py:43
  138.9 9.0 %collective-permute-start.5 = (f32[3,1,6,1664]{3,1,2,0:T(1,128)}, f32[3,1,6,1664]{3,1,2,0:T(1,128)}, u32[]{:S(2)}, u32[]{:S(2)}) collective-permute-start(f32[3,1,6,1664]{3,1,2,0:T(1,128)} %get-tuple-element.51), channel_id=1, source_target_pairs={{0,256},{128,384},{256,0},{384,128},{1,257},{129,385},{257,1},{385... | collective-permute-start | bytes 359432 | tf_op jit(solution)/shard_map/ppermute | solution.py:43
  141.5 7.9 %collective-permute-start.6 = (f32[3,1,6,1664]{3,1,2,0:T(1,128)S(1)}, f32[3,1,6,1664]{3,1,2,0:T(1,128)}, u32[]{:S(2)}, u32[]{:S(2)}) collective-permute-start(f32[3,1,6,1664]{3,1,2,0:T(1,128)S(1)} %get-tuple-element.50), channel_id=1, source_target_pairs={{0,384},{128,256},{256,128},{384,0},{1,385},{129,257},{257,129},{3... | collective-permute-start | bytes 359432 | tf_op jit(solution)/shard_map/ppermute | solution.py:43
  152.7 12.0 %copy-start.13 = (bf16[1,6,1664]{2,1,0:T(8,128)(2,1)}, bf16[1,6,1664]{2,1,0:T(8,128)(2,1)S(1)}, u32[]{:S(2)}) copy-start(bf16[1,6,1664]{2,1,0:T(8,128)(2,1)S(1)} %scatter.9) | copy-start | bytes 59908
  153.3 10.0 %collective-permute-start.7 = (bf16[3,1,6,1664]{3,2,0,1:T(8,128)(2,1)}, bf16[3,1,6,1664]{3,2,0,1:T(8,128)(2,1)}, u32[]{:S(2)}, u32[]{:S(2)}) collective-permute-start(bf16[3,1,6,1664]{3,2,0,1:T(8,128)(2,1)} %maximum_bitcast_fusion.1), channel_id=1, source_target_pairs={{0,128},{128,0},{256,384},{384,256},{1,129},{129,1},{257,385},{385... | collective-permute-start | bytes 179720 | tf_op jit(solution)/shard_map/ppermute | solution.py:52
  157.0 7.7 %collective-permute-start.8 = (bf16[3,1,6,1664]{3,2,0,1:T(8,128)(2,1)}, bf16[3,1,6,1664]{3,2,0,1:T(8,128)(2,1)}, u32[]{:S(2)}, u32[]{:S(2)}) collective-permute-start(bf16[3,1,6,1664]{3,2,0,1:T(8,128)(2,1)} %maximum_bitcast_fusion.1), channel_id=1, source_target_pairs={{0,256},{128,384},{256,0},{384,128},{1,257},{129,385},{257,1},{385... | collective-permute-start | bytes 179720 | tf_op jit(solution)/shard_map/ppermute | solution.py:52
  160.6 6.7 %collective-permute-start.9 = (bf16[3,1,6,1664]{3,2,0,1:T(8,128)(2,1)}, bf16[3,1,6,1664]{3,2,0,1:T(8,128)(2,1)}, u32[]{:S(2)}, u32[]{:S(2)}) collective-permute-start(bf16[3,1,6,1664]{3,2,0,1:T(8,128)(2,1)} %maximum_bitcast_fusion.1), channel_id=1, source_target_pairs={{0,384},{128,256},{256,128},{384,0},{1,385},{129,257},{257,129},{3... | collective-permute-start | bytes 179720 | tf_op jit(solution)/shard_map/ppermute | solution.py:52
  168.3 1.1 copy-start.7
  169.4 0.9 copy-start.9
  169.4 2.8 %copy-start.11 = (bf16[3,1,1,6,1664]{4,3,0,2,1:T(8,128)(2,1)}, bf16[3,1,1,6,1664]{4,3,0,2,1:T(8,128)(2,1)S(1)}, u32[]{:S(2)}) copy-start(bf16[3,1,1,6,1664]{4,3,0,2,1:T(8,128)(2,1)S(1)} %get-tuple-element.53) | copy-start | bytes 179716
  170.2 9.9 %collective-permute-start.10 = (bf16[3,4,6,1664]{3,2,0,1:T(8,128)(2,1)}, bf16[3,4,6,1664]{3,2,0,1:T(8,128)(2,1)}, u32[]{:S(2)}, u32[]{:S(2)}) collective-permute-start(bf16[3,4,6,1664]{3,2,0,1:T(8,128)(2,1)} %maximum_bitcast_fusion), channel_id=1, source_target_pairs={{0,32},{32,0},{64,96},{96,64},{1,33},{33,1},{65,97},{97,65},{2,34}... | collective-permute-start | bytes 718856 | tf_op jit(solution)/shard_map/ppermute | solution.py:52
  172.2 13.1 %collective-permute-start.11 = (bf16[3,4,6,1664]{3,2,0,1:T(8,128)(2,1)}, bf16[3,4,6,1664]{3,2,0,1:T(8,128)(2,1)}, u32[]{:S(2)}, u32[]{:S(2)}) collective-permute-start(bf16[3,4,6,1664]{3,2,0,1:T(8,128)(2,1)} %maximum_bitcast_fusion), channel_id=1, source_target_pairs={{0,64},{32,96},{64,0},{96,32},{1,65},{33,97},{65,1},{97,33},{2,66}... | collective-permute-start | bytes 718856 | tf_op jit(solution)/shard_map/ppermute | solution.py:52
  177.6 14.3 %collective-permute-start.12 = (bf16[3,4,6,1664]{3,2,0,1:T(8,128)(2,1)}, bf16[3,4,6,1664]{3,2,0,1:T(8,128)(2,1)}, u32[]{:S(2)}, u32[]{:S(2)}) collective-permute-start(bf16[3,4,6,1664]{3,2,0,1:T(8,128)(2,1)} %maximum_bitcast_fusion), channel_id=1, source_target_pairs={{0,96},{32,64},{64,32},{96,0},{1,97},{33,65},{65,33},{97,1},{2,98}... | collective-permute-start | bytes 718856 | tf_op jit(solution)/shard_map/ppermute | solution.py:52
  180.1 13.3 %copy-start.8 = (bf16[3,1,1,6,1664]{4,3,0,2,1:T(8,128)(2,1)S(1)}, bf16[3,1,1,6,1664]{4,3,0,2,1:T(8,128)(2,1)}, u32[]{:S(2)}) copy-start(bf16[3,1,1,6,1664]{4,3,0,2,1:T(8,128)(2,1)} %copy-done.7) | copy-start | bytes 179716
  180.1 13.3 %copy-start.10 = (bf16[3,1,1,6,1664]{4,3,0,2,1:T(8,128)(2,1)S(1)}, bf16[3,1,1,6,1664]{4,3,0,2,1:T(8,128)(2,1)}, u32[]{:S(2)}) copy-start(bf16[3,1,1,6,1664]{4,3,0,2,1:T(8,128)(2,1)} %copy-done.9) | copy-start | bytes 179716
  180.1 13.3 %copy-start.12 = (bf16[3,1,1,6,1664]{4,3,0,2,1:T(8,128)(2,1)S(1)}, bf16[3,1,1,6,1664]{4,3,0,2,1:T(8,128)(2,1)}, u32[]{:S(2)}) copy-start(bf16[3,1,1,6,1664]{4,3,0,2,1:T(8,128)(2,1)} %copy-done.11) | copy-start | bytes 179716
  199.0 7.8 %collective-permute-start.13 = (bf16[3,16,6,1664]{3,1,2,0:T(8,128)(2,1)}, bf16[3,16,6,1664]{3,1,2,0:T(8,128)(2,1)}, u32[]{:S(2)}, u32[]{:S(2)}) collective-permute-start(bf16[3,16,6,1664]{3,1,2,0:T(8,128)(2,1)} %reshape.300), channel_id=1, source_target_pairs={{0,16},{16,0},{1,17},{17,1},{2,18},{18,2},{3,19},{19,3},{4,20},{20... | collective-permute-start | bytes 2875400 | tf_op jit(solution)/shard_map/ppermute | solution.py:52
  212.9 2.6 copy-start.5
  224.6 37.6 %copy-start.14 = (bf16[12,512]{1,0:T(8,128)(2,1)S(1)}, bf16[12,512]{1,0:T(8,128)(2,1)}, u32[]{:S(2)}) copy-start(bf16[12,512]{1,0:T(8,128)(2,1)} %param.11) | copy-start | bytes 36868
  224.6 37.6 %copy-start.15 = (bf16[12,512]{1,0:T(8,128)(2,1)S(1)}, bf16[12,512]{1,0:T(8,128)(2,1)}, u32[]{:S(2)}) copy-start(bf16[12,512]{1,0:T(8,128)(2,1)} %param.10) | copy-start | bytes 36868
  225.9 9.3 %collective-permute-start.14 = (f32[4,13,512]{2,1,0:T(8,128)S(1)}, f32[4,13,512]{2,1,0:T(8,128)S(1)}, u32[]{:S(2)}, u32[]{:S(2)}) collective-permute-start(f32[4,13,512]{2,1,0:T(8,128)S(1)} %get-tuple-element.46), channel_id=1, source_target_pairs={{0,1},{1,0},{2,3},{3,2},{4,5},{5,4},{6,7},{7,6},{8,9},{9,8},{10,11... | collective-permute-start | bytes 319496 | tf_op jit(solution)/shard_map/ppermute | solution.py:26
  227.8 13.1 %collective-permute-start.15 = (f32[4,13,512]{2,1,0:T(8,128)S(1)}, f32[4,13,512]{2,1,0:T(8,128)S(1)}, u32[]{:S(2)}, u32[]{:S(2)}) collective-permute-start(f32[4,13,512]{2,1,0:T(8,128)S(1)} %get-tuple-element.47), channel_id=1, source_target_pairs={{0,2},{1,3},{2,0},{3,1},{4,6},{5,7},{6,4},{7,5},{8,10},{9,11},{10,... | collective-permute-start | bytes 319496 | tf_op jit(solution)/shard_map/ppermute | solution.py:26
  229.7 11.2 %collective-permute-start.16 = (f32[4,13,512]{2,1,0:T(8,128)S(1)}, f32[4,13,512]{2,1,0:T(8,128)S(1)}, u32[]{:S(2)}, u32[]{:S(2)}) collective-permute-start(f32[4,13,512]{2,1,0:T(8,128)S(1)} %get-tuple-element.48), channel_id=1, source_target_pairs={{0,3},{1,2},{2,1},{3,0},{4,7},{5,6},{6,5},{7,4},{8,11},{9,10},{10,... | collective-permute-start | bytes 319496 | tf_op jit(solution)/shard_map/ppermute | solution.py:26
  241.0 16.3 %collective-permute-start.17 = (f32[1,13,512]{2,1,0:T(8,128)S(1)}, f32[1,13,512]{2,1,0:T(8,128)S(1)}, u32[]{:S(2)}, u32[]{:S(2)}) collective-permute-start(f32[1,13,512]{2,1,0:T(8,128)S(1)} %get-tuple-element.56), channel_id=1, source_target_pairs={{0,4},{1,5},{2,6},{3,7},{4,0},{5,1},{6,2},{7,3},{8,12},{9,13},{10,... | collective-permute-start | bytes 79880 | tf_op jit(solution)/shard_map/ppermute | solution.py:26
  243.6 13.7 %collective-permute-start.18 = (f32[1,13,512]{2,1,0:T(8,128)S(1)}, f32[1,13,512]{2,1,0:T(8,128)S(1)}, u32[]{:S(2)}, u32[]{:S(2)}) collective-permute-start(f32[1,13,512]{2,1,0:T(8,128)S(1)} %get-tuple-element.58), channel_id=1, source_target_pairs={{0,8},{1,9},{2,10},{3,11},{4,12},{5,13},{6,14},{7,15},{8,0},{9,1},... | collective-permute-start | bytes 79880 | tf_op jit(solution)/shard_map/ppermute | solution.py:26
  253.2 9.0 %collective-permute-start.19 = (f32[1,13,512]{2,1,0:T(8,128)S(1)}, f32[1,13,512]{2,1,0:T(8,128)S(1)}, u32[]{:S(2)}, u32[]{:S(2)}) collective-permute-start(f32[1,13,512]{2,1,0:T(8,128)S(1)} %get-tuple-element.57), channel_id=1, source_target_pairs={{0,12},{1,13},{2,14},{3,15},{4,8},{5,9},{6,10},{7,11},{8,4},{9,5},... | collective-permute-start | bytes 79880 | tf_op jit(solution)/shard_map/ppermute | solution.py:26

commit v7 on v6

--- a/solution.py
+++ b/solution.py
@@ -77,16 +77,17 @@
         piece[1], w_down, (((1,), (1,)), ((), ())), preferred_element_type=jnp.float32
     )
     n_wa, width = lax.axis_size(WA), gate_part.shape[1]
-    partial = jnp.stack([gate_part, up_part, back_part]).reshape(3, n_wa, -1, width)
-    part = scatter_blocks(partial, WA[::-1])[:, 0]
+    partial = jnp.stack([gate_part, up_part, back_part]).reshape(3, n_wa, -1)
+    partial = partial.transpose(1, 0, 2).reshape(1, n_wa, -1)
+    part = scatter_blocks(partial, WA[::-1]).reshape(3, -1, width)
     gate, up, d_hidden = part[0], part[1], part[2]
     d_gate, d_up = gate_grads(gate, up, d_hidden)
     dot_rows = jnp.sum(d_gate.astype(jnp.float32) * gate + d_up.astype(jnp.float32) * up, axis=1)
     dot_hi = dot_rows.astype(jnp.bfloat16)
     dot_lo = (dot_rows - dot_hi.astype(jnp.float32)).astype(jnp.bfloat16)
     extra = jnp.zeros_like(d_gate).at[:, 0].set(dot_hi).at[:, 1].set(dot_lo)
-    grads = gather_blocks(jnp.stack([d_gate, d_up, extra])[:, None], WA[::-1])
-    grads = grads.reshape(3, -1, width)
+    grads = gather_blocks(jnp.stack([d_gate, d_up, extra]).reshape(1, 1, -1), WA[::-1])
+    grads = grads.reshape(n_wa, 3, -1, width).transpose(1, 0, 2, 3).reshape(3, -1, width)
     d_gate, d_up = grads[0], grads[1]
     dot_part = grads[2][:, 0].astype(jnp.float32) + grads[2][:, 1].astype(jnp.float32)
     total = lax.dot_general(

time: 267 us -> 292 us (1.094)
  local copies, waits for them, and re-layouts: 35.8 us -> 55.5 us
  other arithmetic: 25.9 us -> 31.7 us
    another operation x4 -> x8, local copies, waits for them, and re-layouts: 1.94 us -> 23.5 us  [the longest x3 10.5 us: local(): partial = jnp.stack([gate_part, up_part, back_part]).reshape(3, n_wa, -1)]
    transpose x0 -> x1, other arithmetic: none -> 6.7 us  [local(): partial = partial.transpose(1, 0, 2).reshape(1, n_wa, -1)]
    dynamic_slice x1, local copies, waits for them, and re-layouts: 6.32 us -> 0.92 us  [scatter_blocks(): total = lax.dynamic_index_in_dim(groups, mine, axis=2, keepdims=False)]
    slice x3 -> x1, local copies, waits for them, and re-layouts: 3.94 us -> 0.31 us  [local(): gate, up, d_hidden = (part[0], part[1], part[2])]
    squeeze x2, local copies, waits for them, and re-layouts: 2.57 us -> 5.98 us  [scatter_blocks(): send = lax.dynamic_index_in_dim(groups, mine ^ k, axis=2, keepdims=False)]
    squeeze x1 -> x6, local copies, waits for them, and re-layouts: 0.06 us -> 3.13 us  [local(): gate, up, d_hidden = (part[0], part[1], part[2])]
    another operation x7 -> x5, other arithmetic: 8.17 us -> 6.82 us  [gather_blocks(): x = jnp.stack(placed, axis=2).reshape(x.shape[0], -1, *x.shape[2:])]
where the time goes in v7:
time: 292 us; the launch traced here: 288 us
  starting transfers between devices  76.4 us (26%)
  blocking collectives  58.5 us (20%)
  local copies, waits for them, and re-layouts  55.5 us (19%)
  waiting for transfers between devices  52.5 us (18%)
  other arithmetic  31.7 us (11%)
  matrix products  12.8 us (4%)
    all_gather x1, blocking collectives, local(): lax.all_gather(jnp.stack([residual_in, grad_out]), 'ha', axis=1, tiled=True)  31.1 us
    psum x3, blocking collectives, local(): squares = lax.psum(lax.psum(lax.psum(squares, 'core'), 'y'), 'x')  27.4 us
    ppermute x7, waiting for transfers between devices, scatter_blocks(): total = total + lax.ppermute(send, axis, _exchange(axis, k))  26.3 us
    ppermute x7, starting transfers between devices, scatter_blocks(): total = total + lax.ppermute(send, axis, _exchange(axis, k))  25.6 us
    ppermute x6, starting transfers between devices, scatter_sum(): lax.ppermute(send, axis, [(i, i ^ k << shift) for i in range(n)])  25.5 us
    ppermute x7, starting transfers between devices, gather_blocks(): lax.ppermute(x, axis, _exchange(axis, k))  25.3 us
    ppermute x7, waiting for transfers between devices, gather_blocks(): lax.ppermute(x, axis, _exchange(axis, k))  15.5 us
    ppermute x6, waiting for transfers between devices, scatter_sum(): lax.ppermute(send, axis, [(i, i ^ k << shift) for i in range(n)])  10.6 us
  transfers between devices with their start and end apart: 20, of which 12 were waited for; matrix products, arithmetic and copies ran while one was open for 1% of the time, Pallas kernels for 0%

profile of v7, /device:TPU:1, one launch (start us, length us, event | category | flops | bytes accessed | tf_op | source)
XLA Modules:
  0.0 287.9 jit_solution(9662013138112088477)
XLA Ops:
  0.9 31.1 %all_gather.3 = bf16[2,192,512]{2,0,1:T(2,128)(2,1)S(1)} all-gather(bf16[2,12,512]{2,0,1:T(2,128)(2,1)S(1)} %copy.43), channel_id=1, replica_groups=mesh['x'=4,'y'=4,'core'=2,'ha'=16] {'ha'}, dimensions={1}, use_global_device_ids=true | all-gather | bytes 417792 | tf_op jit(solution)/shard_map/all_gather | solution.py:67
  33.4 10.2 %psum.21 = f32[192]{0:T(256)S(1)} all-reduce(f32[192]{0:T(256)S(1)} %fusion.2), channel_id=1, replica_groups=mesh['x'=4,'y'=4,'core'=2,'ha'=16] {'core'}, use_global_device_ids=true, to_apply=%region_1.0 | all-reduce | flops 192 | bytes 1536 | tf_op jit(solution)/shard_map/psum | solution.py:70
  43.7 8.7 %psum.22 = f32[192]{0:T(256)S(1)} all-reduce(f32[192]{0:T(256)S(1)} %psum.21), channel_id=1, replica_groups=mesh['x'=4,'y'=4,'core'=2,'ha'=16] {'y'}, use_global_device_ids=true, to_apply=%region_2.0 | all-reduce | flops 192 | bytes 1536 | tf_op jit(solution)/shard_map/psum | solution.py:70
  52.3 8.5 %psum.23 = f32[192]{0:T(256)S(1)} all-reduce(f32[192]{0:T(256)S(1)} %psum.22), channel_id=1, replica_groups=mesh['x'=4,'y'=4,'core'=2,'ha'=16] {'x'}, use_global_device_ids=true, to_apply=%region_3.0 | all-reduce | flops 192 | bytes 1536 | tf_op jit(solution)/shard_map/psum | solution.py:70
  62.5 3.6 %stack.93 = f32[1,32,9984]{2,0,1:T(1,128)} reshape(f32[192,1664]{1,0:T(8,128)} %fusion.32) | data formatting | bytes 2555904 | tf_op jit(solution)/shard_map/stack | solution.py:80
  66.1 2.6 fusion.30
  68.7 3.4 %stack.94 = f32[1,32,9984]{2,0,1:T(1,128)} reshape(f32[192,1664]{1,0:T(8,128)} %fusion.30) | data formatting | bytes 2555904 | tf_op jit(solution)/shard_map/stack | solution.py:80
  72.1 3.4 %fusion.5 = f32[192,1664]{1,0:T(8,128)} fusion(bf16[1664,512]{1,0:T(8,128)(2,1)} %param.15, bf16[1,192,512]{2,0,1:T(2,128)(2,1)} %get-tuple-element.58), kind=kOutput, calls=%fused_computation.46 | convolution fusion | flops 327155712 | bytes 3178496 | tf_op jit(solution)/shard_map/dot_general | solution.py:76
  75.5 3.5 %stack.95 = f32[1,32,9984]{2,0,1:T(1,128)} reshape(f32[192,1664]{1,0:T(8,128)} %fusion.5) | data formatting | bytes 2555904 | tf_op jit(solution)/shard_map/stack | solution.py:80
  79.0 6.7 %maximum_bitcast_fusion = f32[32,3,9984]{2,1,0:T(4,128)} fusion(f32[1,32,9984]{2,0,1:T(1,128)} %stack.95, f32[1,32,9984]{2,0,1:T(1,128)} %stack.94, f32[1,32,9984]{2,0,1:T(1,128)} %stack.93), kind=kLoop, calls=%fused_computation | loop fusion | flops 1916928 | bytes 7667712 | tf_op jit(solution)/shard_map/transpose | solution.py:81
  85.7 8.4 %reshape_reshape.6 = f32[1,16,2,29952]{3,2,1,0:T(2,128)} reshape(f32[32,3,9984]{2,1,0:T(4,128)} %maximum_bitcast_fusion) | data formatting | bytes 7667712 | tf_op jit(solution)/shard_map/reshape;reshape | solution.py:38
  94.1 5.0 %dynamic-slice_bitcast_fusion = f32[1,16,29952]{2,0,1:T(1,128)} fusion(f32[1,16,2,29952]{3,2,1,0:T(2,128)} %reshape_reshape.6, s32[]{:T(128)S(6)} %select_n.229), kind=kLoop, calls=%fused_computation.3 | loop fusion | bytes 3833860 | tf_op jit(solution)/shard_map/jit(dynamic_index_in_dim)/squeeze | solution.py:42
  99.1 6.5 %collective-permute-start = (f32[1,16,29952]{2,0,1:T(1,128)}, f32[1,16,29952]{2,0,1:T(1,128)}, u32[]{:S(2)}, u32[]{:S(2)}) collective-permute-start(f32[1,16,29952]{2,0,1:T(1,128)} %dynamic-slice_bitcast_fusion), channel_id=1, source_target_pairs={{0,16},{16,0},{1,17},{17,1},{2,18},{18,2},{3,19},{19,3},{4,20},{20... | collective-permute-start | bytes 5750792 | tf_op jit(solution)/shard_map/ppermute | solution.py:43
  105.6 3.6 %collective-permute-done = f32[1,16,29952]{2,0,1:T(1,128)} collective-permute-done((f32[1,16,29952]{2,0,1:T(1,128)}, f32[1,16,29952]{2,0,1:T(1,128)}, u32[]{:S(2)}, u32[]{:S(2)}) %collective-permute-start) | collective-permute-done | bytes 1916960 | tf_op jit(solution)/shard_map/ppermute | solution.py:43
  109.2 5.3 %bitcast_add_fusion = f32[1,16,29952]{2,0,1:T(1,128)S(1)} fusion(f32[1,16,29952]{2,0,1:T(1,128)} %collective-permute-done, f32[1,16,2,29952]{3,2,1,0:T(2,128)} %reshape_reshape.6, s32[]{:T(128)S(6)} %select_n.228), kind=kLoop, calls=%fused_computation.2 | loop fusion | flops 479232 | bytes 5750788 | tf_op jit(solution)/shard_map/add | solution.py:43
  119.1 2.5 collective-permute-start.2
  122.5 5.1 %collective-permute-start.3 = (f32[1,4,29952]{2,1,0:T(4,128)}, f32[1,4,29952]{2,1,0:T(4,128)}, u32[]{:S(2)}, u32[]{:S(2)}) collective-permute-start(f32[1,4,29952]{2,1,0:T(4,128)} %bitcast.121), channel_id=1, source_target_pairs={{0,96},{32,64},{64,32},{96,0},{1,97},{33,65},{65,33},{97,1},{2,98}... | collective-permute-start | bytes 1437704 | tf_op jit(solution)/shard_map/ppermute | solution.py:43
  127.7 2.9 %collective-permute-done.1 = f32[1,4,29952]{2,1,0:T(4,128)} collective-permute-done((f32[1,4,29952]{2,1,0:T(4,128)}, f32[1,4,29952]{2,1,0:T(4,128)}, u32[]{:S(2)}, u32[]{:S(2)}) %collective-permute-start.1) | collective-permute-done | bytes 479264 | tf_op jit(solution)/shard_map/ppermute | solution.py:43
  130.6 9.5 %collective-permute-done.2 = f32[1,4,29952]{2,1,0:T(4,128)} collective-permute-done((f32[1,4,29952]{2,1,0:T(4,128)}, f32[1,4,29952]{2,1,0:T(4,128)}, u32[]{:S(2)}, u32[]{:S(2)}) %collective-permute-start.2) | collective-permute-done | bytes 479264 | tf_op jit(solution)/shard_map/ppermute | solution.py:43
  140.1 8.8 %collective-permute-done.3 = f32[1,4,29952]{2,1,0:T(4,128)} collective-permute-done((f32[1,4,29952]{2,1,0:T(4,128)}, f32[1,4,29952]{2,1,0:T(4,128)}, u32[]{:S(2)}, u32[]{:S(2)}) %collective-permute-start.3) | collective-permute-done | bytes 479264 | tf_op jit(solution)/shard_map/ppermute | solution.py:43
  154.3 2.5 collective-permute-start.5
  156.9 5.1 %collective-permute-start.6 = (f32[1,1,29952]{2,1,0:T(1,128)S(1)}, f32[1,1,29952]{2,1,0:T(1,128)}, u32[]{:S(2)}, u32[]{:S(2)}) collective-permute-start(f32[1,1,29952]{2,1,0:T(1,128)S(1)} %get-tuple-element.55), channel_id=1, source_target_pairs={{0,384},{128,256},{256,128},{384,0},{1,385},{129,257},{257,129},{3... | collective-permute-start | bytes 359432 | tf_op jit(solution)/shard_map/ppermute | solution.py:43
  174.8 3.7 %collective-permute-start.7 = (bf16[1,1,29952]{2,1,0:T(2,128)(2,1)S(1)}, bf16[1,1,29952]{2,1,0:T(2,128)(2,1)}, u32[]{:S(2)}, u32[]{:S(2)}) collective-permute-start(bf16[1,1,29952]{2,1,0:T(2,128)(2,1)S(1)} %reshape.260), channel_id=1, source_target_pairs={{0,128},{128,0},{256,384},{384,256},{1,129},{129,1},{257,385},{385... | collective-permute-start | bytes 179720 | tf_op jit(solution)/shard_map/ppermute | solution.py:52
  178.6 3.6 %collective-permute-start.8 = (bf16[1,1,29952]{2,1,0:T(2,128)(2,1)S(1)}, bf16[1,1,29952]{2,1,0:T(2,128)(2,1)}, u32[]{:S(2)}, u32[]{:S(2)}) collective-permute-start(bf16[1,1,29952]{2,1,0:T(2,128)(2,1)S(1)} %reshape.260), channel_id=1, source_target_pairs={{0,256},{128,384},{256,0},{384,128},{1,257},{129,385},{257,1},{385... | collective-permute-start | bytes 179720 | tf_op jit(solution)/shard_map/ppermute | solution.py:52
  182.1 2.7 collective-permute-start.9
  184.8 2.0 collective-permute-done.8
  186.9 2.7 collective-permute-done.9
  195.1 5.3 %collective-permute-start.11 = (bf16[1,4,29952]{2,1,0:T(4,128)(2,1)}, bf16[1,4,29952]{2,1,0:T(4,128)(2,1)}, u32[]{:S(2)}, u32[]{:S(2)}) collective-permute-start(bf16[1,4,29952]{2,1,0:T(4,128)(2,1)} %maximum_bitcast_fusion.1), channel_id=1, source_target_pairs={{0,64},{32,96},{64,0},{96,32},{1,65},{33,97},{65,1},{97,33},{2,66}... | collective-permute-start | bytes 718856 | tf_op jit(solution)/shard_map/ppermute | solution.py:52
  200.4 2.4 collective-permute-start.12
  202.9 2.5 collective-permute-done.11
  205.3 6.1 %collective-permute-done.12 = bf16[1,4,29952]{2,1,0:T(4,128)(2,1)} collective-permute-done((bf16[1,4,29952]{2,1,0:T(4,128)(2,1)}, bf16[1,4,29952]{2,1,0:T(4,128)(2,1)}, u32[]{:S(2)}, u32[]{:S(2)}) %collective-permute-start.12) | collective-permute-done | bytes 239648 | tf_op jit(solution)/shard_map/ppermute | solution.py:52
  211.4 2.5 select_bitcast_fusion.5
  216.1 2.4 reshape.262
  218.5 5.8 %collective-permute-start.13 = (bf16[1,16,29952]{2,1,0:T(8,128)(2,1)}, bf16[1,16,29952]{2,1,0:T(8,128)(2,1)}, u32[]{:S(2)}, u32[]{:S(2)}) collective-permute-start(bf16[1,16,29952]{2,1,0:T(8,128)(2,1)} %reshape.262), channel_id=1, source_target_pairs={{0,16},{16,0},{1,17},{17,1},{2,18},{18,2},{3,19},{19,3},{4,20},{20... | collective-permute-start | bytes 2875400 | tf_op jit(solution)/shard_map/ppermute | solution.py:52
  224.3 2.2 collective-permute-done.13
  228.4 2.7 copy.51
  231.1 4.4 %reshape_reshape.7 = bf16[32,3,6,1664]{3,2,1,0:T(8,128)(2,1)} reshape(bf16[1,16,2,29952]{3,2,1,0:T(2,128)(2,1)} %copy.51) | data formatting | bytes 3833856 | tf_op jit(solution)/shard_map/reshape;reshape | solution.py:90
  235.5 3.2 %fusion.34 = (bf16[1,32,6,1664]{3,2,0,1:T(8,128)(2,1)}, bf16[1,32,6,1664]{3,2,0,1:T(8,128)(2,1)}, bf16[1,32,6,1664]{3,2,0,1:T(8,128)(2,1)}) fusion(bf16[3,32,6,1664]{3,2,0,1:T(8,128)(2,1)} %bitcast.124), kind=kLoop, calls=%fused_computation.110 | loop fusion | bytes 3833856 | tf_op jit(solution)/shard_map/slice | solution.py:92
  238.7 2.1 squeeze.110
  240.7 2.5 fusion.35
  243.3 2.1 squeeze.111
  245.3 2.6 convolution_add_fusion
  254.7 5.4 %collective-permute-start.16 = (f32[4,13,512]{2,1,0:T(8,128)S(1)}, f32[4,13,512]{2,1,0:T(8,128)S(1)}, u32[]{:S(2)}, u32[]{:S(2)}) collective-permute-start(f32[4,13,512]{2,1,0:T(8,128)S(1)} %get-tuple-element.49), channel_id=1, source_target_pairs={{0,3},{1,2},{2,1},{3,0},{4,7},{5,6},{6,5},{7,4},{8,11},{9,10},{10,... | collective-permute-start | bytes 319496 | tf_op jit(solution)/shard_map/ppermute | solution.py:26
  260.1 5.7 %collective-permute-done.15 = f32[4,13,512]{2,1,0:T(8,128)S(1)} collective-permute-done((f32[4,13,512]{2,1,0:T(8,128)S(1)}, f32[4,13,512]{2,1,0:T(8,128)S(1)}, u32[]{:S(2)}, u32[]{:S(2)}) %collective-permute-start.15) | collective-permute-done | bytes 106528 | tf_op jit(solution)/shard_map/ppermute | solution.py:26
  265.9 2.6 collective-permute-start.17
  268.5 9.6 %collective-permute-start.18 = (f32[1,13,512]{2,1,0:T(8,128)S(1)}, f32[1,13,512]{2,1,0:T(8,128)S(1)}, u32[]{:S(2)}, u32[]{:S(2)}) collective-permute-start(f32[1,13,512]{2,1,0:T(8,128)S(1)} %get-tuple-element.61), channel_id=1, source_target_pairs={{0,8},{1,9},{2,10},{3,11},{4,12},{5,13},{6,14},{7,15},{8,0},{9,1},... | collective-permute-start | bytes 79880 | tf_op jit(solution)/shard_map/ppermute | solution.py:26
  278.1 4.0 %collective-permute-start.19 = (f32[1,13,512]{2,1,0:T(8,128)S(1)}, f32[1,13,512]{2,1,0:T(8,128)S(1)}, u32[]{:S(2)}, u32[]{:S(2)}) collective-permute-start(f32[1,13,512]{2,1,0:T(8,128)S(1)} %get-tuple-element.60), channel_id=1, source_target_pairs={{0,12},{1,13},{2,14},{3,15},{4,8},{5,9},{6,10},{7,11},{8,4},{9,5},... | collective-permute-start | bytes 79880 | tf_op jit(solution)/shard_map/ppermute | solution.py:26
  282.2 4.9 %collective-permute-done.19 = f32[1,13,512]{2,1,0:T(8,128)S(1)} collective-permute-done((f32[1,13,512]{2,1,0:T(8,128)S(1)}, f32[1,13,512]{2,1,0:T(8,128)S(1)}, u32[]{:S(2)}, u32[]{:S(2)}) %collective-permute-start.19) | collective-permute-done | bytes 26656 | tf_op jit(solution)/shard_map/ppermute | solution.py:26
  (88 shorter events, 44.7 us)
Async XLA Ops:
  0.0 60.8 %copy-start = (bf16[512,1664]{1,0:T(8,128)(2,1)S(1)}, bf16[512,1664]{1,0:T(8,128)(2,1)}, u32[]{:S(2)}) copy-start(bf16[512,1664]{1,0:T(8,128)(2,1)} %param.13) | copy-start | bytes 5111812
  0.0 60.8 %copy-start.10 = (bf16[512]{0:T(512)(128)(2,1)S(1)}, bf16[512]{0:T(512)(128)(2,1)}, u32[]{:S(2)}) copy-start(bf16[512]{0:T(512)(128)(2,1)} %param.12) | copy-start | bytes 3076
  33.3 27.5 %copy-start.2 = (f32[1,192,512]{2,0,1:T(1,128)}, f32[1,192,512]{2,0,1:T(1,128)S(1)}, u32[]{:S(2)}) copy-start(f32[1,192,512]{2,0,1:T(1,128)S(1)} %get-tuple-element.57) | copy-start | bytes 1179652
  62.5 3.6 %copy-start.1 = (bf16[512,1664]{1,0:T(8,128)(2,1)S(1)}, bf16[512,1664]{1,0:T(8,128)(2,1)}, u32[]{:S(2)}) copy-start(bf16[512,1664]{1,0:T(8,128)(2,1)} %param.14) | copy-start | bytes 5111812
  99.1 10.1 %collective-permute-start = (f32[1,16,29952]{2,0,1:T(1,128)}, f32[1,16,29952]{2,0,1:T(1,128)}, u32[]{:S(2)}, u32[]{:S(2)}) collective-permute-start(f32[1,16,29952]{2,0,1:T(1,128)} %dynamic-slice_bitcast_fusion), channel_id=1, source_target_pairs={{0,16},{16,0},{1,17},{17,1},{2,18},{18,2},{3,19},{19,3},{4,20},{20... | collective-permute-start | bytes 5750792 | tf_op jit(solution)/shard_map/ppermute | solution.py:43
  116.3 14.3 %collective-permute-start.1 = (f32[1,4,29952]{2,1,0:T(4,128)}, f32[1,4,29952]{2,1,0:T(4,128)}, u32[]{:S(2)}, u32[]{:S(2)}) collective-permute-start(f32[1,4,29952]{2,1,0:T(4,128)} %bitcast.123), channel_id=1, source_target_pairs={{0,32},{32,0},{64,96},{96,64},{1,33},{33,1},{65,97},{97,65},{2,34}... | collective-permute-start | bytes 1437704 | tf_op jit(solution)/shard_map/ppermute | solution.py:43
  119.1 21.0 %collective-permute-start.2 = (f32[1,4,29952]{2,1,0:T(4,128)}, f32[1,4,29952]{2,1,0:T(4,128)}, u32[]{:S(2)}, u32[]{:S(2)}) collective-permute-start(f32[1,4,29952]{2,1,0:T(4,128)} %bitcast.122), channel_id=1, source_target_pairs={{0,64},{32,96},{64,0},{96,32},{1,65},{33,97},{65,1},{97,33},{2,66}... | collective-permute-start | bytes 1437704 | tf_op jit(solution)/shard_map/ppermute | solution.py:43
  122.5 26.4 %collective-permute-start.3 = (f32[1,4,29952]{2,1,0:T(4,128)}, f32[1,4,29952]{2,1,0:T(4,128)}, u32[]{:S(2)}, u32[]{:S(2)}) collective-permute-start(f32[1,4,29952]{2,1,0:T(4,128)} %bitcast.121), channel_id=1, source_target_pairs={{0,96},{32,64},{64,32},{96,0},{1,97},{33,65},{65,33},{97,1},{2,98}... | collective-permute-start | bytes 1437704 | tf_op jit(solution)/shard_map/ppermute | solution.py:43
  150.6 0.8 copy-start.3
  152.4 10.9 %collective-permute-start.4 = (f32[1,1,29952]{2,1,0:T(1,128)}, f32[1,1,29952]{2,1,0:T(1,128)}, u32[]{:S(2)}, u32[]{:S(2)}) collective-permute-start(f32[1,1,29952]{2,1,0:T(1,128)} %get-tuple-element.54), channel_id=1, source_target_pairs={{0,128},{128,0},{256,384},{384,256},{1,129},{129,1},{257,385},{385... | collective-permute-start | bytes 359432 | tf_op jit(solution)/shard_map/ppermute | solution.py:43
  154.3 9.0 %collective-permute-start.5 = (f32[1,1,29952]{2,1,0:T(1,128)}, f32[1,1,29952]{2,1,0:T(1,128)}, u32[]{:S(2)}, u32[]{:S(2)}) collective-permute-start(f32[1,1,29952]{2,1,0:T(1,128)} %get-tuple-element.56), channel_id=1, source_target_pairs={{0,256},{128,384},{256,0},{384,128},{1,257},{129,385},{257,1},{385... | collective-permute-start | bytes 359432 | tf_op jit(solution)/shard_map/ppermute | solution.py:43
  156.9 7.9 %collective-permute-start.6 = (f32[1,1,29952]{2,1,0:T(1,128)S(1)}, f32[1,1,29952]{2,1,0:T(1,128)}, u32[]{:S(2)}, u32[]{:S(2)}) collective-permute-start(f32[1,1,29952]{2,1,0:T(1,128)S(1)} %get-tuple-element.55), channel_id=1, source_target_pairs={{0,384},{128,256},{256,128},{384,0},{1,385},{129,257},{257,129},{3... | collective-permute-start | bytes 359432 | tf_op jit(solution)/shard_map/ppermute | solution.py:43
  174.8 12.0 %copy-start.7 = (bf16[1,1,29952]{2,1,0:T(2,128)(2,1)}, bf16[1,1,29952]{2,1,0:T(2,128)(2,1)S(1)}, u32[]{:S(2)}) copy-start(bf16[1,1,29952]{2,1,0:T(2,128)(2,1)S(1)} %reshape.260) | copy-start | bytes 179716
  174.8 10.0 %collective-permute-start.7 = (bf16[1,1,29952]{2,1,0:T(2,128)(2,1)S(1)}, bf16[1,1,29952]{2,1,0:T(2,128)(2,1)}, u32[]{:S(2)}, u32[]{:S(2)}) collective-permute-start(bf16[1,1,29952]{2,1,0:T(2,128)(2,1)S(1)} %reshape.260), channel_id=1, source_target_pairs={{0,128},{128,0},{256,384},{384,256},{1,129},{129,1},{257,385},{385... | collective-permute-start | bytes 179720 | tf_op jit(solution)/shard_map/ppermute | solution.py:52
  178.6 8.3 %collective-permute-start.8 = (bf16[1,1,29952]{2,1,0:T(2,128)(2,1)S(1)}, bf16[1,1,29952]{2,1,0:T(2,128)(2,1)}, u32[]{:S(2)}, u32[]{:S(2)}) collective-permute-start(bf16[1,1,29952]{2,1,0:T(2,128)(2,1)S(1)} %reshape.260), channel_id=1, source_target_pairs={{0,256},{128,384},{256,0},{384,128},{1,257},{129,385},{257,1},{385... | collective-permute-start | bytes 179720 | tf_op jit(solution)/shard_map/ppermute | solution.py:52
  182.1 7.5 %collective-permute-start.9 = (bf16[1,1,29952]{2,1,0:T(2,128)(2,1)S(1)}, bf16[1,1,29952]{2,1,0:T(2,128)(2,1)}, u32[]{:S(2)}, u32[]{:S(2)}) collective-permute-start(bf16[1,1,29952]{2,1,0:T(2,128)(2,1)S(1)} %reshape.260), channel_id=1, source_target_pairs={{0,384},{128,256},{256,128},{384,0},{1,385},{129,257},{257,129},{3... | collective-permute-start | bytes 179720 | tf_op jit(solution)/shard_map/ppermute | solution.py:52
  191.3 0.6 copy-start.4
  191.3 1.9 copy-start.5
  191.3 3.8 %copy-start.6 = (bf16[1,1,1,29952]{3,2,1,0:T(2,128)(2,1)}, bf16[1,1,1,29952]{3,2,1,0:T(2,128)(2,1)S(1)}, u32[]{:S(2)}) copy-start(bf16[1,1,1,29952]{3,2,1,0:T(2,128)(2,1)S(1)} %get-tuple-element.53) | copy-start | bytes 179716
  193.2 9.6 %collective-permute-start.10 = (bf16[1,4,29952]{2,1,0:T(4,128)(2,1)}, bf16[1,4,29952]{2,1,0:T(4,128)(2,1)}, u32[]{:S(2)}, u32[]{:S(2)}) collective-permute-start(bf16[1,4,29952]{2,1,0:T(4,128)(2,1)} %maximum_bitcast_fusion.1), channel_id=1, source_target_pairs={{0,32},{32,0},{64,96},{96,64},{1,33},{33,1},{65,97},{97,65},{2,34}... | collective-permute-start | bytes 718856 | tf_op jit(solution)/shard_map/ppermute | solution.py:52
  195.1 10.2 %collective-permute-start.11 = (bf16[1,4,29952]{2,1,0:T(4,128)(2,1)}, bf16[1,4,29952]{2,1,0:T(4,128)(2,1)}, u32[]{:S(2)}, u32[]{:S(2)}) collective-permute-start(bf16[1,4,29952]{2,1,0:T(4,128)(2,1)} %maximum_bitcast_fusion.1), channel_id=1, source_target_pairs={{0,64},{32,96},{64,0},{96,32},{1,65},{33,97},{65,1},{97,33},{2,66}... | collective-permute-start | bytes 718856 | tf_op jit(solution)/shard_map/ppermute | solution.py:52
  200.4 11.0 %collective-permute-start.12 = (bf16[1,4,29952]{2,1,0:T(4,128)(2,1)}, bf16[1,4,29952]{2,1,0:T(4,128)(2,1)}, u32[]{:S(2)}, u32[]{:S(2)}) collective-permute-start(bf16[1,4,29952]{2,1,0:T(4,128)(2,1)} %maximum_bitcast_fusion.1), channel_id=1, source_target_pairs={{0,96},{32,64},{64,32},{96,0},{1,97},{33,65},{65,33},{97,1},{2,98}... | collective-permute-start | bytes 718856 | tf_op jit(solution)/shard_map/ppermute | solution.py:52
  218.5 8.1 %collective-permute-start.13 = (bf16[1,16,29952]{2,1,0:T(8,128)(2,1)}, bf16[1,16,29952]{2,1,0:T(8,128)(2,1)}, u32[]{:S(2)}, u32[]{:S(2)}) collective-permute-start(bf16[1,16,29952]{2,1,0:T(8,128)(2,1)} %reshape.262), channel_id=1, source_target_pairs={{0,16},{16,0},{1,17},{17,1},{2,18},{18,2},{3,19},{19,3},{4,20},{20... | collective-permute-start | bytes 2875400 | tf_op jit(solution)/shard_map/ppermute | solution.py:52
  250.4 36.8 %copy-start.8 = (bf16[12,512]{1,0:T(8,128)(2,1)S(1)}, bf16[12,512]{1,0:T(8,128)(2,1)}, u32[]{:S(2)}) copy-start(bf16[12,512]{1,0:T(8,128)(2,1)} %param.11) | copy-start | bytes 36868
  250.4 36.8 %copy-start.9 = (bf16[12,512]{1,0:T(8,128)(2,1)S(1)}, bf16[12,512]{1,0:T(8,128)(2,1)}, u32[]{:S(2)}) copy-start(bf16[12,512]{1,0:T(8,128)(2,1)} %param.10) | copy-start | bytes 36868
  250.8 9.3 %collective-permute-start.14 = (f32[4,13,512]{2,1,0:T(8,128)S(1)}, f32[4,13,512]{2,1,0:T(8,128)S(1)}, u32[]{:S(2)}, u32[]{:S(2)}) collective-permute-start(f32[4,13,512]{2,1,0:T(8,128)S(1)} %get-tuple-element.47), channel_id=1, source_target_pairs={{0,1},{1,0},{2,3},{3,2},{4,5},{5,4},{6,7},{7,6},{8,9},{9,8},{10,11... | collective-permute-start | bytes 319496 | tf_op jit(solution)/shard_map/ppermute | solution.py:26
  252.7 13.1 %collective-permute-start.15 = (f32[4,13,512]{2,1,0:T(8,128)S(1)}, f32[4,13,512]{2,1,0:T(8,128)S(1)}, u32[]{:S(2)}, u32[]{:S(2)}) collective-permute-start(f32[4,13,512]{2,1,0:T(8,128)S(1)} %get-tuple-element.48), channel_id=1, source_target_pairs={{0,2},{1,3},{2,0},{3,1},{4,6},{5,7},{6,4},{7,5},{8,10},{9,11},{10,... | collective-permute-start | bytes 319496 | tf_op jit(solution)/shard_map/ppermute | solution.py:26
  254.7 11.2 %collective-permute-start.16 = (f32[4,13,512]{2,1,0:T(8,128)S(1)}, f32[4,13,512]{2,1,0:T(8,128)S(1)}, u32[]{:S(2)}, u32[]{:S(2)}) collective-permute-start(f32[4,13,512]{2,1,0:T(8,128)S(1)} %get-tuple-element.49), channel_id=1, source_target_pairs={{0,3},{1,2},{2,1},{3,0},{4,7},{5,6},{6,5},{7,4},{8,11},{9,10},{10,... | collective-permute-start | bytes 319496 | tf_op jit(solution)/shard_map/ppermute | solution.py:26
  265.9 16.3 %collective-permute-start.17 = (f32[1,13,512]{2,1,0:T(8,128)S(1)}, f32[1,13,512]{2,1,0:T(8,128)S(1)}, u32[]{:S(2)}, u32[]{:S(2)}) collective-permute-start(f32[1,13,512]{2,1,0:T(8,128)S(1)} %get-tuple-element.59), channel_id=1, source_target_pairs={{0,4},{1,5},{2,6},{3,7},{4,0},{5,1},{6,2},{7,3},{8,12},{9,13},{10,... | collective-permute-start | bytes 79880 | tf_op jit(solution)/shard_map/ppermute | solution.py:26
  268.5 13.7 %collective-permute-start.18 = (f32[1,13,512]{2,1,0:T(8,128)S(1)}, f32[1,13,512]{2,1,0:T(8,128)S(1)}, u32[]{:S(2)}, u32[]{:S(2)}) collective-permute-start(f32[1,13,512]{2,1,0:T(8,128)S(1)} %get-tuple-element.61), channel_id=1, source_target_pairs={{0,8},{1,9},{2,10},{3,11},{4,12},{5,13},{6,14},{7,15},{8,0},{9,1},... | collective-permute-start | bytes 79880 | tf_op jit(solution)/shard_map/ppermute | solution.py:26
  278.1 9.0 %collective-permute-start.19 = (f32[1,13,512]{2,1,0:T(8,128)S(1)}, f32[1,13,512]{2,1,0:T(8,128)S(1)}, u32[]{:S(2)}, u32[]{:S(2)}) collective-permute-start(f32[1,13,512]{2,1,0:T(8,128)S(1)} %get-tuple-element.60), channel_id=1, source_target_pairs={{0,12},{1,13},{2,14},{3,15},{4,8},{5,9},{6,10},{7,11},{8,4},{9,5},... | collective-permute-start | bytes 79880 | tf_op jit(solution)/shard_map/ppermute | solution.py:26

commit v8 on v5

--- a/solution.py
+++ b/solution.py
@@ -44,11 +44,20 @@
     back_part = lax.dot_general(
         piece[1], w_down, (((1,), (1,)), ((), ())), preferred_element_type=jnp.float32
     )
-    summed = lax.psum(jnp.stack([gate_part, up_part, back_part]), WA)
-    gate, up, d_hidden = summed[0], summed[1], summed[2]
-
+    n_wa, width = lax.axis_size(WA), gate_part.shape[1]
+    partial = jnp.stack([gate_part, up_part, back_part]).reshape(3, n_wa, -1)
+    partial = partial.transpose(1, 0, 2).reshape(n_wa, -1, 128)
+    part = lax.psum_scatter(partial, WA, scatter_dimension=0, tiled=True).reshape(3, -1, width)
+    gate, up, d_hidden = part[0], part[1], part[2]
     d_gate, d_up = gate_grads(gate, up, d_hidden)
-    dot_part = jnp.sum(d_gate.astype(jnp.float32) * gate + d_up.astype(jnp.float32) * up, axis=1)
+    dot_rows = jnp.sum(d_gate.astype(jnp.float32) * gate + d_up.astype(jnp.float32) * up, axis=1)
+    dot_hi = dot_rows.astype(jnp.bfloat16)
+    dot_lo = (dot_rows - dot_hi.astype(jnp.float32)).astype(jnp.bfloat16)
+    extra = jnp.zeros_like(d_gate).at[:, 0].set(dot_hi).at[:, 1].set(dot_lo)
+    grads = lax.all_gather(jnp.stack([d_gate, d_up, extra]).reshape(1, -1, 128), WA, axis=0, tiled=True)
+    grads = grads.reshape(n_wa, 3, -1, width).transpose(1, 0, 2, 3).reshape(3, -1, width)
+    d_gate, d_up = grads[0], grads[1]
+    dot_part = grads[2][:, 0].astype(jnp.float32) + grads[2][:, 1].astype(jnp.float32)
     total = lax.dot_general(
         d_gate, w_gate, (((1,), (1,)), ((), ())), preferred_element_type=jnp.float32
     ) + lax.dot_general(

time: 267 us -> 339 us (1.27)
  local copies, waits for them, and re-layouts: 2.9 us -> 35.7 us
  waiting for transfers between devices: 149 us -> 171 us
  other arithmetic: 8.24 us -> 17.2 us
  matrix products: 5.11 us -> 12.8 us
    psum x1 -> x0, waiting for transfers between devices: 137 us -> none  [local(): summed = lax.psum(jnp.stack([gate_part, up_part, back_part]), WA)]
    reduce_scatter x0 -> x1, waiting for transfers between devices: none -> 97.3 us  [local(): lax.psum_scatter(partial, WA, scatter_dimension=0, tiled=True)]
    all_gather x0 -> x1, waiting for transfers between devices: none -> 60.4 us  [local(): lax.all_gather(jnp.stack([d_gate, d_up, extra]).reshape(1, -1, 128), WA,...]
    reshape x1 -> x3, local copies, waits for them, and re-layouts: 0.08 us -> 12.8 us  [the longest x1 7.29 us: local(): partial = partial.transpose(1, 0, 2).reshape(n_wa, -1, 128)]
    another operation x0 -> x6, local copies, waits for them, and re-layouts: none -> 10.7 us  [the longest x3 10.5 us: local(): partial = jnp.stack([gate_part, up_part, back_part]).reshape(3, n_wa, -1)]
    squeeze x0 -> x6, local copies, waits for them, and re-layouts: none -> 6.92 us  [the longest x2 4.15 us: local(): d_gate, d_up = (grads[0], grads[1])]
    transpose x0 -> x1, other arithmetic: none -> 6.72 us  [local(): partial = partial.transpose(1, 0, 2).reshape(n_wa, -1, 128)]
  transfers between devices with their start and end apart: 7 -> 8, of which waited for: 5 -> 6; matrix products, arithmetic and copies ran while one was open for 0% -> 0% of each run, Pallas kernels for 0% -> 0%
where the time goes in v8:
time: 339 us; the launch traced here: 335 us
  waiting for transfers between devices  171 us (50%)
  blocking collectives  58.5 us (17%)
  local copies, waits for them, and re-layouts  35.7 us (11%)
  starting transfers between devices  26.3 us (8%)
  other arithmetic  17.2 us (5%)
  between operations  13.7 us (4%)
  matrix products  12.8 us (4%)
    reduce_scatter x1, waiting for transfers between devices, local(): lax.psum_scatter(partial, WA, scatter_dimension=0, tiled=True)  97.3 us
    all_gather x1, waiting for transfers between devices, local(): lax.all_gather(jnp.stack([d_gate, d_up, extra]).reshape(1, -1, 128), WA,...  60.4 us
    all_gather x1, blocking collectives, local(): lax.all_gather(jnp.stack([residual_in, grad_out]), 'ha', axis=1, tiled=True)  31.1 us
    psum x3, blocking collectives, local(): squares = lax.psum(lax.psum(lax.psum(squares, 'core'), 'y'), 'x')  27.4 us
    ppermute x6, starting transfers between devices, scatter_sum(): lax.ppermute(send, axis, [(i, i ^ k << shift) for i in range(n)])  26.3 us
    ppermute x6, waiting for transfers between devices, scatter_sum(): lax.ppermute(send, axis, [(i, i ^ k << shift) for i in range(n)])  13.4 us
    another operation x3, local copies, waits for them, and re-layouts, local(): partial = jnp.stack([gate_part, up_part, back_part]).reshape(3, n_wa, -1)  10.5 us
    reshape x1, local copies, waits for them, and re-layouts, local(): partial = partial.transpose(1, 0, 2).reshape(n_wa, -1, 128)  7.29 us
  transfers between devices with their start and end apart: 8, of which 6 were waited for; matrix products, arithmetic and copies ran while one was open for 0% of the time, Pallas kernels for 0%

profile of v8, /device:TPU:1, one launch (start us, length us, event | category | flops | bytes accessed | tf_op | source)
XLA Modules:
  0.0 335.3 jit_solution(1222374439481091094)
XLA Ops:
  6.5 0.9 pad_maximum_fusion.1
  7.5 31.1 %all_gather.6 = bf16[2,192,512]{2,0,1:T(2,128)(2,1)S(1)} all-gather(bf16[2,12,512]{2,0,1:T(2,128)(2,1)S(1)} %copy.27), channel_id=1, replica_groups=mesh['x'=4,'y'=4,'core'=2,'ha'=16] {'ha'}, dimensions={1}, use_global_device_ids=true | all-gather | bytes 417792 | tf_op jit(solution)/shard_map/all_gather | solution.py:35
  38.5 1.3 slice_convert_fusion
  40.0 10.2 %psum.21 = f32[192]{0:T(256)S(1)} all-reduce(f32[192]{0:T(256)S(1)} %fusion), channel_id=1, replica_groups=mesh['x'=4,'y'=4,'core'=2,'ha'=16] {'core'}, use_global_device_ids=true, to_apply=%region_1.0 | all-reduce | flops 192 | bytes 1536 | tf_op jit(solution)/shard_map/psum | solution.py:38
  50.2 8.7 %psum.22 = f32[192]{0:T(256)S(1)} all-reduce(f32[192]{0:T(256)S(1)} %psum.21), channel_id=1, replica_groups=mesh['x'=4,'y'=4,'core'=2,'ha'=16] {'y'}, use_global_device_ids=true, to_apply=%region_2.0 | all-reduce | flops 192 | bytes 1536 | tf_op jit(solution)/shard_map/psum | solution.py:38
  58.9 8.5 %psum.23 = f32[192]{0:T(256)S(1)} all-reduce(f32[192]{0:T(256)S(1)} %psum.22), channel_id=1, replica_groups=mesh['x'=4,'y'=4,'core'=2,'ha'=16] {'x'}, use_global_device_ids=true, to_apply=%region_3.0 | all-reduce | flops 192 | bytes 1536 | tf_op jit(solution)/shard_map/psum | solution.py:38
  67.4 1.6 fusion.26
  69.0 3.6 %stack.41 = f32[1,32,9984]{2,0,1:T(1,128)} reshape(f32[192,1664]{1,0:T(8,128)} %fusion.26) | data formatting | bytes 2555904 | tf_op jit(solution)/shard_map/stack | solution.py:48
  72.6 2.6 fusion.24
  75.2 3.4 %stack.42 = f32[1,32,9984]{2,0,1:T(1,128)} reshape(f32[192,1664]{1,0:T(8,128)} %fusion.24) | data formatting | bytes 2555904 | tf_op jit(solution)/shard_map/stack | solution.py:48
  78.6 3.4 %fusion.3 = f32[192,1664]{1,0:T(8,128)} fusion(bf16[1664,512]{1,0:T(8,128)(2,1)} %param.15, bf16[1,192,512]{2,0,1:T(2,128)(2,1)} %get-tuple-element.38), kind=kOutput, calls=%fused_computation.17 | convolution fusion | flops 327155712 | bytes 3178496 | tf_op jit(solution)/shard_map/dot_general | solution.py:44
  82.0 3.5 %stack.43 = f32[1,32,9984]{2,0,1:T(1,128)} reshape(f32[192,1664]{1,0:T(8,128)} %fusion.3) | data formatting | bytes 2555904 | tf_op jit(solution)/shard_map/stack | solution.py:48
  85.5 6.7 %maximum_bitcast_fusion = f32[32,3,9984]{2,1,0:T(4,128)} fusion(f32[1,32,9984]{2,0,1:T(1,128)} %stack.43, f32[1,32,9984]{2,0,1:T(1,128)} %stack.42, f32[1,32,9984]{2,0,1:T(1,128)} %stack.41), kind=kLoop, calls=%fused_computation | loop fusion | flops 1916928 | bytes 7667712 | tf_op jit(solution)/shard_map/transpose | solution.py:49
  92.2 7.3 %reshape.247 = f32[32,234,128]{2,1,0:T(8,128)} reshape(f32[32,3,9984]{2,1,0:T(4,128)} %maximum_bitcast_fusion) | data formatting | bytes 7667712 | tf_op jit(solution)/shard_map/reshape | solution.py:49
  99.6 0.7 compare_reduce_fusion.1
  100.2 0.7 compare_reduce_fusion
  101.0 97.3 %reduce-scatter.2.cloned.1.call-done = f32[1,234,128]{2,1,0:T(8,128)} async-done(((f32[32,234,128]{2,1,0:T(8,128)}), f32[1,234,128]{2,1,0:T(8,128)}) %reduce-scatter.2.cloned.1.call-update) | async-done | bytes 119824 | tf_op jit(solution)/shard_map/reduce_scatter | solution.py:50
  198.3 2.1 fusion.29
  200.4 0.8 squeeze.56
  201.2 0.6 squeeze.57
  201.8 0.7 reduce_sum.29
  202.5 0.1 reduce_sum.30
  202.6 0.6 fusion.20
  203.4 0.6 broadcast_select_fusion
  204.1 1.5 multiply_convert_fusion.1
  205.7 0.8 pad_maximum_fusion
  206.5 0.7 reshape.249
  207.2 60.4 %all-gather.2.cloned.1.call-done = bf16[32,234,128]{2,1,0:T(8,128)(2,1)} async-done(((bf16[1,234,128]{2,1,0:T(8,128)(2,1)}), bf16[32,234,128]{2,1,0:T(8,128)(2,1)}) %all-gather.2.cloned.1.call-update) | async-done | bytes 1916944 | tf_op jit(solution)/shard_map/all_gather | solution.py:57
  267.6 4.8 %reshape.250 = bf16[32,3,6,1664]{3,2,1,0:T(8,128)(2,1)} reshape(bf16[32,234,128]{2,1,0:T(8,128)(2,1)} %all-gather.2.cloned.1.call-done) | data formatting | bytes 3833856 | tf_op jit(solution)/shard_map/reshape | solution.py:58
  272.4 3.2 fusion.28
  275.7 2.1 squeeze.58
  277.7 2.6 fusion.30
  280.3 2.1 squeeze.59
  282.4 2.7 convolution_add_fusion
  285.0 1.0 concatenate.13
  286.1 1.4 squeeze.60
  287.5 0.2 add_reduce_fusion
  287.9 3.2 collective-permute-start
  291.1 4.2 %collective-permute-start.1 = (f32[4,13,512]{2,1,0:T(8,128)S(1)}, f32[4,13,512]{2,1,0:T(8,128)S(1)}, u32[]{:S(2)}, u32[]{:S(2)}) collective-permute-start(f32[4,13,512]{2,1,0:T(8,128)S(1)} %get-tuple-element.35), channel_id=1, source_target_pairs={{0,2},{1,3},{2,0},{3,1},{4,6},{5,7},{6,4},{7,5},{8,10},{9,11},{10,... | collective-permute-start | bytes 319496 | tf_op jit(solution)/shard_map/ppermute | solution.py:26
  295.2 1.9 collective-permute-start.2
  297.2 4.4 %collective-permute-done.1 = f32[4,13,512]{2,1,0:T(8,128)S(1)} collective-permute-done((f32[4,13,512]{2,1,0:T(8,128)S(1)}, f32[4,13,512]{2,1,0:T(8,128)S(1)}, u32[]{:S(2)}, u32[]{:S(2)}) %collective-permute-start.1) | collective-permute-done | bytes 106528 | tf_op jit(solution)/shard_map/ppermute | solution.py:26
  301.6 1.6 collective-permute-done.2
  303.3 7.4 %collective-permute-start.3 = (f32[1,13,512]{2,1,0:T(8,128)S(1)}, f32[1,13,512]{2,1,0:T(8,128)S(1)}, u32[]{:S(2)}, u32[]{:S(2)}) collective-permute-start(f32[1,13,512]{2,1,0:T(8,128)S(1)} %get-tuple-element.39), channel_id=1, source_target_pairs={{0,4},{1,5},{2,6},{3,7},{4,0},{5,1},{6,2},{7,3},{8,12},{9,13},{10,... | collective-permute-start | bytes 79880 | tf_op jit(solution)/shard_map/ppermute | solution.py:26
  310.7 7.7 %collective-permute-start.4 = (f32[1,13,512]{2,1,0:T(8,128)S(1)}, f32[1,13,512]{2,1,0:T(8,128)S(1)}, u32[]{:S(2)}, u32[]{:S(2)}) collective-permute-start(f32[1,13,512]{2,1,0:T(8,128)S(1)} %get-tuple-element.41), channel_id=1, source_target_pairs={{0,8},{1,9},{2,10},{3,11},{4,12},{5,13},{6,14},{7,15},{8,0},{9,1},... | collective-permute-start | bytes 79880 | tf_op jit(solution)/shard_map/ppermute | solution.py:26
  318.4 1.9 collective-permute-start.5
  320.4 3.7 %collective-permute-done.4 = f32[1,13,512]{2,1,0:T(8,128)S(1)} collective-permute-done((f32[1,13,512]{2,1,0:T(8,128)S(1)}, f32[1,13,512]{2,1,0:T(8,128)S(1)}, u32[]{:S(2)}, u32[]{:S(2)}) %collective-permute-start.4) | collective-permute-done | bytes 26656 | tf_op jit(solution)/shard_map/ppermute | solution.py:26
  324.1 3.6 %collective-permute-done.5 = f32[1,13,512]{2,1,0:T(8,128)S(1)} collective-permute-done((f32[1,13,512]{2,1,0:T(8,128)S(1)}, f32[1,13,512]{2,1,0:T(8,128)S(1)}, u32[]{:S(2)}, u32[]{:S(2)}) %collective-permute-start.5) | collective-permute-done | bytes 26656 | tf_op jit(solution)/shard_map/ppermute | solution.py:26
  327.8 0.7 fusion.19
  (44 shorter events, 1.0 us)
Async XLA Ops:
  6.5 60.8 %copy-start = (bf16[512,1664]{1,0:T(8,128)(2,1)S(1)}, bf16[512,1664]{1,0:T(8,128)(2,1)}, u32[]{:S(2)}) copy-start(bf16[512,1664]{1,0:T(8,128)(2,1)} %param.13) | copy-start | bytes 5111812
  6.5 60.8 %copy-start.9 = (bf16[512]{0:T(512)(128)(2,1)S(1)}, bf16[512]{0:T(512)(128)(2,1)}, u32[]{:S(2)}) copy-start(bf16[512]{0:T(512)(128)(2,1)} %param.12) | copy-start | bytes 3076
  6.5 191.7 %reduce-scatter.2.cloned.1.call-start = ((), (), s32[]{:S(2)}) async-start(), calls=%async_computation.1 | async-start | bytes 4055040 | tf_op jit(solution)/shard_map/reduce_scatter | solution.py:50
  39.8 27.5 %copy-start.2 = (f32[1,192,512]{2,0,1:T(1,128)}, f32[1,192,512]{2,0,1:T(1,128)S(1)}, u32[]{:S(2)}) copy-start(f32[1,192,512]{2,0,1:T(1,128)S(1)} %get-tuple-element.37) | copy-start | bytes 1179652
  67.3 5.2 %copy-start.7 = (f32[192]{0:T(256)}, f32[192]{0:T(256)S(1)}, u32[]{:S(2)}) copy-start(f32[192]{0:T(256)S(1)} %add_rsqrt_fusion) | copy-start | bytes 2308
  67.4 5.2 %copy-start.5 = (f32[512]{0:T(512)}, f32[512]{0:T(512)S(1)}, u32[]{:S(2)}) copy-start(f32[512]{0:T(512)S(1)} %convert_element_type.116) | copy-start | bytes 6148
  69.0 3.6 %copy-start.1 = (bf16[512,1664]{1,0:T(8,128)(2,1)S(1)}, bf16[512,1664]{1,0:T(8,128)(2,1)}, u32[]{:S(2)}) copy-start(bf16[512,1664]{1,0:T(8,128)(2,1)} %param.14) | copy-start | bytes 5111812
  99.5 168.1 %all-gather.2.cloned.1.call-start = ((), (), s32[]{:S(2)}) async-start(), calls=%async_computation.2 | async-start | bytes 2027520 | tf_op jit(solution)/shard_map/all_gather | solution.py:57
  286.1 34.2 %copy-start.8 = (f32[192]{0:T(256)S(1)}, f32[192]{0:T(256)}, u32[]{:S(2)}) copy-start(f32[192]{0:T(256)} %copy-done.7) | copy-start | bytes 2308
  287.4 40.3 %copy-start.3 = (bf16[12,512]{1,0:T(8,128)(2,1)S(1)}, bf16[12,512]{1,0:T(8,128)(2,1)}, u32[]{:S(2)}) copy-start(bf16[12,512]{1,0:T(8,128)(2,1)} %param.11) | copy-start | bytes 36868
  287.4 40.3 %copy-start.4 = (bf16[12,512]{1,0:T(8,128)(2,1)S(1)}, bf16[12,512]{1,0:T(8,128)(2,1)}, u32[]{:S(2)}) copy-start(bf16[12,512]{1,0:T(8,128)(2,1)} %param.10) | copy-start | bytes 36868
  287.5 40.3 %copy-start.6 = (f32[512]{0:T(512)S(1)}, f32[512]{0:T(512)}, u32[]{:S(2)}) copy-start(f32[512]{0:T(512)} %copy-done.5) | copy-start | bytes 6148
  287.9 9.3 %collective-permute-start = (f32[4,13,512]{2,1,0:T(8,128)S(1)}, f32[4,13,512]{2,1,0:T(8,128)S(1)}, u32[]{:S(2)}, u32[]{:S(2)}) collective-permute-start(f32[4,13,512]{2,1,0:T(8,128)S(1)} %get-tuple-element.34), channel_id=1, source_target_pairs={{0,1},{1,0},{2,3},{3,2},{4,5},{5,4},{6,7},{7,6},{8,9},{9,8},{10,11... | collective-permute-start | bytes 319496 | tf_op jit(solution)/shard_map/ppermute | solution.py:26
  291.1 10.6 %collective-permute-start.1 = (f32[4,13,512]{2,1,0:T(8,128)S(1)}, f32[4,13,512]{2,1,0:T(8,128)S(1)}, u32[]{:S(2)}, u32[]{:S(2)}) collective-permute-start(f32[4,13,512]{2,1,0:T(8,128)S(1)} %get-tuple-element.35), channel_id=1, source_target_pairs={{0,2},{1,3},{2,0},{3,1},{4,6},{5,7},{6,4},{7,5},{8,10},{9,11},{10,... | collective-permute-start | bytes 319496 | tf_op jit(solution)/shard_map/ppermute | solution.py:26
  295.2 8.0 %collective-permute-start.2 = (f32[4,13,512]{2,1,0:T(8,128)S(1)}, f32[4,13,512]{2,1,0:T(8,128)S(1)}, u32[]{:S(2)}, u32[]{:S(2)}) collective-permute-start(f32[4,13,512]{2,1,0:T(8,128)S(1)} %get-tuple-element.36), channel_id=1, source_target_pairs={{0,3},{1,2},{2,1},{3,0},{4,7},{5,6},{6,5},{7,4},{8,11},{9,10},{10,... | collective-permute-start | bytes 319496 | tf_op jit(solution)/shard_map/ppermute | solution.py:26
  303.3 17.1 %collective-permute-start.3 = (f32[1,13,512]{2,1,0:T(8,128)S(1)}, f32[1,13,512]{2,1,0:T(8,128)S(1)}, u32[]{:S(2)}, u32[]{:S(2)}) collective-permute-start(f32[1,13,512]{2,1,0:T(8,128)S(1)} %get-tuple-element.39), channel_id=1, source_target_pairs={{0,4},{1,5},{2,6},{3,7},{4,0},{5,1},{6,2},{7,3},{8,12},{9,13},{10,... | collective-permute-start | bytes 79880 | tf_op jit(solution)/shard_map/ppermute | solution.py:26
  310.7 13.5 %collective-permute-start.4 = (f32[1,13,512]{2,1,0:T(8,128)S(1)}, f32[1,13,512]{2,1,0:T(8,128)S(1)}, u32[]{:S(2)}, u32[]{:S(2)}) collective-permute-start(f32[1,13,512]{2,1,0:T(8,128)S(1)} %get-tuple-element.41), channel_id=1, source_target_pairs={{0,8},{1,9},{2,10},{3,11},{4,12},{5,13},{6,14},{7,15},{8,0},{9,1},... | collective-permute-start | bytes 79880 | tf_op jit(solution)/shard_map/ppermute | solution.py:26
  318.4 9.4 %collective-permute-start.5 = (f32[1,13,512]{2,1,0:T(8,128)S(1)}, f32[1,13,512]{2,1,0:T(8,128)S(1)}, u32[]{:S(2)}, u32[]{:S(2)}) collective-permute-start(f32[1,13,512]{2,1,0:T(8,128)S(1)} %get-tuple-element.40), channel_id=1, source_target_pairs={{0,12},{1,13},{2,14},{3,15},{4,8},{5,9},{6,10},{7,11},{8,4},{9,5},... | collective-permute-start | bytes 79880 | tf_op jit(solution)/shard_map/ppermute | solution.py:26
Sparse Core Ops, SparseCore 0:
  99.7 98.5 reduce-scatter.1
  207.3 60.2 all-gather.1

commit v9 on v5

--- a/solution.py
+++ b/solution.py
@@ -28,11 +28,27 @@
     return x[0]
 
 
+def gather_rows(x, axis):
+    n = lax.axis_size(axis)
+    held = x[:, None]
+    for shift in reversed(range(0, n.bit_length() - 1, 2)):
+        mine = (lax.axis_index(axis) >> shift) & 3
+        got = [held] + [lax.ppermute(held, axis, [(i, i ^ (k << shift)) for i in range(n)]) for k in (1, 2, 3)]
+        placed = []
+        for d in range(4):
+            pick = got[3]
+            for k in (2, 1, 0):
+                pick = jnp.where((mine ^ d) == k, got[k], pick)
+            placed.append(pick)
+        held = jnp.stack(placed, axis=2).reshape(x.shape[0], -1, *x.shape[1:])
+    return held.reshape(x.shape[0], n * x.shape[1], x.shape[2])
+
+
 def local(residual_in, grad_out, norm_gain, w_gate, w_up, w_down):
     rows = residual_in.shape[0]
     gain_f = norm_gain.astype(jnp.float32)
 
-    piece = lax.all_gather(jnp.stack([residual_in, grad_out]), "ha", axis=1, tiled=True)
+    piece = gather_rows(jnp.stack([residual_in, grad_out]), "ha")
     stream_all = piece[0].astype(jnp.float32)
     squares = jnp.sum(stream_all * stream_all, axis=1)
     squares = lax.psum(lax.psum(lax.psum(squares, "core"), "y"), "x")

time: 267 us -> 290 us (1.086)
  blocking collectives: 58.6 us -> 21.5 us
  starting transfers between devices: 26.6 us -> 58.1 us
  waiting for transfers between devices: 149 us -> 166 us
  local copies, waits for them, and re-layouts: 2.9 us -> 9.33 us
  other arithmetic: 8.24 us -> 11.4 us
    ppermute x0 -> x6, starting transfers between devices: none -> 31.5 us  [gather_rows(): lax.ppermute(held, axis, [(i, i ^ k << shift) for i in range(n)])]
    all_gather x1 -> x0, blocking collectives: 31.2 us -> none  [local(): lax.all_gather(jnp.stack([residual_in, grad_out]), 'ha', axis=1, tiled=True)]
    ppermute x0 -> x6, waiting for transfers between devices: none -> 11.5 us  [gather_rows(): lax.ppermute(held, axis, [(i, i ^ k << shift) for i in range(n)])]
    psum x3, blocking collectives: 27.4 us -> 21.5 us  [local(): squares = lax.psum(lax.psum(lax.psum(squares, 'core'), 'y'), 'x')]
    ppermute x6, waiting for transfers between devices: 12.6 us -> 16.7 us  [scatter_sum(): lax.ppermute(send, axis, [(i, i ^ k << shift) for i in range(n)])]
    convert_element_type x0 -> x2, local copies, waits for them, and re-layouts: none -> 3.83 us  [local(): stream_all = piece[0].astype(jnp.float32)]
  transfers between devices with their start and end apart: 7 -> 13, of which waited for: 5 -> 6; matrix products, arithmetic and copies ran while one was open for 0% -> 0% of each run, Pallas kernels for 0% -> 0%
where the time goes in v9:
time: 290 us; the launch traced here: 286 us
  waiting for transfers between devices  166 us (57%)
  starting transfers between devices  58.1 us (20%)
  blocking collectives  21.5 us (7%)
  between operations  13.8 us (5%)
  other arithmetic  11.4 us (4%)
  local copies, waits for them, and re-layouts  9.33 us (3%)
  matrix products  6.25 us (2%)
    psum x1, waiting for transfers between devices, local(): summed = lax.psum(jnp.stack([gate_part, up_part, back_part]), WA)  137 us
    ppermute x6, starting transfers between devices, gather_rows(): lax.ppermute(held, axis, [(i, i ^ k << shift) for i in range(n)])  31.5 us
    ppermute x6, starting transfers between devices, scatter_sum(): lax.ppermute(send, axis, [(i, i ^ k << shift) for i in range(n)])  26.6 us
    psum x3, blocking collectives, local(): squares = lax.psum(lax.psum(lax.psum(squares, 'core'), 'y'), 'x')  21.5 us
    ppermute x6, waiting for transfers between devices, scatter_sum(): lax.ppermute(send, axis, [(i, i ^ k << shift) for i in range(n)])  16.7 us
    ppermute x6, waiting for transfers between devices, gather_rows(): lax.ppermute(held, axis, [(i, i ^ k << shift) for i in range(n)])  11.5 us
  transfers between devices with their start and end apart: 13, of which 6 were waited for; matrix products, arithmetic and copies ran while one was open for 0% of the time, Pallas kernels for 0%

profile of v9, /device:TPU:1, one launch (start us, length us, event | category | flops | bytes accessed | tf_op | source)
XLA Modules:
  0.0 286.0 jit_solution(1346755035861624785)
XLA Ops:
  6.5 0.9 maximum_bitcast_fusion.1
  7.4 13.3 %collective-permute-start.2 = (bf16[2,1,12,512]{3,2,0,1:T(8,128)(2,1)S(1)}, bf16[2,1,12,512]{3,2,0,1:T(8,128)(2,1)S(1)}, u32[]{:S(2)}, u32[]{:S(2)}) collective-permute-start(bf16[2,1,12,512]{3,2,0,1:T(8,128)(2,1)S(1)} %maximum_bitcast_fusion.1), channel_id=1, source_target_pairs={{0,12},{1,13},{2,14},{3,15},{4,8},{5,9},{6,10},{7,11},{8,4},{9,5},... | collective-permute-start | bytes 73736 | tf_op jit(solution)/shard_map/ppermute | solution.py:36
  20.7 4.9 %collective-permute-start.1 = (bf16[2,1,12,512]{3,2,0,1:T(8,128)(2,1)S(1)}, bf16[2,1,12,512]{3,2,0,1:T(8,128)(2,1)S(1)}, u32[]{:S(2)}, u32[]{:S(2)}) collective-permute-start(bf16[2,1,12,512]{3,2,0,1:T(8,128)(2,1)S(1)} %maximum_bitcast_fusion.1), channel_id=1, source_target_pairs={{0,8},{1,9},{2,10},{3,11},{4,12},{5,13},{6,14},{7,15},{8,0},{9,1},... | collective-permute-start | bytes 73736 | tf_op jit(solution)/shard_map/ppermute | solution.py:36
  25.6 4.0 %collective-permute-start = (bf16[2,1,12,512]{3,2,0,1:T(8,128)(2,1)S(1)}, bf16[2,1,12,512]{3,2,0,1:T(8,128)(2,1)S(1)}, u32[]{:S(2)}, u32[]{:S(2)}) collective-permute-start(bf16[2,1,12,512]{3,2,0,1:T(8,128)(2,1)S(1)} %maximum_bitcast_fusion.1), channel_id=1, source_target_pairs={{0,4},{1,5},{2,6},{3,7},{4,0},{5,1},{6,2},{7,3},{8,12},{9,13},{10,... | collective-permute-start | bytes 73736 | tf_op jit(solution)/shard_map/ppermute | solution.py:36
  29.7 4.8 %collective-permute-done.1 = bf16[2,1,12,512]{3,2,0,1:T(8,128)(2,1)S(1)} collective-permute-done((bf16[2,1,12,512]{3,2,0,1:T(8,128)(2,1)S(1)}, bf16[2,1,12,512]{3,2,0,1:T(8,128)(2,1)S(1)}, u32[]{:S(2)}, u32[]{:S(2)}) %collective-permute-start.1) | collective-permute-done | bytes 24608 | tf_op jit(solution)/shard_map/ppermute | solution.py:36
  34.5 0.7 select_bitcast_fusion.6
  35.3 0.8 select_bitcast_fusion.7
  36.1 4.8 %collective-permute-start.5 = (bf16[2,4,12,512]{3,2,0,1:T(8,128)(2,1)S(1)}, bf16[2,4,12,512]{3,2,0,1:T(8,128)(2,1)S(1)}, u32[]{:S(2)}, u32[]{:S(2)}) collective-permute-start(bf16[2,4,12,512]{3,2,0,1:T(8,128)(2,1)S(1)} %maximum_bitcast_fusion), channel_id=1, source_target_pairs={{0,3},{1,2},{2,1},{3,0},{4,7},{5,6},{6,5},{7,4},{8,11},{9,10},{10,... | collective-permute-start | bytes 294920 | tf_op jit(solution)/shard_map/ppermute | solution.py:36
  40.9 1.9 collective-permute-start.4
  42.8 2.5 collective-permute-start.3
  45.4 0.7 convert_element_type.42
  46.1 6.6 %collective-permute-done.4 = bf16[2,4,12,512]{3,2,0,1:T(8,128)(2,1)S(1)} collective-permute-done((bf16[2,4,12,512]{3,2,0,1:T(8,128)(2,1)S(1)}, bf16[2,4,12,512]{3,2,0,1:T(8,128)(2,1)S(1)}, u32[]{:S(2)}, u32[]{:S(2)}) %collective-permute-start.4) | collective-permute-done | bytes 98336 | tf_op jit(solution)/shard_map/ppermute | solution.py:36
  52.7 0.1 select_bitcast_fusion.2
  52.8 0.1 select_bitcast_fusion.3
  52.8 0.1 pad_maximum_fusion.1
  52.9 0.1 multiply_reduce_fusion
  53.1 1.0 slice_convert_fusion
  54.0 0.1 reduce_sum.21
  54.1 4.3 %psum.28 = f32[192]{0:T(256)S(1)} all-reduce(f32[192]{0:T(256)S(1)} %reduce_sum.21), channel_id=1, replica_groups=mesh['x'=4,'y'=4,'core'=2,'ha'=16] {'core'}, use_global_device_ids=true, to_apply=%region_1.2 | all-reduce | flops 192 | bytes 1536 | tf_op jit(solution)/shard_map/psum | solution.py:54
  58.5 8.7 %psum.29 = f32[192]{0:T(256)S(1)} all-reduce(f32[192]{0:T(256)S(1)} %psum.28), channel_id=1, replica_groups=mesh['x'=4,'y'=4,'core'=2,'ha'=16] {'y'}, use_global_device_ids=true, to_apply=%region_2.3 | all-reduce | flops 192 | bytes 1536 | tf_op jit(solution)/shard_map/psum | solution.py:54
  67.2 8.5 %psum.30 = f32[192]{0:T(256)S(1)} all-reduce(f32[192]{0:T(256)S(1)} %psum.29), channel_id=1, replica_groups=mesh['x'=4,'y'=4,'core'=2,'ha'=16] {'x'}, use_global_device_ids=true, to_apply=%region_3.4 | all-reduce | flops 192 | bytes 1536 | tf_op jit(solution)/shard_map/psum | solution.py:54
  75.6 2.0 copy.12
  77.6 1.8 reshape.40
  79.5 1.7 copy.13
  81.1 1.7 squeeze.42
  82.8 1.6 convolution_bitcast_fusion.1
  84.5 0.6 convolution_bitcast_fusion.2
  85.1 0.9 copy-done.4
  85.9 0.7 convolution_bitcast_fusion
  86.6 2.1 pad_maximum_fusion
  88.8 137.4 %all-reduce.3.cloned.1.call-done = f32[3,192,1664]{2,1,0:T(8,128)} async-done(((f32[3,192,1664]{2,1,0:T(8,128)}), f32[3,192,1664]{2,1,0:T(8,128)}) %all-reduce.3.cloned.1.call-update) | async-done | bytes 3833872 | tf_op jit(solution)/shard_map/psum | solution.py:63
  226.2 4.0 %add_reduce_fusion = (f32[192]{0:T(256)S(1)}, bf16[192,1664]{1,0:T(8,128)(2,1)}, bf16[192,1664]{1,0:T(8,128)(2,1)}) fusion(f32[3,192,1664]{2,1,0:T(8,128)} %all-reduce.3.cloned.1.call-done), kind=kLoop, calls=%fused_computation.7 | loop fusion | flops 6070080 | bytes 5112576 | tf_op jit(solution)/shard_map/reduce_sum | solution.py:67
  230.2 0.1 reshape.39
  230.3 1.9 fusion.17
  232.2 1.5 convolution_add_fusion
  233.7 1.0 concatenate.8
  234.7 0.1 fusion.8
  234.8 3.2 %collective-permute-start.6 = (f32[4,13,512]{2,1,0:T(8,128)S(1)}, f32[4,13,512]{2,1,0:T(8,128)S(1)}, u32[]{:S(2)}, u32[]{:S(2)}) collective-permute-start(f32[4,13,512]{2,1,0:T(8,128)S(1)} %get-tuple-element.10), channel_id=1, source_target_pairs={{0,1},{1,0},{2,3},{3,2},{4,5},{5,4},{6,7},{7,6},{8,9},{9,8},{10,11... | collective-permute-start | bytes 319496 | tf_op jit(solution)/shard_map/ppermute | solution.py:26
  238.0 4.2 %collective-permute-start.7 = (f32[4,13,512]{2,1,0:T(8,128)S(1)}, f32[4,13,512]{2,1,0:T(8,128)S(1)}, u32[]{:S(2)}, u32[]{:S(2)}) collective-permute-start(f32[4,13,512]{2,1,0:T(8,128)S(1)} %get-tuple-element.11), channel_id=1, source_target_pairs={{0,2},{1,3},{2,0},{3,1},{4,6},{5,7},{6,4},{7,5},{8,10},{9,11},{10,... | collective-permute-start | bytes 319496 | tf_op jit(solution)/shard_map/ppermute | solution.py:26
  242.2 1.9 collective-permute-start.8
  244.1 4.3 %collective-permute-done.7 = f32[4,13,512]{2,1,0:T(8,128)S(1)} collective-permute-done((f32[4,13,512]{2,1,0:T(8,128)S(1)}, f32[4,13,512]{2,1,0:T(8,128)S(1)}, u32[]{:S(2)}, u32[]{:S(2)}) %collective-permute-start.7) | collective-permute-done | bytes 106528 | tf_op jit(solution)/shard_map/ppermute | solution.py:26
  248.5 1.3 collective-permute-done.8
  249.9 7.4 %collective-permute-start.9 = (f32[1,13,512]{2,1,0:T(8,128)S(1)}, f32[1,13,512]{2,1,0:T(8,128)S(1)}, u32[]{:S(2)}, u32[]{:S(2)}) collective-permute-start(f32[1,13,512]{2,1,0:T(8,128)S(1)} %get-tuple-element.19), channel_id=1, source_target_pairs={{0,4},{1,5},{2,6},{3,7},{4,0},{5,1},{6,2},{7,3},{8,12},{9,13},{10,... | collective-permute-start | bytes 79880 | tf_op jit(solution)/shard_map/ppermute | solution.py:26
  257.2 7.7 %collective-permute-start.11 = (f32[1,13,512]{2,1,0:T(8,128)S(1)}, f32[1,13,512]{2,1,0:T(8,128)S(1)}, u32[]{:S(2)}, u32[]{:S(2)}) collective-permute-start(f32[1,13,512]{2,1,0:T(8,128)S(1)} %get-tuple-element.20), channel_id=1, source_target_pairs={{0,12},{1,13},{2,14},{3,15},{4,8},{5,9},{6,10},{7,11},{8,4},{9,5},... | collective-permute-start | bytes 79880 | tf_op jit(solution)/shard_map/ppermute | solution.py:26
  264.9 2.3 collective-permute-start.10
  267.2 0.1 multiply_multiply_fusion
  267.3 11.1 %collective-permute-done.10 = f32[1,13,512]{2,1,0:T(8,128)S(1)} collective-permute-done((f32[1,13,512]{2,1,0:T(8,128)S(1)}, f32[1,13,512]{2,1,0:T(8,128)S(1)}, u32[]{:S(2)}, u32[]{:S(2)}) %collective-permute-start.10) | collective-permute-done | bytes 26656 | tf_op jit(solution)/shard_map/ppermute | solution.py:26
  278.4 0.7 fusion.15
  (33 shorter events, 0.2 us)
Async XLA Ops:
  6.5 77.9 %copy-start = (bf16[512,1664]{1,0:T(8,128)(2,1)S(1)}, bf16[512,1664]{1,0:T(8,128)(2,1)}, u32[]{:S(2)}) copy-start(bf16[512,1664]{1,0:T(8,128)(2,1)} %param.9) | copy-start | bytes 5111812
  6.5 219.7 %all-reduce.3.cloned.1.call-start = ((), (), s32[]{:S(2)}) async-start(), calls=%async_computation | async-start | bytes 7667712 | tf_op jit(solution)/shard_map/psum | solution.py:63
  7.4 22.2 %collective-permute-start.2 = (bf16[2,1,12,512]{3,2,0,1:T(8,128)(2,1)S(1)}, bf16[2,1,12,512]{3,2,0,1:T(8,128)(2,1)S(1)}, u32[]{:S(2)}, u32[]{:S(2)}) collective-permute-start(bf16[2,1,12,512]{3,2,0,1:T(8,128)(2,1)S(1)} %maximum_bitcast_fusion.1), channel_id=1, source_target_pairs={{0,12},{1,13},{2,14},{3,15},{4,8},{5,9},{6,10},{7,11},{8,4},{9,5},... | collective-permute-start | bytes 73736 | tf_op jit(solution)/shard_map/ppermute | solution.py:36
  20.7 13.8 %collective-permute-start.1 = (bf16[2,1,12,512]{3,2,0,1:T(8,128)(2,1)S(1)}, bf16[2,1,12,512]{3,2,0,1:T(8,128)(2,1)S(1)}, u32[]{:S(2)}, u32[]{:S(2)}) collective-permute-start(bf16[2,1,12,512]{3,2,0,1:T(8,128)(2,1)S(1)} %maximum_bitcast_fusion.1), channel_id=1, source_target_pairs={{0,8},{1,9},{2,10},{3,11},{4,12},{5,13},{6,14},{7,15},{8,0},{9,1},... | collective-permute-start | bytes 73736 | tf_op jit(solution)/shard_map/ppermute | solution.py:36
  25.6 8.9 %collective-permute-start = (bf16[2,1,12,512]{3,2,0,1:T(8,128)(2,1)S(1)}, bf16[2,1,12,512]{3,2,0,1:T(8,128)(2,1)S(1)}, u32[]{:S(2)}, u32[]{:S(2)}) collective-permute-start(bf16[2,1,12,512]{3,2,0,1:T(8,128)(2,1)S(1)} %maximum_bitcast_fusion.1), channel_id=1, source_target_pairs={{0,4},{1,5},{2,6},{3,7},{4,0},{5,1},{6,2},{7,3},{8,12},{9,13},{10,... | collective-permute-start | bytes 73736 | tf_op jit(solution)/shard_map/ppermute | solution.py:36
  36.1 10.0 %collective-permute-start.5 = (bf16[2,4,12,512]{3,2,0,1:T(8,128)(2,1)S(1)}, bf16[2,4,12,512]{3,2,0,1:T(8,128)(2,1)S(1)}, u32[]{:S(2)}, u32[]{:S(2)}) collective-permute-start(bf16[2,4,12,512]{3,2,0,1:T(8,128)(2,1)S(1)} %maximum_bitcast_fusion), channel_id=1, source_target_pairs={{0,3},{1,2},{2,1},{3,0},{4,7},{5,6},{6,5},{7,4},{8,11},{9,10},{10,... | collective-permute-start | bytes 294920 | tf_op jit(solution)/shard_map/ppermute | solution.py:36
  40.9 11.8 %collective-permute-start.4 = (bf16[2,4,12,512]{3,2,0,1:T(8,128)(2,1)S(1)}, bf16[2,4,12,512]{3,2,0,1:T(8,128)(2,1)S(1)}, u32[]{:S(2)}, u32[]{:S(2)}) collective-permute-start(bf16[2,4,12,512]{3,2,0,1:T(8,128)(2,1)S(1)} %maximum_bitcast_fusion), channel_id=1, source_target_pairs={{0,2},{1,3},{2,0},{3,1},{4,6},{5,7},{6,4},{7,5},{8,10},{9,11},{10,... | collective-permute-start | bytes 294920 | tf_op jit(solution)/shard_map/ppermute | solution.py:36
  42.8 9.9 %collective-permute-start.3 = (bf16[2,4,12,512]{3,2,0,1:T(8,128)(2,1)S(1)}, bf16[2,4,12,512]{3,2,0,1:T(8,128)(2,1)S(1)}, u32[]{:S(2)}, u32[]{:S(2)}) collective-permute-start(bf16[2,4,12,512]{3,2,0,1:T(8,128)(2,1)S(1)} %maximum_bitcast_fusion), channel_id=1, source_target_pairs={{0,1},{1,0},{2,3},{3,2},{4,5},{5,4},{6,7},{7,6},{8,9},{9,8},{10,11... | collective-permute-start | bytes 294920 | tf_op jit(solution)/shard_map/ppermute | solution.py:36
  75.6 7.2 %copy-start.1 = (bf16[512,1664]{1,0:T(8,128)(2,1)S(1)}, bf16[512,1664]{1,0:T(8,128)(2,1)}, u32[]{:S(2)}) copy-start(bf16[512,1664]{1,0:T(8,128)(2,1)} %param.10) | copy-start | bytes 5111812
  82.8 1.7 copy-start.2
  84.4 1.5 copy-start.4
  84.5 1.4 copy-start.5
  230.3 1.9 copy-start.3
  234.7 43.7 %copy-start.6 = (bf16[12,512]{1,0:T(8,128)(2,1)S(1)}, bf16[12,512]{1,0:T(8,128)(2,1)}, u32[]{:S(2)}) copy-start(bf16[12,512]{1,0:T(8,128)(2,1)} %param.7) | copy-start | bytes 36868
  234.7 43.7 %copy-start.7 = (bf16[12,512]{1,0:T(8,128)(2,1)S(1)}, bf16[12,512]{1,0:T(8,128)(2,1)}, u32[]{:S(2)}) copy-start(bf16[12,512]{1,0:T(8,128)(2,1)} %param.6) | copy-start | bytes 36868
  234.8 9.3 %collective-permute-start.6 = (f32[4,13,512]{2,1,0:T(8,128)S(1)}, f32[4,13,512]{2,1,0:T(8,128)S(1)}, u32[]{:S(2)}, u32[]{:S(2)}) collective-permute-start(f32[4,13,512]{2,1,0:T(8,128)S(1)} %get-tuple-element.10), channel_id=1, source_target_pairs={{0,1},{1,0},{2,3},{3,2},{4,5},{5,4},{6,7},{7,6},{8,9},{9,8},{10,11... | collective-permute-start | bytes 319496 | tf_op jit(solution)/shard_map/ppermute | solution.py:26
  238.0 10.5 %collective-permute-start.7 = (f32[4,13,512]{2,1,0:T(8,128)S(1)}, f32[4,13,512]{2,1,0:T(8,128)S(1)}, u32[]{:S(2)}, u32[]{:S(2)}) collective-permute-start(f32[4,13,512]{2,1,0:T(8,128)S(1)} %get-tuple-element.11), channel_id=1, source_target_pairs={{0,2},{1,3},{2,0},{3,1},{4,6},{5,7},{6,4},{7,5},{8,10},{9,11},{10,... | collective-permute-start | bytes 319496 | tf_op jit(solution)/shard_map/ppermute | solution.py:26
  242.2 7.6 %collective-permute-start.8 = (f32[4,13,512]{2,1,0:T(8,128)S(1)}, f32[4,13,512]{2,1,0:T(8,128)S(1)}, u32[]{:S(2)}, u32[]{:S(2)}) collective-permute-start(f32[4,13,512]{2,1,0:T(8,128)S(1)} %get-tuple-element.12), channel_id=1, source_target_pairs={{0,3},{1,2},{2,1},{3,0},{4,7},{5,6},{6,5},{7,4},{8,11},{9,10},{10,... | collective-permute-start | bytes 319496 | tf_op jit(solution)/shard_map/ppermute | solution.py:26
  249.9 17.5 %collective-permute-start.9 = (f32[1,13,512]{2,1,0:T(8,128)S(1)}, f32[1,13,512]{2,1,0:T(8,128)S(1)}, u32[]{:S(2)}, u32[]{:S(2)}) collective-permute-start(f32[1,13,512]{2,1,0:T(8,128)S(1)} %get-tuple-element.19), channel_id=1, source_target_pairs={{0,4},{1,5},{2,6},{3,7},{4,0},{5,1},{6,2},{7,3},{8,12},{9,13},{10,... | collective-permute-start | bytes 79880 | tf_op jit(solution)/shard_map/ppermute | solution.py:26
  257.2 10.1 %collective-permute-start.11 = (f32[1,13,512]{2,1,0:T(8,128)S(1)}, f32[1,13,512]{2,1,0:T(8,128)S(1)}, u32[]{:S(2)}, u32[]{:S(2)}) collective-permute-start(f32[1,13,512]{2,1,0:T(8,128)S(1)} %get-tuple-element.20), channel_id=1, source_target_pairs={{0,12},{1,13},{2,14},{3,15},{4,8},{5,9},{6,10},{7,11},{8,4},{9,5},... | collective-permute-start | bytes 79880 | tf_op jit(solution)/shard_map/ppermute | solution.py:26
  264.9 13.5 %collective-permute-start.10 = (f32[1,13,512]{2,1,0:T(8,128)S(1)}, f32[1,13,512]{2,1,0:T(8,128)S(1)}, u32[]{:S(2)}, u32[]{:S(2)}) collective-permute-start(f32[1,13,512]{2,1,0:T(8,128)S(1)} %get-tuple-element.21), channel_id=1, source_target_pairs={{0,8},{1,9},{2,10},{3,11},{4,12},{5,13},{6,14},{7,15},{8,0},{9,1},... | collective-permute-start | bytes 79880 | tf_op jit(solution)/shard_map/ppermute | solution.py:26
Sparse Core Ops, SparseCore 0:
  88.9 137.2 all-reduce.2
